TPU v7x, 512 devices: a whole 4x8x8 slice. The times are simulated.
512 devices in a mesh: ens: 4 (over z_hi), lon: 32 (over z_lo, y, core), lat: 4 (over x).
Axes of the slice: x: 4, y: 8, z: 8 (z_hi: 4, z_lo: 2; z = z_hi * 2 + z_lo), core: 2. Of those that a mesh axis runs over, the one named last changes fastest.
Arguments:
- ocean_state: bfloat16 [4, 200, 32, 4096], P('ens', None, 'lat', 'lon'), may hold values from -6 to 6
- ocean_mask: int32 [32, 4096], P('lat', 'lon'), may hold values from 0 to 1, as said below
- dw_weight: float32 [200, 49], replicated, may hold values from -0.875 to 0.875
- norm_gain: float32 [200], replicated, may hold values from 0.1 to 1.9
- expand_weight: bfloat16 [200, 800], replicated, may hold values from -0.4375 to 0.4375
- reduce_weight: bfloat16 [800, 200], replicated, may hold values from -0.21875 to 0.21875
- cotangent: bfloat16 [4, 200, 32, 4096], P('ens', None, 'lat', 'lon'), may hold values from -6 to 6
Outputs:
- next_state: bfloat16 [4, 200, 32, 4096], P('ens', None, 'lat', 'lon')
- grad_depthwise: float32 [200, 49], replicated
- grad_gain: float32 [200], replicated
- grad_expand: float32 [200, 800], replicated
- grad_reduce: float32 [800, 200], replicated
Inputs may be any that keep to these rules, and one draw needn't show every extreme that they name: `ocean_mask`: the share of ocean cells differs from tile to tile of 8 x 128 cells, from about a third to nearly all.
All inputs are finite; a program needn't handle non-finite values.
Results may differ from a plain program's by a relative error of at most 0.0058.
Values may be sent and summed in bfloat16 or wider, within the bound.
No kernel may reach another device: no remote copies, remote signals or barrier semaphores. Data moves between devices by JAX's collectives and lax.ppermute only.
A program may use at most 64 MiB of HBM per device.

v0:
```python
import math

import jax
import jax.numpy as jnp
from jax import lax
from jax.sharding import PartitionSpec as P

KS = 7


norm_eps = 1e-06
root_half = 0.7071067811865476
gauss_norm = 0.3989422804014327


def with_halo(cells, sides, width):
    for axis, dim in sides:
        count = lax.axis_size(axis)
        head = lax.slice_in_dim(cells, 0, width, axis=dim)
        tail = lax.slice_in_dim(cells, cells.shape[dim] - width, cells.shape[dim], axis=dim)
        cells = jnp.concatenate(
            [
                lax.ppermute(tail, axis, [(i, (i + 1) % count) for i in range(count)]),
                cells,
                lax.ppermute(head, axis, [((i + 1) % count, i) for i in range(count)]),
            ],
            axis=dim,
        )
    return cells


def swapped(array, axis, stride):
    return lax.ppermute(array, axis, [(i, i ^ 1 << stride) for i in range(lax.axis_size(axis))])


def depthwise(padded, dw_weight, out_rows, out_cols):
    conv_sum = jnp.zeros((padded.shape[0], out_rows, out_cols), jnp.float32)
    for shift_a in range(KS):
        for shift_b in range(KS):
            tap_weight = dw_weight[:, shift_a * KS + shift_b][:, None, None]
            window = padded[:, shift_a : shift_a + out_rows, shift_b : shift_b + out_cols].astype(
                jnp.float32
            )
            conv_sum = conv_sum + tap_weight * window
    return conv_sum


def depthwise_grad(d_conv, padded, out_rows, out_cols):
    columns = []
    for shift_a in range(KS):
        for shift_b in range(KS):
            window = padded[:, shift_a : shift_a + out_rows, shift_b : shift_b + out_cols].astype(
                jnp.float32
            )
            columns.append(jnp.sum(d_conv * window, axis=(1, 2)))
    return jnp.stack(columns, axis=1)


def cell_pass(conv_blk, state_blk, cot_blk, mask_blk, norm_gain, expand_weight, reduce_weight):
    chan_mean = jnp.mean(conv_blk, axis=0, keepdims=True)
    centred = conv_blk - chan_mean
    chan_var = jnp.mean(centred * centred, axis=0, keepdims=True)
    inv_std = lax.rsqrt(chan_var + norm_eps)
    normed = centred * inv_std
    scaled = (normed * norm_gain[:, None]).astype(jnp.bfloat16)
    pre_act = jnp.dot(expand_weight.T, scaled, preferred_element_type=jnp.float32)
    normal_cdf = 0.5 * (1.0 + lax.erf(pre_act * root_half))
    normal_pdf = jnp.exp(-0.5 * pre_act * pre_act) * gauss_norm
    hidden = (pre_act * normal_cdf).astype(jnp.bfloat16)
    gelu_slope = normal_cdf + pre_act * normal_pdf
    branch = jnp.dot(reduce_weight.T, hidden, preferred_element_type=jnp.float32)
    out_blk = ((state_blk.astype(jnp.float32) + branch) * mask_blk[None, :]).astype(jnp.bfloat16)
    grad_reduce = jnp.dot(hidden, cot_blk.T, preferred_element_type=jnp.float32)
    d_hidden = jnp.dot(reduce_weight, cot_blk, preferred_element_type=jnp.float32)
    d_pre = (d_hidden * gelu_slope).astype(jnp.bfloat16)
    grad_expand = jnp.dot(scaled, d_pre.T, preferred_element_type=jnp.float32)
    d_scaled = jnp.dot(expand_weight, d_pre, preferred_element_type=jnp.float32)
    grad_gain = jnp.sum(d_scaled * normed, axis=1)
    d_normed = d_scaled * norm_gain[:, None]
    d_conv = inv_std * (
        d_normed
        - jnp.mean(d_normed, axis=0, keepdims=True)
        - normed * jnp.mean(d_normed * normed, axis=0, keepdims=True)
    )
    return (out_blk, d_conv, grad_expand, grad_reduce, grad_gain)


def body(ocean_state, ocean_mask, dw_weight, norm_gain, expand_weight, reduce_weight, cotangent):
    state_tile = ocean_state[0]
    channels = state_tile.shape[0]
    tile_rows = state_tile.shape[1]
    tile_cols = state_tile.shape[2]
    margin = KS // 2
    mask_bf = ocean_mask.astype(jnp.bfloat16)
    masked = state_tile * mask_bf[None]
    padded = with_halo(masked, (("lon", 2), ("lat", 1)), margin)
    lat_now = lax.axis_index("lat")
    lat_count = lax.axis_size("lat")
    lon_count = lax.axis_size("lon")
    top_strip = padded[:, tile_rows : tile_rows + margin, :][:, ::-1, ::-1]
    mirrored = top_strip
    for bit_number in range(lon_count.bit_length() - 1):
        mirrored = swapped(mirrored, "lon", bit_number)
    north_rows = jnp.where(lat_now == lat_count - 1, mirrored, padded[:, tile_rows + margin :, :])
    south_rows = jnp.where(lat_now == 0, jnp.zeros_like(top_strip), padded[:, :margin, :])
    padded = jnp.concatenate(
        [south_rows, padded[:, margin : tile_rows + margin, :], north_rows], axis=1
    )
    conv_out = depthwise(padded, dw_weight, tile_rows, tile_cols)
    cell_count = tile_rows * tile_cols
    cot_masked = (cotangent[0] * mask_bf[None]).reshape(channels, cell_count)
    out_flat, d_conv, grad_expand, grad_reduce, grad_gain = cell_pass(
        conv_out.reshape(channels, cell_count),
        state_tile.reshape(channels, cell_count),
        cot_masked,
        ocean_mask.astype(jnp.float32).reshape(cell_count),
        norm_gain,
        expand_weight,
        reduce_weight,
    )
    grad_depthwise = depthwise_grad(
        d_conv.reshape(channels, tile_rows, tile_cols), padded, tile_rows, tile_cols
    )
    grad_scale = 1.0 / math.sqrt(lax.axis_size("ens") * lat_count * lon_count * cell_count)
    grad_expand = grad_expand * grad_scale
    grad_reduce = grad_reduce * grad_scale
    grad_gain = grad_gain * grad_scale
    grad_depthwise = grad_depthwise * grad_scale
    grad_expand, grad_reduce, grad_gain, grad_depthwise = lax.psum(
        (grad_expand, grad_reduce, grad_gain, grad_depthwise), ("ens", "lon", "lat")
    )
    next_state = out_flat.reshape(channels, tile_rows, tile_cols)[None]
    return (next_state, grad_depthwise, grad_gain, grad_expand, grad_reduce)


def solution(mesh):
    return jax.shard_map(
        body,
        mesh=mesh,
        in_specs=(
            P("ens", None, "lat", "lon"),
            P("lat", "lon"),
            P(),
            P(),
            P(),
            P(),
            P("ens", None, "lat", "lon"),
        ),
        out_specs=(P("ens", None, "lat", "lon"), P(), P(), P(), P()),
        check_vma=False,
    )
```

profile of v0, /device:TPU:1, one launch (start us, length us, event | category | flops | bytes accessed | tf_op | source)
XLA Modules:
  0.0 393.6 jit_solution(8443036720947394535)
XLA Ops:
  10.1 4.6 %collective-permute-start = (bf16[200,8,3]{0,2,1:T(4,128)(2,1)S(1)}, bf16[200,8,3]{0,2,1:T(4,128)(2,1)S(1)}, u32[]{:S(2)}, u32[]{:S(2)}) collective-permute-start(bf16[200,8,3]{0,2,1:T(4,128)(2,1)S(1)} %get-tuple-element.80), channel_id=1, source_target_pairs={{0,4},{4,8},{8,12},{12,16},{16,20},{20,24},{24,28},{28,32},{32,36}... | collective-permute-start | bytes 28808 | tf_op jit(solution)/shard_map/ppermute | solution.py:23
  14.7 6.1 %collective-permute-start.1 = (bf16[200,8,3]{0,2,1:T(4,128)(2,1)S(1)}, bf16[200,8,3]{0,2,1:T(4,128)(2,1)S(1)}, u32[]{:S(2)}, u32[]{:S(2)}) collective-permute-start(bf16[200,8,3]{0,2,1:T(4,128)(2,1)S(1)} %get-tuple-element.81), channel_id=1, source_target_pairs={{4,0},{8,4},{12,8},{16,12},{20,16},{24,20},{28,24},{32,28},{36,32}... | collective-permute-start | bytes 28808 | tf_op jit(solution)/shard_map/ppermute | solution.py:25
  22.8 6.4 %collective-permute-start.3 = (bf16[200,3,134]{0,2,1:T(8,128)(2,1)S(1)}, bf16[200,3,134]{0,2,1:T(8,128)(2,1)S(1)}, u32[]{:S(2)}, u32[]{:S(2)}) collective-permute-start(bf16[200,3,134]{0,2,1:T(8,128)(2,1)S(1)} %rev.3), channel_id=1, source_target_pairs={{0,4},{4,0},{8,12},{12,8},{16,20},{20,16},{24,28},{28,24},{32,36},... | collective-permute-start | bytes 482408 | tf_op jit(solution)/shard_map/ppermute | solution.py:33
  30.2 1.9 collective-permute-start.4
  32.1 6.3 %collective-permute-done.4 = bf16[200,3,134]{0,2,1:T(8,128)(2,1)S(1)} collective-permute-done((bf16[200,3,134]{0,2,1:T(8,128)(2,1)S(1)}, bf16[200,3,134]{0,2,1:T(8,128)(2,1)S(1)}, u32[]{:S(2)}, u32[]{:S(2)}) %collective-permute-start.4) | collective-permute-done | bytes 160832 | tf_op jit(solution)/shard_map/ppermute | solution.py:33
  38.4 1.9 collective-permute-start.5
  40.4 2.2 collective-permute-start.2
  42.6 10.1 %collective-permute-done.5 = bf16[200,3,134]{0,2,1:T(8,128)(2,1)S(1)} collective-permute-done((bf16[200,3,134]{0,2,1:T(8,128)(2,1)S(1)}, bf16[200,3,134]{0,2,1:T(8,128)(2,1)S(1)}, u32[]{:S(2)}, u32[]{:S(2)}) %collective-permute-start.5) | collective-permute-done | bytes 160832 | tf_op jit(solution)/shard_map/ppermute | solution.py:33
  52.7 1.9 collective-permute-start.6
  54.7 2.7 collective-permute-start.8
  57.4 8.9 %collective-permute-done.6 = bf16[200,3,134]{0,2,1:T(8,128)(2,1)S(1)} collective-permute-done((bf16[200,3,134]{0,2,1:T(8,128)(2,1)S(1)}, bf16[200,3,134]{0,2,1:T(8,128)(2,1)S(1)}, u32[]{:S(2)}, u32[]{:S(2)}) %collective-permute-start.6) | collective-permute-done | bytes 160832 | tf_op jit(solution)/shard_map/ppermute | solution.py:33
  66.3 1.9 collective-permute-start.7
  68.2 5.0 %collective-permute-done.7 = bf16[200,3,134]{0,2,1:T(8,128)(2,1)S(1)} collective-permute-done((bf16[200,3,134]{0,2,1:T(8,128)(2,1)S(1)}, bf16[200,3,134]{0,2,1:T(8,128)(2,1)S(1)}, u32[]{:S(2)}, u32[]{:S(2)}) %collective-permute-start.7) | collective-permute-done | bytes 160832 | tf_op jit(solution)/shard_map/ppermute | solution.py:33
  73.5 8.3 %fusion.118 = (f32[8,128]{1,0:T(8,128)S(1)}, f32[200,8,128]{0,2,1:T(8,128)S(1)}) fusion(bf16[200,11,134]{0,2,1:T(8,128)(2,1)S(1)} %get-tuple-element.77, f32[200]{0:T(256)S(1)} %bitcast.303, f32[200]{0:T(256)S(1)} %bitcast.304, f32[200]{0:T(256)S(1)} %bitcast.257, f32[200]{0:T(256)S(1)} %bitcast.258, f32[200]{0:T(256)S(1)} %bitcast.259, ...), kind=kLoop, calls=%fused_computation.252 | loop fusion | flops 33790976 | bytes 18494496 | tf_op jit(solution)/shard_map/reduce_sum | solution.py:60
  84.4 2.2 fusion.9
  86.6 1.7 fusion.5
  88.3 1.7 convolution_multiply_fusion.1
  94.1 3.8 fusion.59
  97.9 3.8 fusion.109
  101.7 1.6 convolution_multiply_fusion
  103.4 3.0 fusion.91
  109.7 105.6 %all-reduce = (f32[200,49]{0,1:T(8,128)}, f32[200]{0:T(256)}) all-reduce(f32[200,49]{0,1:T(8,128)S(1)} %broadcast_multiply_fusion, f32[200]{0:T(256)S(1)} %broadcast_multiply_fusion.4), channel_id=1, replica_groups=mesh['ens'=4,'lon'=32,'lat'=4] {'ens','lon','lat'}, use_global_device_ids=true, to_apply=%region_53.54 | all-reduce | flops 10000 | bytes 80000 | tf_op jit(solution)/shard_map/psum | solution.py:129
  215.3 168.5 %all-reduce.4.cloned.1.call-done = (f32[200,800]{1,0:T(8,128)}, f32[800,200]{0,1:T(8,128)}) async-done(((f32[200,800]{1,0:T(8,128)}, f32[800,200]{0,1:T(8,128)}), (f32[200,800]{1,0:T(8,128)}, f32[800,200]{0,1:T(8,128)})) %all-reduce.4.cloned.1.call-update) | async-done | bytes 1280016 | tf_op jit(solution)/shard_map/psum | solution.py:129
  383.8 2.1 copy.74
  (133 shorter events, 16.5 us)
Async XLA Ops:
  7.2 77.2 %copy-start = (bf16[200,800]{1,0:T(8,128)(2,1)S(1)}, bf16[200,800]{1,0:T(8,128)(2,1)}, u32[]{:S(2)}) copy-start(bf16[200,800]{1,0:T(8,128)(2,1)} %param.11) | copy-start | bytes 960004
  7.2 376.7 %all-reduce.4.cloned.1.call-start = ((), (), s32[]{:S(2)}) async-start(), calls=%async_computation | async-start | bytes 2867200 | tf_op jit(solution)/shard_map/psum | solution.py:129
  8.6 23.5 %copy-start.7 = (f32[200,49]{0,1:T(8,128)S(1)}, f32[200,49]{0,1:T(8,128)}, u32[]{:S(2)}) copy-start(f32[200,49]{0,1:T(8,128)} %param.9) | copy-start | bytes 117604
  10.1 10.7 %collective-permute-start = (bf16[200,8,3]{0,2,1:T(4,128)(2,1)S(1)}, bf16[200,8,3]{0,2,1:T(4,128)(2,1)S(1)}, u32[]{:S(2)}, u32[]{:S(2)}) collective-permute-start(bf16[200,8,3]{0,2,1:T(4,128)(2,1)S(1)} %get-tuple-element.80), channel_id=1, source_target_pairs={{0,4},{4,8},{8,12},{12,16},{16,20},{20,24},{24,28},{28,32},{32,36}... | collective-permute-start | bytes 28808 | tf_op jit(solution)/shard_map/ppermute | solution.py:23
  14.7 6.9 %collective-permute-start.1 = (bf16[200,8,3]{0,2,1:T(4,128)(2,1)S(1)}, bf16[200,8,3]{0,2,1:T(4,128)(2,1)S(1)}, u32[]{:S(2)}, u32[]{:S(2)}) collective-permute-start(bf16[200,8,3]{0,2,1:T(4,128)(2,1)S(1)} %get-tuple-element.81), channel_id=1, source_target_pairs={{4,0},{8,4},{12,8},{16,12},{20,16},{24,20},{28,24},{32,28},{36,32}... | collective-permute-start | bytes 28808 | tf_op jit(solution)/shard_map/ppermute | solution.py:25
  22.8 7.4 %collective-permute-start.3 = (bf16[200,3,134]{0,2,1:T(8,128)(2,1)S(1)}, bf16[200,3,134]{0,2,1:T(8,128)(2,1)S(1)}, u32[]{:S(2)}, u32[]{:S(2)}) collective-permute-start(bf16[200,3,134]{0,2,1:T(8,128)(2,1)S(1)} %rev.3), channel_id=1, source_target_pairs={{0,4},{4,0},{8,12},{12,8},{16,20},{20,16},{24,28},{28,24},{32,36},... | collective-permute-start | bytes 482408 | tf_op jit(solution)/shard_map/ppermute | solution.py:33
  30.2 8.3 %collective-permute-start.4 = (bf16[200,3,134]{0,2,1:T(8,128)(2,1)S(1)}, bf16[200,3,134]{0,2,1:T(8,128)(2,1)S(1)}, u32[]{:S(2)}, u32[]{:S(2)}) collective-permute-start(bf16[200,3,134]{0,2,1:T(8,128)(2,1)S(1)} %collective-permute-done.3), channel_id=1, source_target_pairs={{0,8},{4,12},{8,0},{12,4},{16,24},{20,28},{24,16},{28,20},{32,40},... | collective-permute-start | bytes 482408 | tf_op jit(solution)/shard_map/ppermute | solution.py:33
  38.4 14.3 %collective-permute-start.5 = (bf16[200,3,134]{0,2,1:T(8,128)(2,1)S(1)}, bf16[200,3,134]{0,2,1:T(8,128)(2,1)S(1)}, u32[]{:S(2)}, u32[]{:S(2)}) collective-permute-start(bf16[200,3,134]{0,2,1:T(8,128)(2,1)S(1)} %collective-permute-done.4), channel_id=1, source_target_pairs={{0,16},{4,20},{8,24},{12,28},{16,0},{20,4},{24,8},{28,12},{32,48},... | collective-permute-start | bytes 482408 | tf_op jit(solution)/shard_map/ppermute | solution.py:33
  40.4 27.8 %collective-permute-start.2 = (bf16[200,3,134]{0,2,1:T(8,128)(2,1)S(1)}, bf16[200,3,134]{0,2,1:T(8,128)(2,1)S(1)}, u32[]{:S(2)}, u32[]{:S(2)}) collective-permute-start(bf16[200,3,134]{0,2,1:T(8,128)(2,1)S(1)} %get-tuple-element.79), channel_id=1, source_target_pairs={{0,1},{1,2},{2,3},{3,0},{4,5},{5,6},{6,7},{7,4},{8,9},{9,10},{10,1... | collective-permute-start | bytes 482408 | tf_op jit(solution)/shard_map/ppermute | solution.py:23
  52.7 13.5 %collective-permute-start.6 = (bf16[200,3,134]{0,2,1:T(8,128)(2,1)S(1)}, bf16[200,3,134]{0,2,1:T(8,128)(2,1)S(1)}, u32[]{:S(2)}, u32[]{:S(2)}) collective-permute-start(bf16[200,3,134]{0,2,1:T(8,128)(2,1)S(1)} %collective-permute-done.5), channel_id=1, source_target_pairs={{0,32},{4,36},{8,40},{12,44},{16,48},{20,52},{24,56},{28,60},{32,0... | collective-permute-start | bytes 482408 | tf_op jit(solution)/shard_map/ppermute | solution.py:33
  54.7 13.6 %collective-permute-start.8 = (bf16[200,3,134]{0,2,1:T(8,128)(2,1)S(1)}, bf16[200,3,134]{0,2,1:T(8,128)(2,1)S(1)}, u32[]{:S(2)}, u32[]{:S(2)}) collective-permute-start(bf16[200,3,134]{0,2,1:T(8,128)(2,1)S(1)} %get-tuple-element.78), channel_id=1, source_target_pairs={{1,0},{2,1},{3,2},{0,3},{5,4},{6,5},{7,6},{4,7},{9,8},{10,9},{11,1... | collective-permute-start | bytes 482408 | tf_op jit(solution)/shard_map/ppermute | solution.py:25
  66.3 7.0 %collective-permute-start.7 = (bf16[200,3,134]{0,2,1:T(8,128)(2,1)S(1)}, bf16[200,3,134]{0,2,1:T(8,128)(2,1)S(1)}, u32[]{:S(2)}, u32[]{:S(2)}) collective-permute-start(bf16[200,3,134]{0,2,1:T(8,128)(2,1)S(1)} %collective-permute-done.6), channel_id=1, source_target_pairs={{0,64},{4,68},{8,72},{12,76},{16,80},{20,84},{24,88},{28,92},{32,9... | collective-permute-start | bytes 482408 | tf_op jit(solution)/shard_map/ppermute | solution.py:33
  97.9 3.8 copy-start.2
  97.9 3.8 copy-start.48
  103.3 3.1 copy-start.3
  103.4 3.1 copy-start.5
  103.4 3.1 copy-start.33
  106.4 2.8 copy-start.9
  106.4 2.8 copy-start.10
  106.4 2.8 copy-start.11
  106.4 2.8 copy-start.12
  106.5 2.8 copy-start.13
  106.5 2.8 copy-start.14
  106.8 2.9 copy-start.46
  (36 other events, 94.5 us)
Sparse Core Ops, SparseCore 0:
  103.5 280.3 all-reduce.3
where the time goes:
time: 394 us
  waiting for transfers between devices  201 us (51%)
  blocking collectives  106 us (27%)
  starting transfers between devices  29.7 us (8%)
  other arithmetic  22.5 us (6%)
  between operations  14.9 us (4%)
  matrix products  10.2 us (3%)
  local copies, waits for them, and re-layouts  10 us (3%)
    psum x1, waiting for transfers between devices, body(): lax.psum((grad_expand, grad_reduce, grad_gain, grad_depthwise), ('ens', '...  169 us
    psum x1, blocking collectives, body(): lax.psum((grad_expand, grad_reduce, grad_gain, grad_depthwise), ('ens', '...  106 us
    ppermute x5, waiting for transfers between devices, swapped(): lax.ppermute(array, axis, [(i, i ^ 1 << stride) for i in range(lax.axis_s...  31.4 us
    ppermute x5, starting transfers between devices, swapped(): lax.ppermute(array, axis, [(i, i ^ 1 << stride) for i in range(lax.axis_s...  14 us
    reduce_sum x4, other arithmetic, depthwise_grad(): columns.append(jnp.sum(d_conv * window, axis=(1, 2)))  11.9 us
    ppermute x2, starting transfers between devices, with_halo(): lax.ppermute(head, axis, [((i + 1) % count, i) for i in range(count)])  8.83 us
    reduce_sum x1, other arithmetic, cell_pass(): chan_mean = jnp.mean(conv_blk, axis=0, keepdims=True)  8.28 us
  transfers between devices with their start and end apart: 10, of which 7 were waited for; matrix products, arithmetic and copies ran while one was open for 1% of the time, Pallas kernels for 0%

commit v1 on v0

--- a/solution.py
+++ b/solution.py
@@ -31,6 +31,42 @@
 
 def swapped(array, axis, stride):
     return lax.ppermute(array, axis, [(i, i ^ 1 << stride) for i in range(lax.axis_size(axis))])
+
+
+def mirrored_across(array, axis):
+    count = lax.axis_size(axis)
+    return lax.ppermute(array, axis, [(i, count - 1 - i) for i in range(count)])
+
+
+REDUCE_ORDER = (
+    ("lon", 0), ("lat", 0), ("lon", 1), ("ens", 0), ("lon", 4),
+    ("lat", 1), ("lon", 2), ("ens", 1), ("lon", 3),
+)
+
+
+def tree_psum(flat, steps, gather_dtype):
+    halved = []
+    for axis, bit in steps:
+        if (1 << bit) >= lax.axis_size(axis):
+            continue
+        upper = (lax.axis_index(axis) >> bit) & 1
+        if flat.shape[0] % 16 == 0:
+            half = flat.shape[0] // 2
+            low, high = flat[:half], flat[half:]
+            keep = jnp.where(upper == 0, low, high)
+            send = jnp.where(upper == 0, high, low)
+            flat = keep + swapped(send, axis, bit)
+            halved.append((axis, bit))
+        else:
+            flat = flat + swapped(flat, axis, bit)
+    flat = flat.astype(gather_dtype)
+    for axis, bit in reversed(halved):
+        upper = (lax.axis_index(axis) >> bit) & 1
+        other = swapped(flat, axis, bit)
+        flat = jnp.where(
+            upper == 0, jnp.concatenate([flat, other]), jnp.concatenate([other, flat])
+        )
+    return flat.astype(jnp.float32)
 
 
 def depthwise(padded, dw_weight, out_rows, out_cols):
@@ -98,9 +134,7 @@
     lat_count = lax.axis_size("lat")
     lon_count = lax.axis_size("lon")
     top_strip = padded[:, tile_rows : tile_rows + margin, :][:, ::-1, ::-1]
-    mirrored = top_strip
-    for bit_number in range(lon_count.bit_length() - 1):
-        mirrored = swapped(mirrored, "lon", bit_number)
+    mirrored = mirrored_across(top_strip, "lon")
     north_rows = jnp.where(lat_now == lat_count - 1, mirrored, padded[:, tile_rows + margin :, :])
     south_rows = jnp.where(lat_now == 0, jnp.zeros_like(top_strip), padded[:, :margin, :])
     padded = jnp.concatenate(
@@ -126,9 +160,23 @@
     grad_reduce = grad_reduce * grad_scale
     grad_gain = grad_gain * grad_scale
     grad_depthwise = grad_depthwise * grad_scale
-    grad_expand, grad_reduce, grad_gain, grad_depthwise = lax.psum(
-        (grad_expand, grad_reduce, grad_gain, grad_depthwise), ("ens", "lon", "lat")
-    )
+    pieces = (grad_expand, grad_reduce, grad_gain, grad_depthwise)
+    flat = jnp.concatenate([piece.reshape(-1) for piece in pieces])
+    lanes = 128
+    rows = -(-flat.shape[0] // (lanes * 256)) * 256
+    flat = jnp.pad(flat, (0, rows * lanes - flat.shape[0])).reshape(rows, lanes)
+    steps = [(axis, bit) for axis, bit in REDUCE_ORDER]
+    for axis in ("ens", "lon", "lat"):
+        for bit in range(lax.axis_size(axis).bit_length() - 1):
+            if (axis, bit) not in steps:
+                steps.append((axis, bit))
+    flat = tree_psum(flat, steps, jnp.float32).reshape(-1)
+    summed = []
+    offset = 0
+    for piece in pieces:
+        summed.append(flat[offset : offset + piece.size].reshape(piece.shape))
+        offset += piece.size
+    grad_expand, grad_reduce, grad_gain, grad_depthwise = summed
     next_state = out_flat.reshape(channels, tile_rows, tile_cols)[None]
     return (next_state, grad_depthwise, grad_gain, grad_expand, grad_reduce)
 

time: 394 us -> 216 us (0.55)
  waiting for transfers between devices: 201 us -> 50.9 us
  blocking collectives: 106 us -> 0 us
  starting transfers between devices: 29.7 us -> 85.8 us
  local copies, waits for them, and re-layouts: 10 us -> 39.4 us
  between operations: 14.9 us -> 1.31 us
    psum x1 -> x0, waiting for transfers between devices: 169 us -> none  [body(): lax.psum((grad_expand, grad_reduce, grad_gain, grad_depthwise), ('ens', '...]
    psum x1 -> x0, blocking collectives: 106 us -> none  [body(): lax.psum((grad_expand, grad_reduce, grad_gain, grad_depthwise), ('ens', '...]
    ppermute x5 -> x14, starting transfers between devices: 14 us -> 62.7 us  [swapped(): lax.ppermute(array, axis, [(i, i ^ 1 << stride) for i in range(lax.axis_s...]
    concatenate x0 -> x3, local copies, waits for them, and re-layouts: none -> 15.6 us  [body(): flat = jnp.concatenate([piece.reshape(-1) for piece in pieces])]
    ppermute x5 -> x14, waiting for transfers between devices: 31.4 us -> 44.6 us  [swapped(): lax.ppermute(array, axis, [(i, i ^ 1 << stride) for i in range(lax.axis_s...]
    reshape x0 -> x5, local copies, waits for them, and re-layouts: none -> 8.04 us  [the longest x2 5.36 us: body(): flat = jnp.concatenate([piece.reshape(-1) for piece in pieces])]
    ppermute x0 -> x1, starting transfers between devices: none -> 5.6 us  [mirrored_across(): return lax.ppermute(array, axis, [(i, count - 1 - i) for i in range(count)])]
    ppermute x0 -> x1, waiting for transfers between devices: none -> 5.57 us  [mirrored_across(): return lax.ppermute(array, axis, [(i, count - 1 - i) for i in range(count)])]
  transfers between devices with their start and end apart: 10 -> 19, of which waited for: 7 -> 16; matrix products, arithmetic and copies ran while one was open for 1% -> 1% of each run, Pallas kernels for 0% -> 0%
where the time goes in v1:
time: 216 us; the launch traced here: 214 us
  starting transfers between devices  85.8 us (40%)
  waiting for transfers between devices  50.9 us (24%)
  local copies, waits for them, and re-layouts  39.4 us (18%)
  other arithmetic  26 us (12%)
  matrix products  10.7 us (5%)
    ppermute x14, starting transfers between devices, swapped(): lax.ppermute(array, axis, [(i, i ^ 1 << stride) for i in range(lax.axis_s...  62.7 us
    ppermute x14, waiting for transfers between devices, swapped(): lax.ppermute(array, axis, [(i, i ^ 1 << stride) for i in range(lax.axis_s...  44.6 us
    concatenate x3, local copies, waits for them, and re-layouts, body(): flat = jnp.concatenate([piece.reshape(-1) for piece in pieces])  15.6 us
    reduce_sum x4, other arithmetic, depthwise_grad(): columns.append(jnp.sum(d_conv * window, axis=(1, 2)))  12 us
    ppermute x2, starting transfers between devices, with_halo(): lax.ppermute(head, axis, [((i + 1) % count, i) for i in range(count)])  11 us
    reduce_sum x1, other arithmetic, cell_pass(): chan_mean = jnp.mean(conv_blk, axis=0, keepdims=True)  8.27 us
    ppermute x2, starting transfers between devices, with_halo(): lax.ppermute(tail, axis, [(i, (i + 1) % count) for i in range(count)])  6.52 us
    ppermute x1, starting transfers between devices, mirrored_across(): return lax.ppermute(array, axis, [(i, count - 1 - i) for i in range(count)])  5.6 us
  transfers between devices with their start and end apart: 19, of which 16 were waited for; matrix products, arithmetic and copies ran while one was open for 1% of the time, Pallas kernels for 0%

profile of v1, /device:TPU:1, one launch (start us, length us, event | category | flops | bytes accessed | tf_op | source)
XLA Modules:
  0.0 214.1 jit_solution(3504315899637507078)
XLA Ops:
  3.5 4.6 %collective-permute-start = (bf16[200,8,3]{0,2,1:T(4,128)(2,1)S(1)}, bf16[200,8,3]{0,2,1:T(4,128)(2,1)S(1)}, u32[]{:S(2)}, u32[]{:S(2)}) collective-permute-start(bf16[200,8,3]{0,2,1:T(4,128)(2,1)S(1)} %get-tuple-element.88), channel_id=1, source_target_pairs={{0,4},{4,8},{8,12},{12,16},{16,20},{20,24},{24,28},{28,32},{32,36}... | collective-permute-start | bytes 28808 | tf_op jit(solution)/shard_map/ppermute | solution.py:23
  8.1 6.1 %collective-permute-start.1 = (bf16[200,8,3]{0,2,1:T(4,128)(2,1)S(1)}, bf16[200,8,3]{0,2,1:T(4,128)(2,1)S(1)}, u32[]{:S(2)}, u32[]{:S(2)}) collective-permute-start(bf16[200,8,3]{0,2,1:T(4,128)(2,1)S(1)} %get-tuple-element.89), channel_id=1, source_target_pairs={{4,0},{8,4},{12,8},{16,12},{20,16},{24,20},{28,24},{32,28},{36,32}... | collective-permute-start | bytes 28808 | tf_op jit(solution)/shard_map/ppermute | solution.py:25
  18.1 5.6 %collective-permute-start.3 = (bf16[200,3,134]{0,2,1:T(8,128)(2,1)S(1)}, bf16[200,3,134]{0,2,1:T(8,128)(2,1)S(1)}, u32[]{:S(2)}, u32[]{:S(2)}) collective-permute-start(bf16[200,3,134]{0,2,1:T(8,128)(2,1)S(1)} %rev.3), channel_id=1, source_target_pairs={{0,124},{4,120},{8,116},{12,112},{16,108},{20,104},{24,100},{28,96... | collective-permute-start | bytes 482408 | tf_op jit(solution)/shard_map/ppermute | solution.py:38
  23.7 4.9 %collective-permute-start.4 = (bf16[200,3,134]{0,2,1:T(8,128)(2,1)S(1)}, bf16[200,3,134]{0,2,1:T(8,128)(2,1)S(1)}, u32[]{:S(2)}, u32[]{:S(2)}) collective-permute-start(bf16[200,3,134]{0,2,1:T(8,128)(2,1)S(1)} %get-tuple-element.86), channel_id=1, source_target_pairs={{1,0},{2,1},{3,2},{0,3},{5,4},{6,5},{7,6},{4,7},{9,8},{10,9},{11,1... | collective-permute-start | bytes 482408 | tf_op jit(solution)/shard_map/ppermute | solution.py:25
  28.6 5.6 %collective-permute-done.3 = bf16[200,3,134]{0,2,1:T(8,128)(2,1)S(1)} collective-permute-done((bf16[200,3,134]{0,2,1:T(8,128)(2,1)S(1)}, bf16[200,3,134]{0,2,1:T(8,128)(2,1)S(1)}, u32[]{:S(2)}, u32[]{:S(2)}) %collective-permute-start.3) | collective-permute-done | bytes 160832 | tf_op jit(solution)/shard_map/ppermute | solution.py:38
  34.5 8.3 %fusion.120 = (f32[8,128]{1,0:T(8,128)S(1)}, f32[200,8,128]{0,2,1:T(8,128)S(1)}) fusion(bf16[200,11,134]{0,2,1:T(8,128)(2,1)S(1)} %get-tuple-element.85, f32[200]{0:T(256)S(1)} %bitcast.312, f32[200]{0:T(256)S(1)} %bitcast.313, f32[200]{0:T(256)S(1)} %bitcast.266, f32[200]{0:T(256)S(1)} %bitcast.267, f32[200]{0:T(256)S(1)} %bitcast.268, ...), kind=kLoop, calls=%fused_computation.270 | loop fusion | flops 33790976 | bytes 18494496 | tf_op jit(solution)/shard_map/reduce_sum | solution.py:96
  53.4 3.7 %fusion.109 = (f32[200]{0:T(256)S(1)}, f32[200]{0:T(256)S(1)}, f32[200]{0:T(256)S(1)}, f32[200]{0:T(256)S(1)}, f32[200]{0:T(256)S(1)}, /*index=5*/f32[200]{0:T(2...) fusion(bf16[200,11,134]{0,2,1:T(8,128)(2,1)S(1)} %get-tuple-ele, ...), kind=kLoop, calls=%fused_computation.214 | loop fusion | flops 11055600 | bytes 8206400 | tf_op jit(solution)/shard_map/reduce_sum | solution.py:91
  57.1 4.0 %fusion.59 = (f32[200]{0:T(256)}, f32[200]{0:T(256)}, f32[200]{0:T(256)}, f32[200]{0:T(256)}, f32[200]{0:T(256)}, /*index=5*/f32[200]{0:T(256)}, f32[200]{0:T(25...) fusion(bf16[200,11,134]{0,2,1:T(8,128)(2,1)S(1)} %get-tuple-ele, ...), kind=kLoop, calls=%fused_computation.164 | loop fusion | flops 11055600 | bytes 8206400 | tf_op jit(solution)/shard_map/reduce_sum | solution.py:91
  67.7 3.1 %convolution_multiply_fusion = f32[800,200]{0,1:T(8,128)} fusion(bf16[800,1024]{1,0:T(8,128)(2,1)} %get-tuple-element.143, bf16[25,8,8,128]{3,2,1,0:T(8,128)(2,1)} %bitcast.326, bf16[1024]{0:T(1024)(128)(2,1)S(1)} %bitcast.227), kind=kOutput, calls=%fused_computation.115 | convolution fusion | flops 328044800 | bytes 2690048 | tf_op jit(solution)/shard_map/dot_general | solution.py:109
  82.1 3.7 %stack.199 = f32[200,49]{0,1:T(8,128)S(1)} concatenate(f32[200,1]{0,1:T(1,128)} %bitcast.317, f32[200,1]{0,1:T(1,128)} %bitcast.318, f32[200,1]{0,1:T(1,128)} %bitcast.319, f32[200,1]{0,1:T(1,128)} %bitcast.264, f32[200,1]{0,1:T(1,128)} %bitcast.263, f32[200,1]{0,1:T(1,128)} %bitcast.262, f32[200,1]{0,1:T(1,128)} %bitcast.261, f32[200,1]{0,1:T(1,128)} %bitcast.260, ...), dimensions={1} | concatenate | bytes 78400 | tf_op jit(solution)/shard_map/stack | solution.py:92
  86.8 10.3 %concatenate.109 = f32[330000]{0:T(1024)S(1)} concatenate(f32[160000]{0:T(1024)} %reshape.158, f32[160000]{0:T(1024)} %reshape.159, f32[200]{0:T(256)S(1)} %broadcast_multiply_fusion.4, f32[9800]{0:T(1024)S(1)} %mul.1016), dimensions={0} | concatenate | bytes 2640000 | tf_op jit(solution)/shard_map/concatenate | solution.py:164
  98.0 4.2 %collective-permute-start.5 = (f32[1408,128]{1,0:T(8,128)}, f32[1408,128]{1,0:T(8,128)}, u32[]{:S(2)}, u32[]{:S(2)}) collective-permute-start(f32[1408,128]{1,0:T(8,128)} %fusion.111), channel_id=1, source_target_pairs={{0,4},{4,0},{8,12},{12,8},{16,20},{20,16},{24,28},{28,24},{32,36},... | collective-permute-start | bytes 2162696 | tf_op jit(solution)/shard_map/ppermute | solution.py:33
  107.5 9.6 %collective-permute-done.6 = f32[704,128]{1,0:T(8,128)S(1)} collective-permute-done((f32[704,128]{1,0:T(8,128)S(1)}, f32[704,128]{1,0:T(8,128)S(1)}, u32[]{:S(2)}, u32[]{:S(2)}) %collective-permute-start.6) | collective-permute-done | bytes 360480 | tf_op jit(solution)/shard_map/ppermute | solution.py:33
  119.2 4.8 %collective-permute-done.7 = f32[352,128]{1,0:T(8,128)S(1)} collective-permute-done((f32[352,128]{1,0:T(8,128)S(1)}, f32[352,128]{1,0:T(8,128)S(1)}, u32[]{:S(2)}, u32[]{:S(2)}) %collective-permute-start.7) | collective-permute-done | bytes 180256 | tf_op jit(solution)/shard_map/ppermute | solution.py:33
  124.0 3.6 %collective-permute-start.8 = (f32[176,128]{1,0:T(8,128)S(1)}, f32[176,128]{1,0:T(8,128)S(1)}, u32[]{:S(2)}, u32[]{:S(2)}) collective-permute-start(f32[176,128]{1,0:T(8,128)S(1)} %slice_select_fusion.2), channel_id=1, source_target_pairs={{0,128},{128,0},{256,384},{384,256},{1,129},{129,1},{257,385},{385... | collective-permute-start | bytes 270344 | tf_op jit(solution)/shard_map/ppermute | solution.py:33
  130.2 3.1 %collective-permute-start.9 = (f32[88,128]{1,0:T(8,128)S(1)}, f32[88,128]{1,0:T(8,128)S(1)}, u32[]{:S(2)}, u32[]{:S(2)}) collective-permute-start(f32[88,128]{1,0:T(8,128)S(1)} %slice_select_fusion.3), channel_id=1, source_target_pairs={{0,64},{4,68},{8,72},{12,76},{16,80},{20,84},{24,88},{28,92},{32,9... | collective-permute-start | bytes 135176 | tf_op jit(solution)/shard_map/ppermute | solution.py:33
  135.1 6.4 %collective-permute-start.10 = (f32[88,128]{1,0:T(8,128)S(1)}, f32[88,128]{1,0:T(8,128)S(1)}, u32[]{:S(2)}, u32[]{:S(2)}) collective-permute-start(f32[88,128]{1,0:T(8,128)S(1)} %select_add_fusion.4), channel_id=1, source_target_pairs={{0,2},{1,3},{2,0},{3,1},{4,6},{5,7},{6,4},{7,5},{8,10},{9,11},{10,... | collective-permute-start | bytes 135176 | tf_op jit(solution)/shard_map/ppermute | solution.py:33
  144.8 4.2 %collective-permute-done.11 = f32[88,128]{1,0:T(8,128)S(1)} collective-permute-done((f32[88,128]{1,0:T(8,128)S(1)}, f32[88,128]{1,0:T(8,128)S(1)}, u32[]{:S(2)}, u32[]{:S(2)}) %collective-permute-start.11) | collective-permute-done | bytes 45088 | tf_op jit(solution)/shard_map/ppermute | solution.py:33
  149.1 6.8 %collective-permute-start.12 = (f32[88,128]{1,0:T(8,128)S(1)}, f32[88,128]{1,0:T(8,128)S(1)}, u32[]{:S(2)}, u32[]{:S(2)}) collective-permute-start(f32[88,128]{1,0:T(8,128)S(1)} %add.257), channel_id=1, source_target_pairs={{0,256},{128,384},{256,0},{384,128},{1,257},{129,385},{257,1},{385... | collective-permute-start | bytes 135176 | tf_op jit(solution)/shard_map/ppermute | solution.py:33
  157.8 6.1 %collective-permute-start.13 = (f32[88,128]{1,0:T(8,128)S(1)}, f32[88,128]{1,0:T(8,128)S(1)}, u32[]{:S(2)}, u32[]{:S(2)}) collective-permute-start(f32[88,128]{1,0:T(8,128)S(1)} %add.258), channel_id=1, source_target_pairs={{0,32},{4,36},{8,40},{12,44},{16,48},{20,52},{24,56},{28,60},{32,0... | collective-permute-start | bytes 135176 | tf_op jit(solution)/shard_map/ppermute | solution.py:33
  171.3 4.5 %collective-permute-start.15 = (f32[176,128]{1,0:T(8,128)S(1)}, f32[176,128]{1,0:T(8,128)S(1)}, u32[]{:S(2)}, u32[]{:S(2)}) collective-permute-start(f32[176,128]{1,0:T(8,128)S(1)} %maximum_select_fusion.4), channel_id=1, source_target_pairs={{0,128},{128,0},{256,384},{384,256},{1,129},{129,1},{257,385},{385... | collective-permute-start | bytes 270344 | tf_op jit(solution)/shard_map/ppermute | solution.py:33
  179.6 4.3 %collective-permute-done.16 = f32[352,128]{1,0:T(8,128)S(1)} collective-permute-done((f32[352,128]{1,0:T(8,128)S(1)}, f32[352,128]{1,0:T(8,128)S(1)}, u32[]{:S(2)}, u32[]{:S(2)}) %collective-permute-start.16) | collective-permute-done | bytes 180256 | tf_op jit(solution)/shard_map/ppermute | solution.py:33
  186.9 5.2 %collective-permute-done.17 = f32[704,128]{1,0:T(8,128)S(1)} collective-permute-done((f32[704,128]{1,0:T(8,128)S(1)}, f32[704,128]{1,0:T(8,128)S(1)}, u32[]{:S(2)}, u32[]{:S(2)}) %collective-permute-start.17) | collective-permute-done | bytes 360480 | tf_op jit(solution)/shard_map/ppermute | solution.py:33
  192.2 14.6 %collective-permute-start.18 = (f32[1408,128]{1,0:T(8,128)S(1)}, f32[1408,128]{1,0:T(8,128)S(1)}, u32[]{:S(2)}, u32[]{:S(2)}) collective-permute-start(f32[1408,128]{1,0:T(8,128)S(1)} %maximum_select_fusion.1), channel_id=1, source_target_pairs={{0,4},{4,0},{8,12},{12,8},{16,20},{20,16},{24,28},{28,24},{32,36},... | collective-permute-start | bytes 2162696 | tf_op jit(solution)/shard_map/ppermute | solution.py:33
  (124 shorter events, 75.5 us)
Async XLA Ops:
  0.6 44.7 %copy-start = (bf16[200,800]{1,0:T(8,128)(2,1)S(1)}, bf16[200,800]{1,0:T(8,128)(2,1)}, u32[]{:S(2)}) copy-start(bf16[200,800]{1,0:T(8,128)(2,1)} %param.11) | copy-start | bytes 960004
  3.5 10.8 %collective-permute-start = (bf16[200,8,3]{0,2,1:T(4,128)(2,1)S(1)}, bf16[200,8,3]{0,2,1:T(4,128)(2,1)S(1)}, u32[]{:S(2)}, u32[]{:S(2)}) collective-permute-start(bf16[200,8,3]{0,2,1:T(4,128)(2,1)S(1)} %get-tuple-element.88), channel_id=1, source_target_pairs={{0,4},{4,8},{8,12},{12,16},{16,20},{20,24},{24,28},{28,32},{32,36}... | collective-permute-start | bytes 28808 | tf_op jit(solution)/shard_map/ppermute | solution.py:23
  8.1 6.9 %collective-permute-start.1 = (bf16[200,8,3]{0,2,1:T(4,128)(2,1)S(1)}, bf16[200,8,3]{0,2,1:T(4,128)(2,1)S(1)}, u32[]{:S(2)}, u32[]{:S(2)}) collective-permute-start(bf16[200,8,3]{0,2,1:T(4,128)(2,1)S(1)} %get-tuple-element.89), channel_id=1, source_target_pairs={{4,0},{8,4},{12,8},{16,12},{20,16},{24,20},{28,24},{32,28},{36,32}... | collective-permute-start | bytes 28808 | tf_op jit(solution)/shard_map/ppermute | solution.py:25
  15.2 13.4 %collective-permute-start.2 = (bf16[200,3,134]{0,2,1:T(8,128)(2,1)S(1)}, bf16[200,3,134]{0,2,1:T(8,128)(2,1)S(1)}, u32[]{:S(2)}, u32[]{:S(2)}) collective-permute-start(bf16[200,3,134]{0,2,1:T(8,128)(2,1)S(1)} %get-tuple-element.87), channel_id=1, source_target_pairs={{0,1},{1,2},{2,3},{3,0},{4,5},{5,6},{6,7},{7,4},{8,9},{9,10},{10,1... | collective-permute-start | bytes 482408 | tf_op jit(solution)/shard_map/ppermute | solution.py:23
  18.1 16.1 %collective-permute-start.3 = (bf16[200,3,134]{0,2,1:T(8,128)(2,1)S(1)}, bf16[200,3,134]{0,2,1:T(8,128)(2,1)S(1)}, u32[]{:S(2)}, u32[]{:S(2)}) collective-permute-start(bf16[200,3,134]{0,2,1:T(8,128)(2,1)S(1)} %rev.3), channel_id=1, source_target_pairs={{0,124},{4,120},{8,116},{12,112},{16,108},{20,104},{24,100},{28,96... | collective-permute-start | bytes 482408 | tf_op jit(solution)/shard_map/ppermute | solution.py:38
  23.7 10.5 %collective-permute-start.4 = (bf16[200,3,134]{0,2,1:T(8,128)(2,1)S(1)}, bf16[200,3,134]{0,2,1:T(8,128)(2,1)S(1)}, u32[]{:S(2)}, u32[]{:S(2)}) collective-permute-start(bf16[200,3,134]{0,2,1:T(8,128)(2,1)S(1)} %get-tuple-element.86), channel_id=1, source_target_pairs={{1,0},{2,1},{3,2},{0,3},{5,4},{6,5},{7,6},{4,7},{9,8},{10,9},{11,1... | collective-permute-start | bytes 482408 | tf_op jit(solution)/shard_map/ppermute | solution.py:25
  98.0 6.3 %collective-permute-start.5 = (f32[1408,128]{1,0:T(8,128)}, f32[1408,128]{1,0:T(8,128)}, u32[]{:S(2)}, u32[]{:S(2)}) collective-permute-start(f32[1408,128]{1,0:T(8,128)} %fusion.111), channel_id=1, source_target_pairs={{0,4},{4,0},{8,12},{12,8},{16,20},{20,16},{24,28},{28,24},{32,36},... | collective-permute-start | bytes 2162696 | tf_op jit(solution)/shard_map/ppermute | solution.py:33
  105.6 11.5 %collective-permute-start.6 = (f32[704,128]{1,0:T(8,128)S(1)}, f32[704,128]{1,0:T(8,128)S(1)}, u32[]{:S(2)}, u32[]{:S(2)}) collective-permute-start(f32[704,128]{1,0:T(8,128)S(1)} %slice_select_fusion), channel_id=1, source_target_pairs={{0,1},{1,0},{2,3},{3,2},{4,5},{5,4},{6,7},{7,6},{8,9},{9,8},{10,11... | collective-permute-start | bytes 1081352 | tf_op jit(solution)/shard_map/ppermute | solution.py:33
  117.2 6.7 %collective-permute-start.7 = (f32[352,128]{1,0:T(8,128)S(1)}, f32[352,128]{1,0:T(8,128)S(1)}, u32[]{:S(2)}, u32[]{:S(2)}) collective-permute-start(f32[352,128]{1,0:T(8,128)S(1)} %slice_select_fusion.1), channel_id=1, source_target_pairs={{0,8},{4,12},{8,0},{12,4},{16,24},{20,28},{24,16},{28,20},{32,40},... | collective-permute-start | bytes 540680 | tf_op jit(solution)/shard_map/ppermute | solution.py:33
  124.0 6.2 %collective-permute-start.8 = (f32[176,128]{1,0:T(8,128)S(1)}, f32[176,128]{1,0:T(8,128)S(1)}, u32[]{:S(2)}, u32[]{:S(2)}) collective-permute-start(f32[176,128]{1,0:T(8,128)S(1)} %slice_select_fusion.2), channel_id=1, source_target_pairs={{0,128},{128,0},{256,384},{384,256},{1,129},{129,1},{257,385},{385... | collective-permute-start | bytes 270344 | tf_op jit(solution)/shard_map/ppermute | solution.py:33
  130.2 4.8 %collective-permute-start.9 = (f32[88,128]{1,0:T(8,128)S(1)}, f32[88,128]{1,0:T(8,128)S(1)}, u32[]{:S(2)}, u32[]{:S(2)}) collective-permute-start(f32[88,128]{1,0:T(8,128)S(1)} %slice_select_fusion.3), channel_id=1, source_target_pairs={{0,64},{4,68},{8,72},{12,76},{16,80},{20,84},{24,88},{28,92},{32,9... | collective-permute-start | bytes 135176 | tf_op jit(solution)/shard_map/ppermute | solution.py:33
  135.0 71.8 %copy-start.6 = (bf16[800,1024]{1,0:T(8,128)(2,1)S(1)}, bf16[800,1024]{1,0:T(8,128)(2,1)}, u32[]{:S(2)}) copy-start(bf16[800,1024]{1,0:T(8,128)(2,1)} %get-tuple-element.143) | copy-start | bytes 4915204
  135.0 71.8 %copy-start.10 = (bf16[1,200,8,128]{3,2,1,0:T(8,128)(2,1)S(1)}, bf16[1,200,8,128]{3,2,1,0:T(8,128)(2,1)}, u32[]{:S(2)}) copy-start(bf16[1,200,8,128]{3,2,1,0:T(8,128)(2,1)} %param.7) | copy-start | bytes 1228804
  135.1 71.8 %copy-start.17 = (f32[1024]{0:T(1024)S(1)}, f32[1024]{0:T(1024)}, u32[]{:S(2)}) copy-start(f32[1024]{0:T(1024)} %get-tuple-element.139) | copy-start | bytes 12292
  135.1 71.8 %copy-start.20 = (bf16[800,200]{0,1:T(8,128)(2,1)S(1)}, bf16[800,200]{0,1:T(8,128)(2,1)}, u32[]{:S(2)}) copy-start(bf16[800,200]{0,1:T(8,128)(2,1)} %param.12) | copy-start | bytes 960004
  135.1 7.8 %collective-permute-start.10 = (f32[88,128]{1,0:T(8,128)S(1)}, f32[88,128]{1,0:T(8,128)S(1)}, u32[]{:S(2)}, u32[]{:S(2)}) collective-permute-start(f32[88,128]{1,0:T(8,128)S(1)} %select_add_fusion.4), channel_id=1, source_target_pairs={{0,2},{1,3},{2,0},{3,1},{4,6},{5,7},{6,4},{7,5},{8,10},{9,11},{10,... | collective-permute-start | bytes 135176 | tf_op jit(solution)/shard_map/ppermute | solution.py:33
  142.9 6.2 %collective-permute-start.11 = (f32[88,128]{1,0:T(8,128)S(1)}, f32[88,128]{1,0:T(8,128)S(1)}, u32[]{:S(2)}, u32[]{:S(2)}) collective-permute-start(f32[88,128]{1,0:T(8,128)S(1)} %add.256), channel_id=1, source_target_pairs={{0,16},{4,20},{8,24},{12,28},{16,0},{20,4},{24,8},{28,12},{32,48},... | collective-permute-start | bytes 135176 | tf_op jit(solution)/shard_map/ppermute | solution.py:33
  149.1 8.7 %collective-permute-start.12 = (f32[88,128]{1,0:T(8,128)S(1)}, f32[88,128]{1,0:T(8,128)S(1)}, u32[]{:S(2)}, u32[]{:S(2)}) collective-permute-start(f32[88,128]{1,0:T(8,128)S(1)} %add.257), channel_id=1, source_target_pairs={{0,256},{128,384},{256,0},{384,128},{1,257},{129,385},{257,1},{385... | collective-permute-start | bytes 135176 | tf_op jit(solution)/shard_map/ppermute | solution.py:33
  157.8 8.7 %collective-permute-start.13 = (f32[88,128]{1,0:T(8,128)S(1)}, f32[88,128]{1,0:T(8,128)S(1)}, u32[]{:S(2)}, u32[]{:S(2)}) collective-permute-start(f32[88,128]{1,0:T(8,128)S(1)} %add.258), channel_id=1, source_target_pairs={{0,32},{4,36},{8,40},{12,44},{16,48},{20,52},{24,56},{28,60},{32,0... | collective-permute-start | bytes 135176 | tf_op jit(solution)/shard_map/ppermute | solution.py:33
  166.5 4.8 %collective-permute-start.14 = (f32[88,128]{1,0:T(8,128)S(1)}, f32[88,128]{1,0:T(8,128)S(1)}, u32[]{:S(2)}, u32[]{:S(2)}) collective-permute-start(f32[88,128]{1,0:T(8,128)S(1)} %add.259), channel_id=1, source_target_pairs={{0,64},{4,68},{8,72},{12,76},{16,80},{20,84},{24,88},{28,92},{32,9... | collective-permute-start | bytes 135176 | tf_op jit(solution)/shard_map/ppermute | solution.py:33
  171.3 6.4 %collective-permute-start.15 = (f32[176,128]{1,0:T(8,128)S(1)}, f32[176,128]{1,0:T(8,128)S(1)}, u32[]{:S(2)}, u32[]{:S(2)}) collective-permute-start(f32[176,128]{1,0:T(8,128)S(1)} %maximum_select_fusion.4), channel_id=1, source_target_pairs={{0,128},{128,0},{256,384},{384,256},{1,129},{129,1},{257,385},{385... | collective-permute-start | bytes 270344 | tf_op jit(solution)/shard_map/ppermute | solution.py:33
  177.7 6.2 %collective-permute-start.16 = (f32[352,128]{1,0:T(8,128)S(1)}, f32[352,128]{1,0:T(8,128)S(1)}, u32[]{:S(2)}, u32[]{:S(2)}) collective-permute-start(f32[352,128]{1,0:T(8,128)S(1)} %maximum_select_fusion.3), channel_id=1, source_target_pairs={{0,8},{4,12},{8,0},{12,4},{16,24},{20,28},{24,16},{28,20},{32,40},... | collective-permute-start | bytes 540680 | tf_op jit(solution)/shard_map/ppermute | solution.py:33
  184.0 8.2 %collective-permute-start.17 = (f32[704,128]{1,0:T(8,128)S(1)}, f32[704,128]{1,0:T(8,128)S(1)}, u32[]{:S(2)}, u32[]{:S(2)}) collective-permute-start(f32[704,128]{1,0:T(8,128)S(1)} %maximum_select_fusion.2), channel_id=1, source_target_pairs={{0,1},{1,0},{2,3},{3,2},{4,5},{5,4},{6,7},{7,6},{8,9},{9,8},{10,11... | collective-permute-start | bytes 1081352 | tf_op jit(solution)/shard_map/ppermute | solution.py:33
  192.2 16.4 %collective-permute-start.18 = (f32[1408,128]{1,0:T(8,128)S(1)}, f32[1408,128]{1,0:T(8,128)S(1)}, u32[]{:S(2)}, u32[]{:S(2)}) collective-permute-start(f32[1408,128]{1,0:T(8,128)S(1)} %maximum_select_fusion.1), channel_id=1, source_target_pairs={{0,4},{4,0},{8,12},{12,8},{16,20},{20,16},{24,28},{28,24},{32,36},... | collective-permute-start | bytes 2162696 | tf_op jit(solution)/shard_map/ppermute | solution.py:33
  (16 other events, 79.9 us)

commit v2 on v1

--- a/solution.py
+++ b/solution.py
@@ -39,8 +39,8 @@
 
 
 REDUCE_ORDER = (
-    ("lon", 0), ("lat", 0), ("lon", 1), ("ens", 0), ("lon", 4),
-    ("lat", 1), ("lon", 2), ("ens", 1), ("lon", 3),
+    ("lon", 0), ("lat", 0), ("lon", 1), ("lon", 4), ("lat", 1),
+    ("lon", 2), ("ens", 0), ("lon", 3), ("ens", 1),
 )
 
 
@@ -50,7 +50,7 @@
         if (1 << bit) >= lax.axis_size(axis):
             continue
         upper = (lax.axis_index(axis) >> bit) & 1
-        if flat.shape[0] % 16 == 0:
+        if flat.shape[0] % 2 == 0 and flat.shape[0] >= 8:
             half = flat.shape[0] // 2
             low, high = flat[:half], flat[half:]
             keep = jnp.where(upper == 0, low, high)
@@ -160,23 +160,23 @@
     grad_reduce = grad_reduce * grad_scale
     grad_gain = grad_gain * grad_scale
     grad_depthwise = grad_depthwise * grad_scale
-    pieces = (grad_expand, grad_reduce, grad_gain, grad_depthwise)
-    flat = jnp.concatenate([piece.reshape(-1) for piece in pieces])
-    lanes = 128
-    rows = -(-flat.shape[0] // (lanes * 256)) * 256
-    flat = jnp.pad(flat, (0, rows * lanes - flat.shape[0])).reshape(rows, lanes)
+    width = grad_expand.shape[1]
+    small = jnp.concatenate([grad_depthwise, grad_gain[:, None]], axis=1).reshape(-1)
+    small_rows = -(-small.shape[0] // width)
+    small_rows += -small_rows % 8
+    small = jnp.pad(small, (0, small_rows * width - small.shape[0])).reshape(small_rows, width)
+    packed = jnp.concatenate([grad_expand, grad_reduce.T, small], axis=0)
     steps = [(axis, bit) for axis, bit in REDUCE_ORDER]
     for axis in ("ens", "lon", "lat"):
         for bit in range(lax.axis_size(axis).bit_length() - 1):
             if (axis, bit) not in steps:
                 steps.append((axis, bit))
-    flat = tree_psum(flat, steps, jnp.float32).reshape(-1)
-    summed = []
-    offset = 0
-    for piece in pieces:
-        summed.append(flat[offset : offset + piece.size].reshape(piece.shape))
-        offset += piece.size
-    grad_expand, grad_reduce, grad_gain, grad_depthwise = summed
+    packed = tree_psum(packed, steps, jnp.float32)
+    grad_expand = packed[:channels]
+    grad_reduce = packed[channels : 2 * channels].T
+    small = packed[2 * channels :].reshape(-1)[: channels * (KS * KS + 1)].reshape(channels, -1)
+    grad_depthwise = small[:, : KS * KS]
+    grad_gain = small[:, KS * KS]
     next_state = out_flat.reshape(channels, tile_rows, tile_cols)[None]
     return (next_state, grad_depthwise, grad_gain, grad_expand, grad_reduce)
 

time: 216 us -> 190 us (0.88)
  local copies, waits for them, and re-layouts: 39.4 us -> 13.6 us
  waiting for transfers between devices: 50.9 us -> 58.8 us
  starting transfers between devices: 85.8 us -> 81.3 us
    concatenate x3 -> x1, local copies, waits for them, and re-layouts: 15.6 us -> 0.11 us  [body(): jnp.concatenate([grad_depthwise, grad_gain[:, None]], axis=1).reshape(-1)]
    ppermute x14, waiting for transfers between devices: 44.6 us -> 52.4 us  [swapped(): lax.ppermute(array, axis, [(i, i ^ 1 << stride) for i in range(lax.axis_s...]
    reshape x5 -> x2, local copies, waits for them, and re-layouts: 8.04 us -> 0.23 us  [the longest x1 0.13 us: body(): jnp.concatenate([grad_depthwise, grad_gain[:, None]], axis=1).reshape(-1)]
    ppermute x14, starting transfers between devices: 62.7 us -> 58.2 us  [swapped(): lax.ppermute(array, axis, [(i, i ^ 1 << stride) for i in range(lax.axis_s...]
    mul x3 -> x0, local copies, waits for them, and re-layouts: 2.6 us -> none  [the longest x1 2.29 us: body(): grad_reduce = grad_reduce * grad_scale]
    unnamed x46 -> x27, local copies, waits for them, and re-layouts: 4.6 us -> 3.42 us
where the time goes in v2:
time: 190 us; the launch traced here: 189 us
  starting transfers between devices  81.3 us (43%)
  waiting for transfers between devices  58.8 us (31%)
  other arithmetic  24 us (13%)
  local copies, waits for them, and re-layouts  13.6 us (7%)
  matrix products  9.87 us (5%)
    ppermute x14, starting transfers between devices, swapped(): lax.ppermute(array, axis, [(i, i ^ 1 << stride) for i in range(lax.axis_s...  58.2 us
    ppermute x14, waiting for transfers between devices, swapped(): lax.ppermute(array, axis, [(i, i ^ 1 << stride) for i in range(lax.axis_s...  52.4 us
    reduce_sum x4, other arithmetic, depthwise_grad(): columns.append(jnp.sum(d_conv * window, axis=(1, 2)))  11.8 us
    ppermute x2, starting transfers between devices, with_halo(): lax.ppermute(head, axis, [((i + 1) % count, i) for i in range(count)])  11 us
    reduce_sum x1, other arithmetic, cell_pass(): chan_mean = jnp.mean(conv_blk, axis=0, keepdims=True)  8.31 us
    ppermute x2, starting transfers between devices, with_halo(): lax.ppermute(tail, axis, [(i, (i + 1) % count) for i in range(count)])  6.52 us
    ppermute x1, starting transfers between devices, mirrored_across(): return lax.ppermute(array, axis, [(i, count - 1 - i) for i in range(count)])  5.6 us
    ppermute x1, waiting for transfers between devices, mirrored_across(): return lax.ppermute(array, axis, [(i, count - 1 - i) for i in range(count)])  5.57 us
  transfers between devices with their start and end apart: 19, of which 16 were waited for; matrix products, arithmetic and copies ran while one was open for 1% of the time, Pallas kernels for 0%

profile of v2, /device:TPU:1, one launch (start us, length us, event | category | flops | bytes accessed | tf_op | source)
XLA Modules:
  0.0 188.7 jit_solution(3223356192333674958)
XLA Ops:
  3.5 4.6 %collective-permute-start = (bf16[200,8,3]{0,2,1:T(4,128)(2,1)S(1)}, bf16[200,8,3]{0,2,1:T(4,128)(2,1)S(1)}, u32[]{:S(2)}, u32[]{:S(2)}) collective-permute-start(bf16[200,8,3]{0,2,1:T(4,128)(2,1)S(1)} %get-tuple-element.88), channel_id=1, source_target_pairs={{0,4},{4,8},{8,12},{12,16},{16,20},{20,24},{24,28},{28,32},{32,36}... | collective-permute-start | bytes 28808 | tf_op jit(solution)/shard_map/ppermute | solution.py:23
  8.1 6.1 %collective-permute-start.1 = (bf16[200,8,3]{0,2,1:T(4,128)(2,1)S(1)}, bf16[200,8,3]{0,2,1:T(4,128)(2,1)S(1)}, u32[]{:S(2)}, u32[]{:S(2)}) collective-permute-start(bf16[200,8,3]{0,2,1:T(4,128)(2,1)S(1)} %get-tuple-element.89), channel_id=1, source_target_pairs={{4,0},{8,4},{12,8},{16,12},{20,16},{24,20},{28,24},{32,28},{36,32}... | collective-permute-start | bytes 28808 | tf_op jit(solution)/shard_map/ppermute | solution.py:25
  18.1 5.6 %collective-permute-start.3 = (bf16[200,3,134]{0,2,1:T(8,128)(2,1)S(1)}, bf16[200,3,134]{0,2,1:T(8,128)(2,1)S(1)}, u32[]{:S(2)}, u32[]{:S(2)}) collective-permute-start(bf16[200,3,134]{0,2,1:T(8,128)(2,1)S(1)} %rev.3), channel_id=1, source_target_pairs={{0,124},{4,120},{8,116},{12,112},{16,108},{20,104},{24,100},{28,96... | collective-permute-start | bytes 482408 | tf_op jit(solution)/shard_map/ppermute | solution.py:38
  23.7 4.9 %collective-permute-start.4 = (bf16[200,3,134]{0,2,1:T(8,128)(2,1)S(1)}, bf16[200,3,134]{0,2,1:T(8,128)(2,1)S(1)}, u32[]{:S(2)}, u32[]{:S(2)}) collective-permute-start(bf16[200,3,134]{0,2,1:T(8,128)(2,1)S(1)} %get-tuple-element.86), channel_id=1, source_target_pairs={{1,0},{2,1},{3,2},{0,3},{5,4},{6,5},{7,6},{4,7},{9,8},{10,9},{11,1... | collective-permute-start | bytes 482408 | tf_op jit(solution)/shard_map/ppermute | solution.py:25
  28.6 5.6 %collective-permute-done.3 = bf16[200,3,134]{0,2,1:T(8,128)(2,1)S(1)} collective-permute-done((bf16[200,3,134]{0,2,1:T(8,128)(2,1)S(1)}, bf16[200,3,134]{0,2,1:T(8,128)(2,1)S(1)}, u32[]{:S(2)}, u32[]{:S(2)}) %collective-permute-start.3) | collective-permute-done | bytes 160832 | tf_op jit(solution)/shard_map/ppermute | solution.py:38
  34.5 8.3 %fusion.119 = (f32[8,128]{1,0:T(8,128)S(1)}, f32[200,8,128]{0,2,1:T(8,128)S(1)}) fusion(bf16[200,11,134]{0,2,1:T(8,128)(2,1)S(1)} %get-tuple-element.85, f32[200]{0:T(256)S(1)} %bitcast.306, f32[200]{0:T(256)S(1)} %bitcast.307, f32[200]{0:T(256)S(1)} %bitcast.260, f32[200]{0:T(256)S(1)} %bitcast.261, f32[200]{0:T(256)S(1)} %bitcast.262, ...), kind=kLoop, calls=%fused_computation.272 | loop fusion | flops 33790976 | bytes 18494496 | tf_op jit(solution)/shard_map/reduce_sum | solution.py:96
  55.1 3.8 %fusion.109 = (f32[200]{0:T(256)S(1)}, f32[200]{0:T(256)S(1)}, f32[200]{0:T(256)S(1)}, f32[200]{0:T(256)S(1)}, f32[200]{0:T(256)S(1)}, /*index=5*/f32[200]{0:T(2...) fusion(bf16[200,11,134]{0,2,1:T(8,128)(2,1)S(1)} %get-tuple-ele, ...), kind=kLoop, calls=%fused_computation.213 | loop fusion | flops 11055600 | bytes 8206400 | tf_op jit(solution)/shard_map/reduce_sum | solution.py:91
  58.9 3.8 %fusion.59 = (f32[200]{0:T(256)}, f32[200]{0:T(256)}, f32[200]{0:T(256)}, f32[200]{0:T(256)}, f32[200]{0:T(256)}, /*index=5*/f32[200]{0:T(256)}, f32[200]{0:T(25...) fusion(bf16[200,11,134]{0,2,1:T(8,128)(2,1)S(1)} %get-tuple-ele, ...), kind=kLoop, calls=%fused_computation.163 | loop fusion | flops 11055600 | bytes 8206400 | tf_op jit(solution)/shard_map/reduce_sum | solution.py:91
  65.6 3.7 %stack.199 = f32[200,49]{0,1:T(8,128)S(1)} concatenate(f32[200,1]{0,1:T(1,128)} %bitcast.312, f32[200,1]{0,1:T(1,128)} %bitcast.313, f32[200,1]{0,1:T(1,128)} %bitcast.314, f32[200,1]{0,1:T(1,128)} %bitcast.258, f32[200,1]{0,1:T(1,128)} %bitcast.257, f32[200,1]{0,1:T(1,128)} %bitcast.256, f32[200,1]{0,1:T(1,128)} %bitcast.255, f32[200,1]{0,1:T(1,128)} %bitcast.254, ...), dimensions={1} | concatenate | bytes 78400 | tf_op jit(solution)/shard_map/stack | solution.py:92
  72.8 4.4 %collective-permute-start.5 = (f32[208,800]{1,0:T(8,128)S(1)}, f32[208,800]{1,0:T(8,128)S(1)}, u32[]{:S(2)}, u32[]{:S(2)}) collective-permute-start(f32[208,800]{1,0:T(8,128)S(1)} %fusion.110), channel_id=1, source_target_pairs={{0,4},{4,0},{8,12},{12,8},{16,20},{20,16},{24,28},{28,24},{32,36},... | collective-permute-start | bytes 1996808 | tf_op jit(solution)/shard_map/ppermute | solution.py:33
  81.0 9.8 %collective-permute-done.6 = f32[104,800]{1,0:T(8,128)S(1)} collective-permute-done((f32[104,800]{1,0:T(8,128)S(1)}, f32[104,800]{1,0:T(8,128)S(1)}, u32[]{:S(2)}, u32[]{:S(2)}) %collective-permute-start.6) | collective-permute-done | bytes 332832 | tf_op jit(solution)/shard_map/ppermute | solution.py:33
  92.9 5.2 %collective-permute-done.7 = f32[52,800]{1,0:T(8,128)S(1)} collective-permute-done((f32[52,800]{1,0:T(8,128)S(1)}, f32[52,800]{1,0:T(8,128)S(1)}, u32[]{:S(2)}, u32[]{:S(2)}) %collective-permute-start.7) | collective-permute-done | bytes 166432 | tf_op jit(solution)/shard_map/ppermute | solution.py:33
  100.1 3.6 %collective-permute-done.8 = f32[26,800]{1,0:T(8,128)S(1)} collective-permute-done((f32[26,800]{1,0:T(8,128)S(1)}, f32[26,800]{1,0:T(8,128)S(1)}, u32[]{:S(2)}, u32[]{:S(2)}) %collective-permute-start.8) | collective-permute-done | bytes 83232 | tf_op jit(solution)/shard_map/ppermute | solution.py:33
  103.8 5.7 %collective-permute-start.9 = (f32[13,800]{1,0:T(8,128)S(1)}, f32[13,800]{1,0:T(8,128)S(1)}, u32[]{:S(2)}, u32[]{:S(2)}) collective-permute-start(f32[13,800]{1,0:T(8,128)S(1)} %slice_select_fusion.3), channel_id=1, source_target_pairs={{0,2},{1,3},{2,0},{3,1},{4,6},{5,7},{6,4},{7,5},{8,10},{9,11},{10,... | collective-permute-start | bytes 124808 | tf_op jit(solution)/shard_map/ppermute | solution.py:33
  113.0 4.5 %collective-permute-done.10 = f32[13,800]{1,0:T(8,128)S(1)} collective-permute-done((f32[13,800]{1,0:T(8,128)S(1)}, f32[13,800]{1,0:T(8,128)S(1)}, u32[]{:S(2)}, u32[]{:S(2)}) %collective-permute-start.10) | collective-permute-done | bytes 41632 | tf_op jit(solution)/shard_map/ppermute | solution.py:33
  117.5 3.2 %collective-permute-start.11 = (f32[13,800]{1,0:T(8,128)S(1)}, f32[13,800]{1,0:T(8,128)S(1)}, u32[]{:S(2)}, u32[]{:S(2)}) collective-permute-start(f32[13,800]{1,0:T(8,128)S(1)} %add.256), channel_id=1, source_target_pairs={{0,128},{128,0},{256,384},{384,256},{1,129},{129,1},{257,385},{385... | collective-permute-start | bytes 124808 | tf_op jit(solution)/shard_map/ppermute | solution.py:33
  124.0 5.0 %collective-permute-start.12 = (f32[13,800]{1,0:T(8,128)S(1)}, f32[13,800]{1,0:T(8,128)S(1)}, u32[]{:S(2)}, u32[]{:S(2)}) collective-permute-start(f32[13,800]{1,0:T(8,128)S(1)} %add.257), channel_id=1, source_target_pairs={{0,32},{4,36},{8,40},{12,44},{16,48},{20,52},{24,56},{28,60},{32,0... | collective-permute-start | bytes 124808 | tf_op jit(solution)/shard_map/ppermute | solution.py:33
  129.0 4.5 %collective-permute-done.12 = f32[13,800]{1,0:T(8,128)S(1)} collective-permute-done((f32[13,800]{1,0:T(8,128)S(1)}, f32[13,800]{1,0:T(8,128)S(1)}, u32[]{:S(2)}, u32[]{:S(2)}) %collective-permute-start.12) | collective-permute-done | bytes 41632 | tf_op jit(solution)/shard_map/ppermute | solution.py:33
  133.6 6.2 %collective-permute-start.13 = (f32[13,800]{1,0:T(8,128)S(1)}, f32[13,800]{1,0:T(8,128)S(1)}, u32[]{:S(2)}, u32[]{:S(2)}) collective-permute-start(f32[13,800]{1,0:T(8,128)S(1)} %add.258), channel_id=1, source_target_pairs={{0,256},{128,384},{256,0},{384,128},{1,257},{129,385},{257,1},{385... | collective-permute-start | bytes 124808 | tf_op jit(solution)/shard_map/ppermute | solution.py:33
  142.4 4.5 %collective-permute-start.14 = (f32[13,800]{1,0:T(8,128)S(1)}, f32[13,800]{1,0:T(8,128)S(1)}, u32[]{:S(2)}, u32[]{:S(2)}) collective-permute-start(f32[13,800]{1,0:T(8,128)S(1)} %add.259), channel_id=1, source_target_pairs={{0,2},{1,3},{2,0},{3,1},{4,6},{5,7},{6,4},{7,5},{8,10},{9,11},{10,... | collective-permute-start | bytes 124808 | tf_op jit(solution)/shard_map/ppermute | solution.py:33
  150.9 3.5 %collective-permute-done.15 = f32[26,800]{1,0:T(8,128)S(1)} collective-permute-done((f32[26,800]{1,0:T(8,128)S(1)}, f32[26,800]{1,0:T(8,128)S(1)}, u32[]{:S(2)}, u32[]{:S(2)}) %collective-permute-start.15) | collective-permute-done | bytes 83232 | tf_op jit(solution)/shard_map/ppermute | solution.py:33
  156.4 4.5 %collective-permute-done.16 = f32[52,800]{1,0:T(8,128)S(1)} collective-permute-done((f32[52,800]{1,0:T(8,128)S(1)}, f32[52,800]{1,0:T(8,128)S(1)}, u32[]{:S(2)}, u32[]{:S(2)}) %collective-permute-start.16) | collective-permute-done | bytes 166432 | tf_op jit(solution)/shard_map/ppermute | solution.py:33
  163.9 5.4 %collective-permute-done.17 = f32[104,800]{1,0:T(8,128)S(1)} collective-permute-done((f32[104,800]{1,0:T(8,128)S(1)}, f32[104,800]{1,0:T(8,128)S(1)}, u32[]{:S(2)}, u32[]{:S(2)}) %collective-permute-start.17) | collective-permute-done | bytes 332832 | tf_op jit(solution)/shard_map/ppermute | solution.py:33
  169.4 14.6 %collective-permute-start.18 = (f32[208,800]{1,0:T(8,128)S(1)}, f32[208,800]{1,0:T(8,128)S(1)}, u32[]{:S(2)}, u32[]{:S(2)}) collective-permute-start(f32[208,800]{1,0:T(8,128)S(1)} %maximum_select_fusion.1), channel_id=1, source_target_pairs={{0,4},{4,0},{8,12},{12,8},{16,20},{20,16},{24,28},{28,24},{32,36},... | collective-permute-start | bytes 1996808 | tf_op jit(solution)/shard_map/ppermute | solution.py:33
  (101 shorter events, 56.4 us)
Async XLA Ops:
  0.6 44.7 %copy-start = (bf16[200,800]{1,0:T(8,128)(2,1)S(1)}, bf16[200,800]{1,0:T(8,128)(2,1)}, u32[]{:S(2)}) copy-start(bf16[200,800]{1,0:T(8,128)(2,1)} %param.11) | copy-start | bytes 960004
  3.5 10.8 %collective-permute-start = (bf16[200,8,3]{0,2,1:T(4,128)(2,1)S(1)}, bf16[200,8,3]{0,2,1:T(4,128)(2,1)S(1)}, u32[]{:S(2)}, u32[]{:S(2)}) collective-permute-start(bf16[200,8,3]{0,2,1:T(4,128)(2,1)S(1)} %get-tuple-element.88), channel_id=1, source_target_pairs={{0,4},{4,8},{8,12},{12,16},{16,20},{20,24},{24,28},{28,32},{32,36}... | collective-permute-start | bytes 28808 | tf_op jit(solution)/shard_map/ppermute | solution.py:23
  8.1 6.9 %collective-permute-start.1 = (bf16[200,8,3]{0,2,1:T(4,128)(2,1)S(1)}, bf16[200,8,3]{0,2,1:T(4,128)(2,1)S(1)}, u32[]{:S(2)}, u32[]{:S(2)}) collective-permute-start(bf16[200,8,3]{0,2,1:T(4,128)(2,1)S(1)} %get-tuple-element.89), channel_id=1, source_target_pairs={{4,0},{8,4},{12,8},{16,12},{20,16},{24,20},{28,24},{32,28},{36,32}... | collective-permute-start | bytes 28808 | tf_op jit(solution)/shard_map/ppermute | solution.py:25
  15.2 13.4 %collective-permute-start.2 = (bf16[200,3,134]{0,2,1:T(8,128)(2,1)S(1)}, bf16[200,3,134]{0,2,1:T(8,128)(2,1)S(1)}, u32[]{:S(2)}, u32[]{:S(2)}) collective-permute-start(bf16[200,3,134]{0,2,1:T(8,128)(2,1)S(1)} %get-tuple-element.87), channel_id=1, source_target_pairs={{0,1},{1,2},{2,3},{3,0},{4,5},{5,6},{6,7},{7,4},{8,9},{9,10},{10,1... | collective-permute-start | bytes 482408 | tf_op jit(solution)/shard_map/ppermute | solution.py:23
  18.1 16.1 %collective-permute-start.3 = (bf16[200,3,134]{0,2,1:T(8,128)(2,1)S(1)}, bf16[200,3,134]{0,2,1:T(8,128)(2,1)S(1)}, u32[]{:S(2)}, u32[]{:S(2)}) collective-permute-start(bf16[200,3,134]{0,2,1:T(8,128)(2,1)S(1)} %rev.3), channel_id=1, source_target_pairs={{0,124},{4,120},{8,116},{12,112},{16,108},{20,104},{24,100},{28,96... | collective-permute-start | bytes 482408 | tf_op jit(solution)/shard_map/ppermute | solution.py:38
  23.7 10.5 %collective-permute-start.4 = (bf16[200,3,134]{0,2,1:T(8,128)(2,1)S(1)}, bf16[200,3,134]{0,2,1:T(8,128)(2,1)S(1)}, u32[]{:S(2)}, u32[]{:S(2)}) collective-permute-start(bf16[200,3,134]{0,2,1:T(8,128)(2,1)S(1)} %get-tuple-element.86), channel_id=1, source_target_pairs={{1,0},{2,1},{3,2},{0,3},{5,4},{6,5},{7,6},{4,7},{9,8},{10,9},{11,1... | collective-permute-start | bytes 482408 | tf_op jit(solution)/shard_map/ppermute | solution.py:25
  72.8 6.0 %collective-permute-start.5 = (f32[208,800]{1,0:T(8,128)S(1)}, f32[208,800]{1,0:T(8,128)S(1)}, u32[]{:S(2)}, u32[]{:S(2)}) collective-permute-start(f32[208,800]{1,0:T(8,128)S(1)} %fusion.110), channel_id=1, source_target_pairs={{0,4},{4,0},{8,12},{12,8},{16,20},{20,16},{24,28},{28,24},{32,36},... | collective-permute-start | bytes 1996808 | tf_op jit(solution)/shard_map/ppermute | solution.py:33
  79.1 11.8 %collective-permute-start.6 = (f32[104,800]{1,0:T(8,128)S(1)}, f32[104,800]{1,0:T(8,128)S(1)}, u32[]{:S(2)}, u32[]{:S(2)}) collective-permute-start(f32[104,800]{1,0:T(8,128)S(1)} %slice_select_fusion), channel_id=1, source_target_pairs={{0,1},{1,0},{2,3},{3,2},{4,5},{5,4},{6,7},{7,6},{8,9},{9,8},{10,11... | collective-permute-start | bytes 998408 | tf_op jit(solution)/shard_map/ppermute | solution.py:33
  91.0 7.2 %collective-permute-start.7 = (f32[52,800]{1,0:T(8,128)S(1)}, f32[52,800]{1,0:T(8,128)S(1)}, u32[]{:S(2)}, u32[]{:S(2)}) collective-permute-start(f32[52,800]{1,0:T(8,128)S(1)} %slice_select_fusion.1), channel_id=1, source_target_pairs={{0,8},{4,12},{8,0},{12,4},{16,24},{20,28},{24,16},{28,20},{32,40},... | collective-permute-start | bytes 499208 | tf_op jit(solution)/shard_map/ppermute | solution.py:33
  98.2 5.5 %collective-permute-start.8 = (f32[26,800]{1,0:T(8,128)S(1)}, f32[26,800]{1,0:T(8,128)S(1)}, u32[]{:S(2)}, u32[]{:S(2)}) collective-permute-start(f32[26,800]{1,0:T(8,128)S(1)} %slice_select_fusion.2), channel_id=1, source_target_pairs={{0,64},{4,68},{8,72},{12,76},{16,80},{20,84},{24,88},{28,92},{32,9... | collective-permute-start | bytes 249608 | tf_op jit(solution)/shard_map/ppermute | solution.py:33
  103.8 7.3 %collective-permute-start.9 = (f32[13,800]{1,0:T(8,128)S(1)}, f32[13,800]{1,0:T(8,128)S(1)}, u32[]{:S(2)}, u32[]{:S(2)}) collective-permute-start(f32[13,800]{1,0:T(8,128)S(1)} %slice_select_fusion.3), channel_id=1, source_target_pairs={{0,2},{1,3},{2,0},{3,1},{4,6},{5,7},{6,4},{7,5},{8,10},{9,11},{10,... | collective-permute-start | bytes 124808 | tf_op jit(solution)/shard_map/ppermute | solution.py:33
  111.1 6.4 %collective-permute-start.10 = (f32[13,800]{1,0:T(8,128)S(1)}, f32[13,800]{1,0:T(8,128)S(1)}, u32[]{:S(2)}, u32[]{:S(2)}) collective-permute-start(f32[13,800]{1,0:T(8,128)S(1)} %select_add_fusion.4), channel_id=1, source_target_pairs={{0,16},{4,20},{8,24},{12,28},{16,0},{20,4},{24,8},{28,12},{32,48},... | collective-permute-start | bytes 124808 | tf_op jit(solution)/shard_map/ppermute | solution.py:33
  117.5 6.4 %collective-permute-start.11 = (f32[13,800]{1,0:T(8,128)S(1)}, f32[13,800]{1,0:T(8,128)S(1)}, u32[]{:S(2)}, u32[]{:S(2)}) collective-permute-start(f32[13,800]{1,0:T(8,128)S(1)} %add.256), channel_id=1, source_target_pairs={{0,128},{128,0},{256,384},{384,256},{1,129},{129,1},{257,385},{385... | collective-permute-start | bytes 124808 | tf_op jit(solution)/shard_map/ppermute | solution.py:33
  123.9 60.1 %copy-start.3 = (bf16[800,1024]{1,0:T(8,128)(2,1)S(1)}, bf16[800,1024]{1,0:T(8,128)(2,1)}, u32[]{:S(2)}) copy-start(bf16[800,1024]{1,0:T(8,128)(2,1)} %get-tuple-element.143) | copy-start | bytes 4915204
  124.0 60.1 %copy-start.5 = (bf16[1,200,8,128]{3,2,1,0:T(8,128)(2,1)S(1)}, bf16[1,200,8,128]{3,2,1,0:T(8,128)(2,1)}, u32[]{:S(2)}) copy-start(bf16[1,200,8,128]{3,2,1,0:T(8,128)(2,1)} %param.7) | copy-start | bytes 1228804
  124.0 60.1 %copy-start.8 = (f32[1024]{0:T(1024)S(1)}, f32[1024]{0:T(1024)}, u32[]{:S(2)}) copy-start(f32[1024]{0:T(1024)} %get-tuple-element.139) | copy-start | bytes 12292
  124.0 60.0 %copy-start.11 = (bf16[800,200]{0,1:T(8,128)(2,1)S(1)}, bf16[800,200]{0,1:T(8,128)(2,1)}, u32[]{:S(2)}) copy-start(bf16[800,200]{0,1:T(8,128)(2,1)} %param.12) | copy-start | bytes 960004
  124.0 9.6 %collective-permute-start.12 = (f32[13,800]{1,0:T(8,128)S(1)}, f32[13,800]{1,0:T(8,128)S(1)}, u32[]{:S(2)}, u32[]{:S(2)}) collective-permute-start(f32[13,800]{1,0:T(8,128)S(1)} %add.257), channel_id=1, source_target_pairs={{0,32},{4,36},{8,40},{12,44},{16,48},{20,52},{24,56},{28,60},{32,0... | collective-permute-start | bytes 124808 | tf_op jit(solution)/shard_map/ppermute | solution.py:33
  133.6 8.8 %collective-permute-start.13 = (f32[13,800]{1,0:T(8,128)S(1)}, f32[13,800]{1,0:T(8,128)S(1)}, u32[]{:S(2)}, u32[]{:S(2)}) collective-permute-start(f32[13,800]{1,0:T(8,128)S(1)} %add.258), channel_id=1, source_target_pairs={{0,256},{128,384},{256,0},{384,128},{1,257},{129,385},{257,1},{385... | collective-permute-start | bytes 124808 | tf_op jit(solution)/shard_map/ppermute | solution.py:33
  142.4 6.4 %collective-permute-start.14 = (f32[13,800]{1,0:T(8,128)S(1)}, f32[13,800]{1,0:T(8,128)S(1)}, u32[]{:S(2)}, u32[]{:S(2)}) collective-permute-start(f32[13,800]{1,0:T(8,128)S(1)} %add.259), channel_id=1, source_target_pairs={{0,2},{1,3},{2,0},{3,1},{4,6},{5,7},{6,4},{7,5},{8,10},{9,11},{10,... | collective-permute-start | bytes 124808 | tf_op jit(solution)/shard_map/ppermute | solution.py:33
  148.9 5.5 %collective-permute-start.15 = (f32[26,800]{1,0:T(8,128)S(1)}, f32[26,800]{1,0:T(8,128)S(1)}, u32[]{:S(2)}, u32[]{:S(2)}) collective-permute-start(f32[26,800]{1,0:T(8,128)S(1)} %maximum_select_fusion.4), channel_id=1, source_target_pairs={{0,64},{4,68},{8,72},{12,76},{16,80},{20,84},{24,88},{28,92},{32,9... | collective-permute-start | bytes 249608 | tf_op jit(solution)/shard_map/ppermute | solution.py:33
  154.4 6.5 %collective-permute-start.16 = (f32[52,800]{1,0:T(8,128)S(1)}, f32[52,800]{1,0:T(8,128)S(1)}, u32[]{:S(2)}, u32[]{:S(2)}) collective-permute-start(f32[52,800]{1,0:T(8,128)S(1)} %maximum_select_fusion.3), channel_id=1, source_target_pairs={{0,8},{4,12},{8,0},{12,4},{16,24},{20,28},{24,16},{28,20},{32,40},... | collective-permute-start | bytes 499208 | tf_op jit(solution)/shard_map/ppermute | solution.py:33
  161.0 8.3 %collective-permute-start.17 = (f32[104,800]{1,0:T(8,128)S(1)}, f32[104,800]{1,0:T(8,128)S(1)}, u32[]{:S(2)}, u32[]{:S(2)}) collective-permute-start(f32[104,800]{1,0:T(8,128)S(1)} %maximum_select_fusion.2), channel_id=1, source_target_pairs={{0,1},{1,0},{2,3},{3,2},{4,5},{5,4},{6,7},{7,6},{8,9},{9,8},{10,11... | collective-permute-start | bytes 998408 | tf_op jit(solution)/shard_map/ppermute | solution.py:33
  169.4 16.5 %collective-permute-start.18 = (f32[208,800]{1,0:T(8,128)S(1)}, f32[208,800]{1,0:T(8,128)S(1)}, u32[]{:S(2)}, u32[]{:S(2)}) collective-permute-start(f32[208,800]{1,0:T(8,128)S(1)} %maximum_select_fusion.1), channel_id=1, source_target_pairs={{0,4},{4,0},{8,12},{12,8},{16,20},{20,16},{24,28},{28,24},{32,36},... | collective-permute-start | bytes 1996808 | tf_op jit(solution)/shard_map/ppermute | solution.py:33
  (7 other events, 25.6 us)

commit v3 on v2

--- a/solution.py
+++ b/solution.py
@@ -39,28 +39,47 @@
 
 
 REDUCE_ORDER = (
-    ("lon", 0), ("lat", 0), ("lon", 1), ("lon", 4), ("lat", 1),
-    ("lon", 2), ("ens", 0), ("lon", 3), ("ens", 1),
+    ("lon", 0), ("lat", None), ("ens", None), ("lon", 1), ("lon", 4), ("lon", 2), ("lon", 3),
 )
 
 
+def spread(array, axis):
+    count = lax.axis_size(axis)
+    copies = jnp.broadcast_to(array[None], (count,) + array.shape)
+    return lax.all_to_all(copies, axis, 0, 0, tiled=False)
+
+
 def tree_psum(flat, steps, gather_dtype):
-    halved = []
+    scattered = []
     for axis, bit in steps:
+        rows = flat.shape[0]
+        if bit is None:
+            count = lax.axis_size(axis)
+            if rows % count == 0:
+                chunks = flat.reshape((count, rows // count) + flat.shape[1:])
+                flat = lax.all_to_all(chunks, axis, 0, 0, tiled=False).sum(0)
+                scattered.append((axis, bit))
+            else:
+                flat = spread(flat, axis).sum(0)
+            continue
         if (1 << bit) >= lax.axis_size(axis):
             continue
         upper = (lax.axis_index(axis) >> bit) & 1
-        if flat.shape[0] % 2 == 0 and flat.shape[0] >= 8:
-            half = flat.shape[0] // 2
+        if rows % 2 == 0 and rows >= 8:
+            half = rows // 2
             low, high = flat[:half], flat[half:]
             keep = jnp.where(upper == 0, low, high)
             send = jnp.where(upper == 0, high, low)
             flat = keep + swapped(send, axis, bit)
-            halved.append((axis, bit))
+            scattered.append((axis, bit))
         else:
             flat = flat + swapped(flat, axis, bit)
     flat = flat.astype(gather_dtype)
-    for axis, bit in reversed(halved):
+    for axis, bit in reversed(scattered):
+        if bit is None:
+            gathered = spread(flat, axis)
+            flat = gathered.reshape((-1,) + flat.shape[1:])
+            continue
         upper = (lax.axis_index(axis) >> bit) & 1
         other = swapped(flat, axis, bit)
         flat = jnp.where(
@@ -166,11 +185,10 @@
     small_rows += -small_rows % 8
     small = jnp.pad(small, (0, small_rows * width - small.shape[0])).reshape(small_rows, width)
     packed = jnp.concatenate([grad_expand, grad_reduce.T, small], axis=0)
-    steps = [(axis, bit) for axis, bit in REDUCE_ORDER]
-    for axis in ("ens", "lon", "lat"):
-        for bit in range(lax.axis_size(axis).bit_length() - 1):
-            if (axis, bit) not in steps:
-                steps.append((axis, bit))
+    steps = list(REDUCE_ORDER)
+    for bit in range(lax.axis_size("lon").bit_length() - 1):
+        if ("lon", bit) not in steps:
+            steps.append(("lon", bit))
     packed = tree_psum(packed, steps, jnp.float32)
     grad_expand = packed[:channels]
     grad_reduce = packed[channels : 2 * channels].T

time: 190 us -> 178 us (0.937)
  blocking collectives: 0 us -> 54 us
  waiting for transfers between devices: 58.8 us -> 19.5 us
  starting transfers between devices: 81.3 us -> 52.2 us
    all_to_all x0 -> x4, blocking collectives: none -> 54 us  [the longest x2 31.6 us: tree_psum(): flat = lax.all_to_all(chunks, axis, 0, 0, tiled=False).sum(0)]
    ppermute x14 -> x6, waiting for transfers between devices: 52.4 us -> 13.2 us  [swapped(): lax.ppermute(array, axis, [(i, i ^ 1 << stride) for i in range(lax.axis_s...]
    ppermute x14 -> x6, starting transfers between devices: 58.2 us -> 29.1 us  [swapped(): lax.ppermute(array, axis, [(i, i ^ 1 << stride) for i in range(lax.axis_s...]
  transfers between devices with their start and end apart: 19 -> 11, of which waited for: 16 -> 7; matrix products, arithmetic and copies ran while one was open for 1% -> 2% of each run, Pallas kernels for 0% -> 0%
where the time goes in v3:
time: 178 us
  blocking collectives  54 us (30%)
  starting transfers between devices  52.2 us (29%)
  other arithmetic  25.5 us (14%)
  waiting for transfers between devices  19.5 us (11%)
  local copies, waits for them, and re-layouts  14.6 us (8%)
  matrix products  10.6 us (6%)
    all_to_all x2, blocking collectives, tree_psum(): flat = lax.all_to_all(chunks, axis, 0, 0, tiled=False).sum(0)  31.6 us
    ppermute x6, starting transfers between devices, swapped(): lax.ppermute(array, axis, [(i, i ^ 1 << stride) for i in range(lax.axis_s...  29.1 us
    all_to_all x2, blocking collectives, spread(): return lax.all_to_all(copies, axis, 0, 0, tiled=False)  22.5 us
    ppermute x6, waiting for transfers between devices, swapped(): lax.ppermute(array, axis, [(i, i ^ 1 << stride) for i in range(lax.axis_s...  13.2 us
    reduce_sum x4, other arithmetic, depthwise_grad(): columns.append(jnp.sum(d_conv * window, axis=(1, 2)))  11.9 us
    ppermute x2, starting transfers between devices, with_halo(): lax.ppermute(head, axis, [((i + 1) % count, i) for i in range(count)])  11 us
    reduce_sum x1, other arithmetic, cell_pass(): chan_mean = jnp.mean(conv_blk, axis=0, keepdims=True)  8.26 us
    ppermute x2, starting transfers between devices, with_halo(): lax.ppermute(tail, axis, [(i, (i + 1) % count) for i in range(count)])  6.52 us
  transfers between devices with their start and end apart: 11, of which 7 were waited for; matrix products, arithmetic and copies ran while one was open for 2% of the time, Pallas kernels for 0%

profile of v3, /device:TPU:1, one launch (start us, length us, event | category | flops | bytes accessed | tf_op | source)
XLA Modules:
  0.0 177.5 jit_solution(2000688667588051253)
XLA Ops:
  3.5 4.6 %collective-permute-start = (bf16[200,8,3]{0,2,1:T(4,128)(2,1)S(1)}, bf16[200,8,3]{0,2,1:T(4,128)(2,1)S(1)}, u32[]{:S(2)}, u32[]{:S(2)}) collective-permute-start(bf16[200,8,3]{0,2,1:T(4,128)(2,1)S(1)} %get-tuple-element.88), channel_id=1, source_target_pairs={{0,4},{4,8},{8,12},{12,16},{16,20},{20,24},{24,28},{28,32},{32,36}... | collective-permute-start | bytes 28808 | tf_op jit(solution)/shard_map/ppermute | solution.py:23
  8.1 6.1 %collective-permute-start.1 = (bf16[200,8,3]{0,2,1:T(4,128)(2,1)S(1)}, bf16[200,8,3]{0,2,1:T(4,128)(2,1)S(1)}, u32[]{:S(2)}, u32[]{:S(2)}) collective-permute-start(bf16[200,8,3]{0,2,1:T(4,128)(2,1)S(1)} %get-tuple-element.89), channel_id=1, source_target_pairs={{4,0},{8,4},{12,8},{16,12},{20,16},{24,20},{28,24},{32,28},{36,32}... | collective-permute-start | bytes 28808 | tf_op jit(solution)/shard_map/ppermute | solution.py:25
  18.1 5.6 %collective-permute-start.3 = (bf16[200,3,134]{0,2,1:T(8,128)(2,1)S(1)}, bf16[200,3,134]{0,2,1:T(8,128)(2,1)S(1)}, u32[]{:S(2)}, u32[]{:S(2)}) collective-permute-start(bf16[200,3,134]{0,2,1:T(8,128)(2,1)S(1)} %rev.3), channel_id=1, source_target_pairs={{0,124},{4,120},{8,116},{12,112},{16,108},{20,104},{24,100},{28,96... | collective-permute-start | bytes 482408 | tf_op jit(solution)/shard_map/ppermute | solution.py:38
  23.7 4.9 %collective-permute-start.4 = (bf16[200,3,134]{0,2,1:T(8,128)(2,1)S(1)}, bf16[200,3,134]{0,2,1:T(8,128)(2,1)S(1)}, u32[]{:S(2)}, u32[]{:S(2)}) collective-permute-start(bf16[200,3,134]{0,2,1:T(8,128)(2,1)S(1)} %get-tuple-element.86), channel_id=1, source_target_pairs={{1,0},{2,1},{3,2},{0,3},{5,4},{6,5},{7,6},{4,7},{9,8},{10,9},{11,1... | collective-permute-start | bytes 482408 | tf_op jit(solution)/shard_map/ppermute | solution.py:25
  28.6 5.6 %collective-permute-done.3 = bf16[200,3,134]{0,2,1:T(8,128)(2,1)S(1)} collective-permute-done((bf16[200,3,134]{0,2,1:T(8,128)(2,1)S(1)}, bf16[200,3,134]{0,2,1:T(8,128)(2,1)S(1)}, u32[]{:S(2)}, u32[]{:S(2)}) %collective-permute-start.3) | collective-permute-done | bytes 160832 | tf_op jit(solution)/shard_map/ppermute | solution.py:38
  34.5 8.3 %fusion.119 = (f32[8,128]{1,0:T(8,128)S(1)}, f32[200,8,128]{0,2,1:T(8,128)S(1)}) fusion(bf16[200,11,134]{0,2,1:T(8,128)(2,1)S(1)} %get-tuple-element.85, f32[200]{0:T(256)S(1)} %bitcast.306, f32[200]{0:T(256)S(1)} %bitcast.307, f32[200]{0:T(256)S(1)} %bitcast.260, f32[200]{0:T(256)S(1)} %bitcast.261, f32[200]{0:T(256)S(1)} %bitcast.262, ...), kind=kLoop, calls=%fused_computation.260 | loop fusion | flops 33790976 | bytes 18494496 | tf_op jit(solution)/shard_map/reduce_sum | solution.py:115
  45.3 2.2 %fusion.9 = (bf16[800,1024]{1,0:T(8,128)(2,1)}, f32[1024,800]{0,1:T(8,128)S(1)}) fusion(bf16[200,800]{1,0:T(8,128)(2,1)S(1)} %copy-done, f32[200,1024]{1,0:T(8,128)S(1)} %copy.67, f32[200]{0:T(256)S(1)} %copy-done.8, f32[1024]{0:T(1024)S(1)} %rsqrt_bitcast_fusion, f32[1024]{0:T(1024)S(1)} %get-tuple-element.141), kind=kOutput, calls=%fused_computation.12 | convolution fusion | flops 332595200 | bytes 6063392 | tf_op jit(solution)/shard_map/dot_general | solution.py:121
  55.0 3.8 %fusion.59 = (f32[200]{0:T(256)S(1)}, f32[200]{0:T(256)S(1)}, f32[200]{0:T(256)S(1)}, f32[200]{0:T(256)S(1)}, f32[200]{0:T(256)S(1)}, /*index=5*/f32[200]{0:T(25...) fusion(bf16[200,11,134]{0,2,1:T(8,128)(2,1)S(1)} %get-tuple-ele, ...), kind=kLoop, calls=%fused_computation.163 | loop fusion | flops 11055600 | bytes 8206400 | tf_op jit(solution)/shard_map/reduce_sum | solution.py:110
  58.8 3.8 %fusion.109 = (f32[200]{0:T(256)}, f32[200]{0:T(256)}, f32[200]{0:T(256)}, f32[200]{0:T(256)}, f32[200]{0:T(256)}, /*index=5*/f32[200]{0:T(256)}, f32[200]{0:T(2...) fusion(bf16[200,11,134]{0,2,1:T(8,128)(2,1)S(1)} %get-tuple-ele, ...), kind=kLoop, calls=%fused_computation.213 | loop fusion | flops 11055600 | bytes 8206400 | tf_op jit(solution)/shard_map/reduce_sum | solution.py:110
  64.8 3.0 %fusion.91 = (f32[200]{0:T(256)}, f32[200]{0:T(256)}, f32[200]{0:T(256)}, f32[200]{0:T(256)}, f32[200]{0:T(256)}, /*index=5*/f32[200]{0:T(256)}, f32[200]{0:T(25...) fusion(bf16[200,11,134]{0,2,1:T(8,128)(2,1)S(1)} %get-tuple-element.85, ...), kind=kLoop, calls=%fused_computation.195 | loop fusion | flops 11056800 | bytes 3715200 | tf_op jit(solution)/shard_map/reduce_sum | solution.py:110
  67.9 4.4 %stack.199 = f32[200,49]{0,1:T(8,128)S(1)} concatenate(f32[200,1]{0,1:T(1,128)} %bitcast.312, f32[200,1]{0,1:T(1,128)} %bitcast.313, f32[200,1]{0,1:T(1,128)} %bitcast.314, f32[200,1]{0,1:T(1,128)} %bitcast.240, f32[200,1]{0,1:T(1,128)} %bitcast.239, f32[200,1]{0,1:T(1,128)} %bitcast.238, f32[200,1]{0,1:T(1,128)} %bitcast.237, f32[200,1]{0,1:T(1,128)} %bitcast.236, ...), dimensions={1} | concatenate | bytes 78400 | tf_op jit(solution)/shard_map/stack | solution.py:111
  74.8 4.4 %collective-permute-start.5 = (f32[208,800]{1,0:T(8,128)S(1)}, f32[208,800]{1,0:T(8,128)S(1)}, u32[]{:S(2)}, u32[]{:S(2)}) collective-permute-start(f32[208,800]{1,0:T(8,128)S(1)} %fusion.110), channel_id=1, source_target_pairs={{0,4},{4,0},{8,12},{12,8},{16,20},{20,16},{24,28},{28,24},{32,36},... | collective-permute-start | bytes 1996808 | tf_op jit(solution)/shard_map/ppermute | solution.py:33
  81.0 16.4 %all_to_all.20 = f32[4,52,800]{2,1,0:T(8,128)S(1)} all-to-all(f32[4,52,800]{2,1,0:T(8,128)S(1)} %reshape.147), channel_id=1, replica_groups=mesh['ens'=4,'lon'=32,'lat'=4] {'lat'}, dimensions={0} | all-to-all | bytes 1331200 | tf_op jit(solution)/shard_map/all_to_all | solution.py:60
  97.5 15.2 %all_to_all.21 = f32[4,13,800]{2,1,0:T(8,128)S(1)} all-to-all(f32[4,13,800]{2,1,0:T(8,128)S(1)} %reshape.148), channel_id=1, replica_groups=mesh['ens'=4,'lon'=32,'lat'=4] {'ens'}, dimensions={0} | all-to-all | bytes 332800 | tf_op jit(solution)/shard_map/all_to_all | solution.py:60
  114.6 3.0 %collective-permute-done.6 = f32[13,800]{1,0:T(8,128)S(1)} collective-permute-done((f32[13,800]{1,0:T(8,128)S(1)}, f32[13,800]{1,0:T(8,128)S(1)}, u32[]{:S(2)}, u32[]{:S(2)}) %collective-permute-start.6) | collective-permute-done | bytes 41632 | tf_op jit(solution)/shard_map/ppermute | solution.py:33
  117.7 2.1 %collective-permute-start.7 = (f32[13,800]{1,0:T(8,128)S(1)}, f32[13,800]{1,0:T(8,128)S(1)}, u32[]{:S(2)}, u32[]{:S(2)}) collective-permute-start(f32[13,800]{1,0:T(8,128)S(1)} %add.240), channel_id=1, source_target_pairs={{0,64},{4,68},{8,72},{12,76},{16,80},{20,84},{24,88},{28,92},{32,9... | collective-permute-start | bytes 124808 | tf_op jit(solution)/shard_map/ppermute | solution.py:33
  119.8 2.8 %collective-permute-done.7 = f32[13,800]{1,0:T(8,128)S(1)} collective-permute-done((f32[13,800]{1,0:T(8,128)S(1)}, f32[13,800]{1,0:T(8,128)S(1)}, u32[]{:S(2)}, u32[]{:S(2)}) %collective-permute-start.7) | collective-permute-done | bytes 41632 | tf_op jit(solution)/shard_map/ppermute | solution.py:33
  122.6 2.7 %collective-permute-start.8 = (f32[13,800]{1,0:T(8,128)S(1)}, f32[13,800]{1,0:T(8,128)S(1)}, u32[]{:S(2)}, u32[]{:S(2)}) collective-permute-start(f32[13,800]{1,0:T(8,128)S(1)} %add.241), channel_id=1, source_target_pairs={{0,16},{4,20},{8,24},{12,28},{16,0},{20,4},{24,8},{28,12},{32,48},... | collective-permute-start | bytes 124808 | tf_op jit(solution)/shard_map/ppermute | solution.py:33
  125.3 3.5 %collective-permute-done.8 = f32[13,800]{1,0:T(8,128)S(1)} collective-permute-done((f32[13,800]{1,0:T(8,128)S(1)}, f32[13,800]{1,0:T(8,128)S(1)}, u32[]{:S(2)}, u32[]{:S(2)}) %collective-permute-start.8) | collective-permute-done | bytes 41632 | tf_op jit(solution)/shard_map/ppermute | solution.py:33
  128.8 6.5 %collective-permute-start.9 = (f32[13,800]{1,0:T(8,128)S(1)}, f32[13,800]{1,0:T(8,128)S(1)}, u32[]{:S(2)}, u32[]{:S(2)}) collective-permute-start(f32[13,800]{1,0:T(8,128)S(1)} %add.242), channel_id=1, source_target_pairs={{0,32},{4,36},{8,40},{12,44},{16,48},{20,52},{24,56},{28,60},{32,0... | collective-permute-start | bytes 124808 | tf_op jit(solution)/shard_map/ppermute | solution.py:33
  135.3 2.3 %collective-permute-done.9 = f32[13,800]{1,0:T(8,128)S(1)} collective-permute-done((f32[13,800]{1,0:T(8,128)S(1)}, f32[13,800]{1,0:T(8,128)S(1)}, u32[]{:S(2)}, u32[]{:S(2)}) %collective-permute-start.9) | collective-permute-done | bytes 41632 | tf_op jit(solution)/shard_map/ppermute | solution.py:33
  137.6 11.5 %all_to_all.22 = f32[4,13,800]{2,1,0:T(8,128)S(1)} all-to-all(f32[4,13,800]{2,1,0:T(8,128)S(1)} %broadcast_in_dim.9), channel_id=1, replica_groups=mesh['ens'=4,'lon'=32,'lat'=4] {'ens'}, dimensions={0} | all-to-all | bytes 332800 | tf_op jit(solution)/shard_map/all_to_all | solution.py:49
  149.3 10.9 %all_to_all.23 = f32[4,52,800]{2,1,0:T(8,128)S(1)} all-to-all(f32[4,52,800]{2,1,0:T(8,128)S(1)} %broadcast_in_dim.11), channel_id=1, replica_groups=mesh['ens'=4,'lon'=32,'lat'=4] {'lat'}, dimensions={0} | all-to-all | bytes 1331200 | tf_op jit(solution)/shard_map/all_to_all | solution.py:49
  160.3 11.4 %collective-permute-start.10 = (f32[208,800]{1,0:T(8,128)S(1)}, f32[208,800]{1,0:T(8,128)S(1)}, u32[]{:S(2)}, u32[]{:S(2)}) collective-permute-start(f32[208,800]{1,0:T(8,128)S(1)} %reshape.149), channel_id=1, source_target_pairs={{0,4},{4,0},{8,12},{12,8},{16,20},{20,16},{24,28},{28,24},{32,36},... | collective-permute-start | bytes 1996808 | tf_op jit(solution)/shard_map/ppermute | solution.py:33
  (93 shorter events, 31.5 us)
Async XLA Ops:
  0.6 44.7 %copy-start = (bf16[200,800]{1,0:T(8,128)(2,1)S(1)}, bf16[200,800]{1,0:T(8,128)(2,1)}, u32[]{:S(2)}) copy-start(bf16[200,800]{1,0:T(8,128)(2,1)} %param.11) | copy-start | bytes 960004
  0.6 13.6 %copy-start.7 = (f32[200,49]{0,1:T(8,128)S(1)}, f32[200,49]{0,1:T(8,128)}, u32[]{:S(2)}) copy-start(f32[200,49]{0,1:T(8,128)} %param.9) | copy-start | bytes 117604
  3.5 10.8 %collective-permute-start = (bf16[200,8,3]{0,2,1:T(4,128)(2,1)S(1)}, bf16[200,8,3]{0,2,1:T(4,128)(2,1)S(1)}, u32[]{:S(2)}, u32[]{:S(2)}) collective-permute-start(bf16[200,8,3]{0,2,1:T(4,128)(2,1)S(1)} %get-tuple-element.88), channel_id=1, source_target_pairs={{0,4},{4,8},{8,12},{12,16},{16,20},{20,24},{24,28},{28,32},{32,36}... | collective-permute-start | bytes 28808 | tf_op jit(solution)/shard_map/ppermute | solution.py:23
  8.1 6.9 %collective-permute-start.1 = (bf16[200,8,3]{0,2,1:T(4,128)(2,1)S(1)}, bf16[200,8,3]{0,2,1:T(4,128)(2,1)S(1)}, u32[]{:S(2)}, u32[]{:S(2)}) collective-permute-start(bf16[200,8,3]{0,2,1:T(4,128)(2,1)S(1)} %get-tuple-element.89), channel_id=1, source_target_pairs={{4,0},{8,4},{12,8},{16,12},{20,16},{24,20},{28,24},{32,28},{36,32}... | collective-permute-start | bytes 28808 | tf_op jit(solution)/shard_map/ppermute | solution.py:25
  15.2 13.4 %collective-permute-start.2 = (bf16[200,3,134]{0,2,1:T(8,128)(2,1)S(1)}, bf16[200,3,134]{0,2,1:T(8,128)(2,1)S(1)}, u32[]{:S(2)}, u32[]{:S(2)}) collective-permute-start(bf16[200,3,134]{0,2,1:T(8,128)(2,1)S(1)} %get-tuple-element.87), channel_id=1, source_target_pairs={{0,1},{1,2},{2,3},{3,0},{4,5},{5,6},{6,7},{7,4},{8,9},{9,10},{10,1... | collective-permute-start | bytes 482408 | tf_op jit(solution)/shard_map/ppermute | solution.py:23
  18.1 16.1 %collective-permute-start.3 = (bf16[200,3,134]{0,2,1:T(8,128)(2,1)S(1)}, bf16[200,3,134]{0,2,1:T(8,128)(2,1)S(1)}, u32[]{:S(2)}, u32[]{:S(2)}) collective-permute-start(bf16[200,3,134]{0,2,1:T(8,128)(2,1)S(1)} %rev.3), channel_id=1, source_target_pairs={{0,124},{4,120},{8,116},{12,112},{16,108},{20,104},{24,100},{28,96... | collective-permute-start | bytes 482408 | tf_op jit(solution)/shard_map/ppermute | solution.py:38
  23.7 10.5 %collective-permute-start.4 = (bf16[200,3,134]{0,2,1:T(8,128)(2,1)S(1)}, bf16[200,3,134]{0,2,1:T(8,128)(2,1)S(1)}, u32[]{:S(2)}, u32[]{:S(2)}) collective-permute-start(bf16[200,3,134]{0,2,1:T(8,128)(2,1)S(1)} %get-tuple-element.86), channel_id=1, source_target_pairs={{1,0},{2,1},{3,2},{0,3},{5,4},{6,5},{7,6},{4,7},{9,8},{10,9},{11,1... | collective-permute-start | bytes 482408 | tf_op jit(solution)/shard_map/ppermute | solution.py:25
  42.8 2.5 %copy-start.8 = (f32[200]{0:T(256)S(1)}, f32[200]{0:T(256)}, u32[]{:S(2)}) copy-start(f32[200]{0:T(256)} %param.10) | copy-start | bytes 2404
  45.3 2.2 %copy-start.12 = (bf16[1,200,8,128]{3,2,1,0:T(8,128)(2,1)S(1)}, bf16[1,200,8,128]{3,2,1,0:T(8,128)(2,1)}, u32[]{:S(2)}) copy-start(bf16[1,200,8,128]{3,2,1,0:T(8,128)(2,1)} %param.13) | copy-start | bytes 1228804
  45.3 2.2 %copy-start.14 = (bf16[800,200]{0,1:T(8,128)(2,1)S(1)}, bf16[800,200]{0,1:T(8,128)(2,1)}, u32[]{:S(2)}) copy-start(bf16[800,200]{0,1:T(8,128)(2,1)} %param.12) | copy-start | bytes 960004
  58.8 3.8 %copy-start.4 = (bf16[800,1024]{1,0:T(8,128)(2,1)S(1)}, bf16[800,1024]{1,0:T(8,128)(2,1)}, u32[]{:S(2)}) copy-start(bf16[800,1024]{1,0:T(8,128)(2,1)} %get-tuple-element.143) | copy-start | bytes 4915204
  58.8 3.8 %copy-start.13 = (bf16[1,200,8,128]{3,2,1,0:T(8,128)(2,1)S(1)}, bf16[1,200,8,128]{3,2,1,0:T(8,128)(2,1)}, u32[]{:S(2)}) copy-start(bf16[1,200,8,128]{3,2,1,0:T(8,128)(2,1)} %param.13) | copy-start | bytes 1228804
  64.8 3.0 %copy-start.9 = (f32[200]{0:T(256)S(1)}, f32[200]{0:T(256)}, u32[]{:S(2)}) copy-start(f32[200]{0:T(256)} %get-tuple-element.48) | copy-start | bytes 2404
  67.8 12.9 %copy-start.2 = (f32[200,800]{1,0:T(8,128)S(1)}, f32[200,800]{1,0:T(8,128)}, u32[]{:S(2)}) copy-start(f32[200,800]{1,0:T(8,128)} %convolution_multiply_fusion.1) | copy-start | bytes 1920004
  67.8 12.9 %copy-start.3 = (f32[200,800]{1,0:T(8,128)S(1)}, f32[200,800]{1,0:T(8,128)}, u32[]{:S(2)}) copy-start(f32[200,800]{1,0:T(8,128)} %convolution_multiply_fusion) | copy-start | bytes 1920004
  74.8 6.0 %collective-permute-start.5 = (f32[208,800]{1,0:T(8,128)S(1)}, f32[208,800]{1,0:T(8,128)S(1)}, u32[]{:S(2)}, u32[]{:S(2)}) collective-permute-start(f32[208,800]{1,0:T(8,128)S(1)} %fusion.110), channel_id=1, source_target_pairs={{0,4},{4,0},{8,12},{12,8},{16,20},{20,16},{24,28},{28,24},{32,36},... | collective-permute-start | bytes 1996808 | tf_op jit(solution)/shard_map/ppermute | solution.py:33
  112.7 4.9 %collective-permute-start.6 = (f32[13,800]{1,0:T(8,128)S(1)}, f32[13,800]{1,0:T(8,128)S(1)}, u32[]{:S(2)}, u32[]{:S(2)}) collective-permute-start(f32[13,800]{1,0:T(8,128)S(1)} %reduce_sum.559), channel_id=1, source_target_pairs={{0,8},{4,12},{8,0},{12,4},{16,24},{20,28},{24,16},{28,20},{32,40},... | collective-permute-start | bytes 124808 | tf_op jit(solution)/shard_map/ppermute | solution.py:33
  117.7 4.9 %collective-permute-start.7 = (f32[13,800]{1,0:T(8,128)S(1)}, f32[13,800]{1,0:T(8,128)S(1)}, u32[]{:S(2)}, u32[]{:S(2)}) collective-permute-start(f32[13,800]{1,0:T(8,128)S(1)} %add.240), channel_id=1, source_target_pairs={{0,64},{4,68},{8,72},{12,76},{16,80},{20,84},{24,88},{28,92},{32,9... | collective-permute-start | bytes 124808 | tf_op jit(solution)/shard_map/ppermute | solution.py:33
  122.6 6.2 %collective-permute-start.8 = (f32[13,800]{1,0:T(8,128)S(1)}, f32[13,800]{1,0:T(8,128)S(1)}, u32[]{:S(2)}, u32[]{:S(2)}) collective-permute-start(f32[13,800]{1,0:T(8,128)S(1)} %add.241), channel_id=1, source_target_pairs={{0,16},{4,20},{8,24},{12,28},{16,0},{20,4},{24,8},{28,12},{32,48},... | collective-permute-start | bytes 124808 | tf_op jit(solution)/shard_map/ppermute | solution.py:33
  128.8 8.8 %collective-permute-start.9 = (f32[13,800]{1,0:T(8,128)S(1)}, f32[13,800]{1,0:T(8,128)S(1)}, u32[]{:S(2)}, u32[]{:S(2)}) collective-permute-start(f32[13,800]{1,0:T(8,128)S(1)} %add.242), channel_id=1, source_target_pairs={{0,32},{4,36},{8,40},{12,44},{16,48},{20,52},{24,56},{28,60},{32,0... | collective-permute-start | bytes 124808 | tf_op jit(solution)/shard_map/ppermute | solution.py:33
  149.2 22.5 %copy-start.6 = (bf16[1,200,8,128]{3,2,1,0:T(8,128)(2,1)S(1)}, bf16[1,200,8,128]{3,2,1,0:T(8,128)(2,1)}, u32[]{:S(2)}) copy-start(bf16[1,200,8,128]{3,2,1,0:T(8,128)(2,1)} %param.7) | copy-start | bytes 1228804
  149.2 22.5 %copy-start.10 = (f32[1024]{0:T(1024)S(1)}, f32[1024]{0:T(1024)}, u32[]{:S(2)}) copy-start(f32[1024]{0:T(1024)} %get-tuple-element.139) | copy-start | bytes 12292
  149.3 22.5 %copy-start.15 = (bf16[800,200]{0,1:T(8,128)(2,1)S(1)}, bf16[800,200]{0,1:T(8,128)(2,1)}, u32[]{:S(2)}) copy-start(bf16[800,200]{0,1:T(8,128)(2,1)} %param.12) | copy-start | bytes 960004
  160.3 14.3 %collective-permute-start.10 = (f32[208,800]{1,0:T(8,128)S(1)}, f32[208,800]{1,0:T(8,128)S(1)}, u32[]{:S(2)}, u32[]{:S(2)}) collective-permute-start(f32[208,800]{1,0:T(8,128)S(1)} %reshape.149), channel_id=1, source_target_pairs={{0,4},{4,0},{8,12},{12,8},{16,20},{20,16},{24,28},{28,24},{32,36},... | collective-permute-start | bytes 1996808 | tf_op jit(solution)/shard_map/ppermute | solution.py:33
  (3 other events, 4.0 us)

commit v4 on v3

--- a/solution.py
+++ b/solution.py
@@ -108,7 +108,7 @@
                 jnp.float32
             )
             columns.append(jnp.sum(d_conv * window, axis=(1, 2)))
-    return jnp.stack(columns, axis=1)
+    return jnp.stack(columns, axis=0)
 
 
 def cell_pass(conv_blk, state_blk, cot_blk, mask_blk, norm_gain, expand_weight, reduce_weight):
@@ -180,7 +180,7 @@
     grad_gain = grad_gain * grad_scale
     grad_depthwise = grad_depthwise * grad_scale
     width = grad_expand.shape[1]
-    small = jnp.concatenate([grad_depthwise, grad_gain[:, None]], axis=1).reshape(-1)
+    small = jnp.concatenate([grad_depthwise, grad_gain[None]], axis=0).reshape(-1)
     small_rows = -(-small.shape[0] // width)
     small_rows += -small_rows % 8
     small = jnp.pad(small, (0, small_rows * width - small.shape[0])).reshape(small_rows, width)
@@ -192,9 +192,9 @@
     packed = tree_psum(packed, steps, jnp.float32)
     grad_expand = packed[:channels]
     grad_reduce = packed[channels : 2 * channels].T
-    small = packed[2 * channels :].reshape(-1)[: channels * (KS * KS + 1)].reshape(channels, -1)
-    grad_depthwise = small[:, : KS * KS]
-    grad_gain = small[:, KS * KS]
+    small = packed[2 * channels :].reshape(-1)[: channels * (KS * KS + 1)].reshape(-1, channels)
+    grad_depthwise = small[: KS * KS].T
+    grad_gain = small[KS * KS]
     next_state = out_flat.reshape(channels, tile_rows, tile_cols)[None]
     return (next_state, grad_depthwise, grad_gain, grad_expand, grad_reduce)
 

time: 178 us -> 178 us (level)
  no operation moved by 1% of the time
where the time goes in v4:
time: 178 us; the launch traced here: 177 us
  blocking collectives  54 us (30%)
  starting transfers between devices  52.2 us (29%)
  other arithmetic  25.5 us (14%)
  waiting for transfers between devices  19.5 us (11%)
  local copies, waits for them, and re-layouts  14.3 us (8%)
  matrix products  10.6 us (6%)
    all_to_all x2, blocking collectives, tree_psum(): flat = lax.all_to_all(chunks, axis, 0, 0, tiled=False).sum(0)  31.6 us
    ppermute x6, starting transfers between devices, swapped(): lax.ppermute(array, axis, [(i, i ^ 1 << stride) for i in range(lax.axis_s...  29.1 us
    all_to_all x2, blocking collectives, spread(): return lax.all_to_all(copies, axis, 0, 0, tiled=False)  22.5 us
    ppermute x6, waiting for transfers between devices, swapped(): lax.ppermute(array, axis, [(i, i ^ 1 << stride) for i in range(lax.axis_s...  13.2 us
    reduce_sum x4, other arithmetic, depthwise_grad(): columns.append(jnp.sum(d_conv * window, axis=(1, 2)))  11.9 us
    ppermute x2, starting transfers between devices, with_halo(): lax.ppermute(head, axis, [((i + 1) % count, i) for i in range(count)])  11 us
    reduce_sum x1, other arithmetic, cell_pass(): chan_mean = jnp.mean(conv_blk, axis=0, keepdims=True)  8.26 us
    ppermute x2, starting transfers between devices, with_halo(): lax.ppermute(tail, axis, [(i, (i + 1) % count) for i in range(count)])  6.52 us
  transfers between devices with their start and end apart: 11, of which 7 were waited for; matrix products, arithmetic and copies ran while one was open for 2% of the time, Pallas kernels for 0%

profile of v4, /device:TPU:1, one launch (start us, length us, event | category | flops | bytes accessed | tf_op | source)
XLA Modules:
  0.0 177.2 jit_solution(2219659084166925131)
XLA Ops:
  3.5 4.6 %collective-permute-start = (bf16[200,8,3]{0,2,1:T(4,128)(2,1)S(1)}, bf16[200,8,3]{0,2,1:T(4,128)(2,1)S(1)}, u32[]{:S(2)}, u32[]{:S(2)}) collective-permute-start(bf16[200,8,3]{0,2,1:T(4,128)(2,1)S(1)} %get-tuple-element.78), channel_id=1, source_target_pairs={{0,4},{4,8},{8,12},{12,16},{16,20},{20,24},{24,28},{28,32},{32,36}... | collective-permute-start | bytes 28808 | tf_op jit(solution)/shard_map/ppermute | solution.py:23
  8.1 6.1 %collective-permute-start.1 = (bf16[200,8,3]{0,2,1:T(4,128)(2,1)S(1)}, bf16[200,8,3]{0,2,1:T(4,128)(2,1)S(1)}, u32[]{:S(2)}, u32[]{:S(2)}) collective-permute-start(bf16[200,8,3]{0,2,1:T(4,128)(2,1)S(1)} %get-tuple-element.79), channel_id=1, source_target_pairs={{4,0},{8,4},{12,8},{16,12},{20,16},{24,20},{28,24},{32,28},{36,32}... | collective-permute-start | bytes 28808 | tf_op jit(solution)/shard_map/ppermute | solution.py:25
  18.1 5.6 %collective-permute-start.3 = (bf16[200,3,134]{0,2,1:T(8,128)(2,1)S(1)}, bf16[200,3,134]{0,2,1:T(8,128)(2,1)S(1)}, u32[]{:S(2)}, u32[]{:S(2)}) collective-permute-start(bf16[200,3,134]{0,2,1:T(8,128)(2,1)S(1)} %rev.3), channel_id=1, source_target_pairs={{0,124},{4,120},{8,116},{12,112},{16,108},{20,104},{24,100},{28,96... | collective-permute-start | bytes 482408 | tf_op jit(solution)/shard_map/ppermute | solution.py:38
  23.7 4.9 %collective-permute-start.4 = (bf16[200,3,134]{0,2,1:T(8,128)(2,1)S(1)}, bf16[200,3,134]{0,2,1:T(8,128)(2,1)S(1)}, u32[]{:S(2)}, u32[]{:S(2)}) collective-permute-start(bf16[200,3,134]{0,2,1:T(8,128)(2,1)S(1)} %get-tuple-element.76), channel_id=1, source_target_pairs={{1,0},{2,1},{3,2},{0,3},{5,4},{6,5},{7,6},{4,7},{9,8},{10,9},{11,1... | collective-permute-start | bytes 482408 | tf_op jit(solution)/shard_map/ppermute | solution.py:25
  28.6 5.6 %collective-permute-done.3 = bf16[200,3,134]{0,2,1:T(8,128)(2,1)S(1)} collective-permute-done((bf16[200,3,134]{0,2,1:T(8,128)(2,1)S(1)}, bf16[200,3,134]{0,2,1:T(8,128)(2,1)S(1)}, u32[]{:S(2)}, u32[]{:S(2)}) %collective-permute-start.3) | collective-permute-done | bytes 160832 | tf_op jit(solution)/shard_map/ppermute | solution.py:38
  34.5 8.3 %fusion.119 = (f32[8,128]{1,0:T(8,128)S(1)}, f32[200,8,128]{0,2,1:T(8,128)S(1)}) fusion(bf16[200,11,134]{0,2,1:T(8,128)(2,1)S(1)} %get-tuple-element.75, f32[200]{0:T(256)S(1)} %bitcast.308, f32[200]{0:T(256)S(1)} %bitcast.309, f32[200]{0:T(256)S(1)} %bitcast.262, f32[200]{0:T(256)S(1)} %bitcast.263, f32[200]{0:T(256)S(1)} %bitcast.264, ...), kind=kLoop, calls=%fused_computation.260 | loop fusion | flops 33790976 | bytes 18494496 | tf_op jit(solution)/shard_map/reduce_sum | solution.py:115
  45.3 2.2 %fusion.9 = (bf16[800,1024]{1,0:T(8,128)(2,1)}, f32[1024,800]{0,1:T(8,128)S(1)}) fusion(bf16[200,800]{1,0:T(8,128)(2,1)S(1)} %copy-done, f32[200,1024]{1,0:T(8,128)S(1)} %copy.62, f32[200]{0:T(256)S(1)} %copy-done.8, f32[1024]{0:T(1024)S(1)} %rsqrt_bitcast_fusion, f32[1024]{0:T(1024)S(1)} %get-tuple-element.131), kind=kOutput, calls=%fused_computation.12 | convolution fusion | flops 332595200 | bytes 6063392 | tf_op jit(solution)/shard_map/dot_general | solution.py:121
  55.0 3.8 %fusion.59 = (f32[200]{0:T(256)S(1)}, f32[200]{0:T(256)S(1)}, f32[200]{0:T(256)S(1)}, f32[200]{0:T(256)S(1)}, f32[200]{0:T(256)S(1)}, /*index=5*/f32[200]{0:T(25...) fusion(bf16[200,11,134]{0,2,1:T(8,128)(2,1)S(1)} %get-tuple-ele, ...), kind=kLoop, calls=%fused_computation.163 | loop fusion | flops 11055600 | bytes 8206400 | tf_op jit(solution)/shard_map/reduce_sum | solution.py:110
  58.8 3.8 %fusion.109 = (f32[200]{0:T(256)}, f32[200]{0:T(256)}, f32[200]{0:T(256)}, f32[200]{0:T(256)}, f32[200]{0:T(256)}, /*index=5*/f32[200]{0:T(256)}, f32[200]{0:T(2...) fusion(bf16[200,11,134]{0,2,1:T(8,128)(2,1)S(1)} %get-tuple-ele, ...), kind=kLoop, calls=%fused_computation.213 | loop fusion | flops 11055600 | bytes 8206400 | tf_op jit(solution)/shard_map/reduce_sum | solution.py:110
  64.8 3.0 %fusion.91 = (f32[200]{0:T(256)}, f32[200]{0:T(256)}, f32[200]{0:T(256)}, f32[200]{0:T(256)}, f32[200]{0:T(256)}, /*index=5*/f32[200]{0:T(256)}, f32[200]{0:T(25...) fusion(bf16[200,11,134]{0,2,1:T(8,128)(2,1)S(1)} %get-tuple-element.75, ...), kind=kLoop, calls=%fused_computation.195 | loop fusion | flops 11056800 | bytes 3715200 | tf_op jit(solution)/shard_map/reduce_sum | solution.py:110
  67.9 4.4 %stack.199 = f32[49,200]{1,0:T(8,128)S(1)} concatenate(f32[1,200]{1,0:T(1,128)} %bitcast.314, f32[1,200]{1,0:T(1,128)} %bitcast.315, f32[1,200]{1,0:T(1,128)} %bitcast.316, f32[1,200]{1,0:T(1,128)} %bitcast.242, f32[1,200]{1,0:T(1,128)} %bitcast.241, f32[1,200]{1,0:T(1,128)} %bitcast.240, f32[1,200]{1,0:T(1,128)} %bitcast.239, f32[1,200]{1,0:T(1,128)} %bitcast.238, ...), dimensions={0} | concatenate | bytes 78400 | tf_op jit(solution)/shard_map/stack | solution.py:111
  74.6 4.4 %collective-permute-start.5 = (f32[208,800]{1,0:T(8,128)S(1)}, f32[208,800]{1,0:T(8,128)S(1)}, u32[]{:S(2)}, u32[]{:S(2)}) collective-permute-start(f32[208,800]{1,0:T(8,128)S(1)} %fusion.110), channel_id=1, source_target_pairs={{0,4},{4,0},{8,12},{12,8},{16,20},{20,16},{24,28},{28,24},{32,36},... | collective-permute-start | bytes 1996808 | tf_op jit(solution)/shard_map/ppermute | solution.py:33
  80.9 16.4 %all_to_all.20 = f32[4,52,800]{2,1,0:T(8,128)S(1)} all-to-all(f32[4,52,800]{2,1,0:T(8,128)S(1)} %reshape.153), channel_id=1, replica_groups=mesh['ens'=4,'lon'=32,'lat'=4] {'lat'}, dimensions={0} | all-to-all | bytes 1331200 | tf_op jit(solution)/shard_map/all_to_all | solution.py:60
  97.4 15.2 %all_to_all.21 = f32[4,13,800]{2,1,0:T(8,128)S(1)} all-to-all(f32[4,13,800]{2,1,0:T(8,128)S(1)} %reshape.154), channel_id=1, replica_groups=mesh['ens'=4,'lon'=32,'lat'=4] {'ens'}, dimensions={0} | all-to-all | bytes 332800 | tf_op jit(solution)/shard_map/all_to_all | solution.py:60
  114.5 3.0 %collective-permute-done.6 = f32[13,800]{1,0:T(8,128)S(1)} collective-permute-done((f32[13,800]{1,0:T(8,128)S(1)}, f32[13,800]{1,0:T(8,128)S(1)}, u32[]{:S(2)}, u32[]{:S(2)}) %collective-permute-start.6) | collective-permute-done | bytes 41632 | tf_op jit(solution)/shard_map/ppermute | solution.py:33
  117.5 2.1 %collective-permute-start.7 = (f32[13,800]{1,0:T(8,128)S(1)}, f32[13,800]{1,0:T(8,128)S(1)}, u32[]{:S(2)}, u32[]{:S(2)}) collective-permute-start(f32[13,800]{1,0:T(8,128)S(1)} %add.240), channel_id=1, source_target_pairs={{0,64},{4,68},{8,72},{12,76},{16,80},{20,84},{24,88},{28,92},{32,9... | collective-permute-start | bytes 124808 | tf_op jit(solution)/shard_map/ppermute | solution.py:33
  119.7 2.8 %collective-permute-done.7 = f32[13,800]{1,0:T(8,128)S(1)} collective-permute-done((f32[13,800]{1,0:T(8,128)S(1)}, f32[13,800]{1,0:T(8,128)S(1)}, u32[]{:S(2)}, u32[]{:S(2)}) %collective-permute-start.7) | collective-permute-done | bytes 41632 | tf_op jit(solution)/shard_map/ppermute | solution.py:33
  122.4 2.7 %collective-permute-start.8 = (f32[13,800]{1,0:T(8,128)S(1)}, f32[13,800]{1,0:T(8,128)S(1)}, u32[]{:S(2)}, u32[]{:S(2)}) collective-permute-start(f32[13,800]{1,0:T(8,128)S(1)} %add.241), channel_id=1, source_target_pairs={{0,16},{4,20},{8,24},{12,28},{16,0},{20,4},{24,8},{28,12},{32,48},... | collective-permute-start | bytes 124808 | tf_op jit(solution)/shard_map/ppermute | solution.py:33
  125.2 3.5 %collective-permute-done.8 = f32[13,800]{1,0:T(8,128)S(1)} collective-permute-done((f32[13,800]{1,0:T(8,128)S(1)}, f32[13,800]{1,0:T(8,128)S(1)}, u32[]{:S(2)}, u32[]{:S(2)}) %collective-permute-start.8) | collective-permute-done | bytes 41632 | tf_op jit(solution)/shard_map/ppermute | solution.py:33
  128.6 6.5 %collective-permute-start.9 = (f32[13,800]{1,0:T(8,128)S(1)}, f32[13,800]{1,0:T(8,128)S(1)}, u32[]{:S(2)}, u32[]{:S(2)}) collective-permute-start(f32[13,800]{1,0:T(8,128)S(1)} %add.242), channel_id=1, source_target_pairs={{0,32},{4,36},{8,40},{12,44},{16,48},{20,52},{24,56},{28,60},{32,0... | collective-permute-start | bytes 124808 | tf_op jit(solution)/shard_map/ppermute | solution.py:33
  135.2 2.3 %collective-permute-done.9 = f32[13,800]{1,0:T(8,128)S(1)} collective-permute-done((f32[13,800]{1,0:T(8,128)S(1)}, f32[13,800]{1,0:T(8,128)S(1)}, u32[]{:S(2)}, u32[]{:S(2)}) %collective-permute-start.9) | collective-permute-done | bytes 41632 | tf_op jit(solution)/shard_map/ppermute | solution.py:33
  137.5 11.5 %all_to_all.22 = f32[4,13,800]{2,1,0:T(8,128)S(1)} all-to-all(f32[4,13,800]{2,1,0:T(8,128)S(1)} %broadcast_in_dim.9), channel_id=1, replica_groups=mesh['ens'=4,'lon'=32,'lat'=4] {'ens'}, dimensions={0} | all-to-all | bytes 332800 | tf_op jit(solution)/shard_map/all_to_all | solution.py:49
  149.1 10.9 %all_to_all.23 = f32[4,52,800]{2,1,0:T(8,128)S(1)} all-to-all(f32[4,52,800]{2,1,0:T(8,128)S(1)} %broadcast_in_dim.11), channel_id=1, replica_groups=mesh['ens'=4,'lon'=32,'lat'=4] {'lat'}, dimensions={0} | all-to-all | bytes 1331200 | tf_op jit(solution)/shard_map/all_to_all | solution.py:49
  160.1 11.4 %collective-permute-start.10 = (f32[208,800]{1,0:T(8,128)S(1)}, f32[208,800]{1,0:T(8,128)S(1)}, u32[]{:S(2)}, u32[]{:S(2)}) collective-permute-start(f32[208,800]{1,0:T(8,128)S(1)} %reshape.155), channel_id=1, source_target_pairs={{0,4},{4,0},{8,12},{12,8},{16,20},{20,16},{24,28},{28,24},{32,36},... | collective-permute-start | bytes 1996808 | tf_op jit(solution)/shard_map/ppermute | solution.py:33
  (92 shorter events, 31.2 us)
Async XLA Ops:
  0.6 44.7 %copy-start = (bf16[200,800]{1,0:T(8,128)(2,1)S(1)}, bf16[200,800]{1,0:T(8,128)(2,1)}, u32[]{:S(2)}) copy-start(bf16[200,800]{1,0:T(8,128)(2,1)} %param.11) | copy-start | bytes 960004
  0.6 13.6 %copy-start.7 = (f32[200,49]{0,1:T(8,128)S(1)}, f32[200,49]{0,1:T(8,128)}, u32[]{:S(2)}) copy-start(f32[200,49]{0,1:T(8,128)} %param.9) | copy-start | bytes 117604
  3.5 10.8 %collective-permute-start = (bf16[200,8,3]{0,2,1:T(4,128)(2,1)S(1)}, bf16[200,8,3]{0,2,1:T(4,128)(2,1)S(1)}, u32[]{:S(2)}, u32[]{:S(2)}) collective-permute-start(bf16[200,8,3]{0,2,1:T(4,128)(2,1)S(1)} %get-tuple-element.78), channel_id=1, source_target_pairs={{0,4},{4,8},{8,12},{12,16},{16,20},{20,24},{24,28},{28,32},{32,36}... | collective-permute-start | bytes 28808 | tf_op jit(solution)/shard_map/ppermute | solution.py:23
  8.1 6.9 %collective-permute-start.1 = (bf16[200,8,3]{0,2,1:T(4,128)(2,1)S(1)}, bf16[200,8,3]{0,2,1:T(4,128)(2,1)S(1)}, u32[]{:S(2)}, u32[]{:S(2)}) collective-permute-start(bf16[200,8,3]{0,2,1:T(4,128)(2,1)S(1)} %get-tuple-element.79), channel_id=1, source_target_pairs={{4,0},{8,4},{12,8},{16,12},{20,16},{24,20},{28,24},{32,28},{36,32}... | collective-permute-start | bytes 28808 | tf_op jit(solution)/shard_map/ppermute | solution.py:25
  15.2 13.4 %collective-permute-start.2 = (bf16[200,3,134]{0,2,1:T(8,128)(2,1)S(1)}, bf16[200,3,134]{0,2,1:T(8,128)(2,1)S(1)}, u32[]{:S(2)}, u32[]{:S(2)}) collective-permute-start(bf16[200,3,134]{0,2,1:T(8,128)(2,1)S(1)} %get-tuple-element.77), channel_id=1, source_target_pairs={{0,1},{1,2},{2,3},{3,0},{4,5},{5,6},{6,7},{7,4},{8,9},{9,10},{10,1... | collective-permute-start | bytes 482408 | tf_op jit(solution)/shard_map/ppermute | solution.py:23
  18.1 16.1 %collective-permute-start.3 = (bf16[200,3,134]{0,2,1:T(8,128)(2,1)S(1)}, bf16[200,3,134]{0,2,1:T(8,128)(2,1)S(1)}, u32[]{:S(2)}, u32[]{:S(2)}) collective-permute-start(bf16[200,3,134]{0,2,1:T(8,128)(2,1)S(1)} %rev.3), channel_id=1, source_target_pairs={{0,124},{4,120},{8,116},{12,112},{16,108},{20,104},{24,100},{28,96... | collective-permute-start | bytes 482408 | tf_op jit(solution)/shard_map/ppermute | solution.py:38
  23.7 10.5 %collective-permute-start.4 = (bf16[200,3,134]{0,2,1:T(8,128)(2,1)S(1)}, bf16[200,3,134]{0,2,1:T(8,128)(2,1)S(1)}, u32[]{:S(2)}, u32[]{:S(2)}) collective-permute-start(bf16[200,3,134]{0,2,1:T(8,128)(2,1)S(1)} %get-tuple-element.76), channel_id=1, source_target_pairs={{1,0},{2,1},{3,2},{0,3},{5,4},{6,5},{7,6},{4,7},{9,8},{10,9},{11,1... | collective-permute-start | bytes 482408 | tf_op jit(solution)/shard_map/ppermute | solution.py:25
  42.8 2.5 %copy-start.8 = (f32[200]{0:T(256)S(1)}, f32[200]{0:T(256)}, u32[]{:S(2)}) copy-start(f32[200]{0:T(256)} %param.10) | copy-start | bytes 2404
  45.3 2.2 %copy-start.12 = (bf16[1,200,8,128]{3,2,1,0:T(8,128)(2,1)S(1)}, bf16[1,200,8,128]{3,2,1,0:T(8,128)(2,1)}, u32[]{:S(2)}) copy-start(bf16[1,200,8,128]{3,2,1,0:T(8,128)(2,1)} %param.13) | copy-start | bytes 1228804
  45.3 2.2 %copy-start.14 = (bf16[800,200]{0,1:T(8,128)(2,1)S(1)}, bf16[800,200]{0,1:T(8,128)(2,1)}, u32[]{:S(2)}) copy-start(bf16[800,200]{0,1:T(8,128)(2,1)} %param.12) | copy-start | bytes 960004
  58.8 3.8 %copy-start.4 = (bf16[800,1024]{1,0:T(8,128)(2,1)S(1)}, bf16[800,1024]{1,0:T(8,128)(2,1)}, u32[]{:S(2)}) copy-start(bf16[800,1024]{1,0:T(8,128)(2,1)} %get-tuple-element.133) | copy-start | bytes 4915204
  58.8 3.8 %copy-start.13 = (bf16[1,200,8,128]{3,2,1,0:T(8,128)(2,1)S(1)}, bf16[1,200,8,128]{3,2,1,0:T(8,128)(2,1)}, u32[]{:S(2)}) copy-start(bf16[1,200,8,128]{3,2,1,0:T(8,128)(2,1)} %param.13) | copy-start | bytes 1228804
  64.8 3.0 %copy-start.9 = (f32[200]{0:T(256)S(1)}, f32[200]{0:T(256)}, u32[]{:S(2)}) copy-start(f32[200]{0:T(256)} %get-tuple-element.38) | copy-start | bytes 2404
  67.8 12.8 %copy-start.2 = (f32[200,800]{1,0:T(8,128)S(1)}, f32[200,800]{1,0:T(8,128)}, u32[]{:S(2)}) copy-start(f32[200,800]{1,0:T(8,128)} %convolution_multiply_fusion.1) | copy-start | bytes 1920004
  67.8 12.8 %copy-start.3 = (f32[200,800]{1,0:T(8,128)S(1)}, f32[200,800]{1,0:T(8,128)}, u32[]{:S(2)}) copy-start(f32[200,800]{1,0:T(8,128)} %convolution_multiply_fusion) | copy-start | bytes 1920004
  74.6 6.0 %collective-permute-start.5 = (f32[208,800]{1,0:T(8,128)S(1)}, f32[208,800]{1,0:T(8,128)S(1)}, u32[]{:S(2)}, u32[]{:S(2)}) collective-permute-start(f32[208,800]{1,0:T(8,128)S(1)} %fusion.110), channel_id=1, source_target_pairs={{0,4},{4,0},{8,12},{12,8},{16,20},{20,16},{24,28},{28,24},{32,36},... | collective-permute-start | bytes 1996808 | tf_op jit(solution)/shard_map/ppermute | solution.py:33
  112.6 4.9 %collective-permute-start.6 = (f32[13,800]{1,0:T(8,128)S(1)}, f32[13,800]{1,0:T(8,128)S(1)}, u32[]{:S(2)}, u32[]{:S(2)}) collective-permute-start(f32[13,800]{1,0:T(8,128)S(1)} %reduce_sum.559), channel_id=1, source_target_pairs={{0,8},{4,12},{8,0},{12,4},{16,24},{20,28},{24,16},{28,20},{32,40},... | collective-permute-start | bytes 124808 | tf_op jit(solution)/shard_map/ppermute | solution.py:33
  117.5 4.9 %collective-permute-start.7 = (f32[13,800]{1,0:T(8,128)S(1)}, f32[13,800]{1,0:T(8,128)S(1)}, u32[]{:S(2)}, u32[]{:S(2)}) collective-permute-start(f32[13,800]{1,0:T(8,128)S(1)} %add.240), channel_id=1, source_target_pairs={{0,64},{4,68},{8,72},{12,76},{16,80},{20,84},{24,88},{28,92},{32,9... | collective-permute-start | bytes 124808 | tf_op jit(solution)/shard_map/ppermute | solution.py:33
  122.4 6.2 %collective-permute-start.8 = (f32[13,800]{1,0:T(8,128)S(1)}, f32[13,800]{1,0:T(8,128)S(1)}, u32[]{:S(2)}, u32[]{:S(2)}) collective-permute-start(f32[13,800]{1,0:T(8,128)S(1)} %add.241), channel_id=1, source_target_pairs={{0,16},{4,20},{8,24},{12,28},{16,0},{20,4},{24,8},{28,12},{32,48},... | collective-permute-start | bytes 124808 | tf_op jit(solution)/shard_map/ppermute | solution.py:33
  128.6 8.8 %collective-permute-start.9 = (f32[13,800]{1,0:T(8,128)S(1)}, f32[13,800]{1,0:T(8,128)S(1)}, u32[]{:S(2)}, u32[]{:S(2)}) collective-permute-start(f32[13,800]{1,0:T(8,128)S(1)} %add.242), channel_id=1, source_target_pairs={{0,32},{4,36},{8,40},{12,44},{16,48},{20,52},{24,56},{28,60},{32,0... | collective-permute-start | bytes 124808 | tf_op jit(solution)/shard_map/ppermute | solution.py:33
  149.1 22.5 %copy-start.6 = (bf16[1,200,8,128]{3,2,1,0:T(8,128)(2,1)S(1)}, bf16[1,200,8,128]{3,2,1,0:T(8,128)(2,1)}, u32[]{:S(2)}) copy-start(bf16[1,200,8,128]{3,2,1,0:T(8,128)(2,1)} %param.7) | copy-start | bytes 1228804
  149.1 22.5 %copy-start.10 = (f32[1024]{0:T(1024)S(1)}, f32[1024]{0:T(1024)}, u32[]{:S(2)}) copy-start(f32[1024]{0:T(1024)} %get-tuple-element.129) | copy-start | bytes 12292
  149.1 22.5 %copy-start.15 = (bf16[800,200]{0,1:T(8,128)(2,1)S(1)}, bf16[800,200]{0,1:T(8,128)(2,1)}, u32[]{:S(2)}) copy-start(bf16[800,200]{0,1:T(8,128)(2,1)} %param.12) | copy-start | bytes 960004
  160.1 14.3 %collective-permute-start.10 = (f32[208,800]{1,0:T(8,128)S(1)}, f32[208,800]{1,0:T(8,128)S(1)}, u32[]{:S(2)}, u32[]{:S(2)}) collective-permute-start(f32[208,800]{1,0:T(8,128)S(1)} %reshape.155), channel_id=1, source_target_pairs={{0,4},{4,0},{8,12},{12,8},{16,20},{20,16},{24,28},{28,24},{32,36},... | collective-permute-start | bytes 1996808 | tf_op jit(solution)/shard_map/ppermute | solution.py:33
  (3 other events, 4.0 us)

commit v5 on v4

--- a/solution.py
+++ b/solution.py
@@ -3,7 +3,7 @@
 import jax
 import jax.numpy as jnp
 from jax import lax
-from jax.sharding import PartitionSpec as P
+from jax.sharding import Mesh, PartitionSpec as P
 
 KS = 7
 
@@ -38,9 +38,8 @@
     return lax.ppermute(array, axis, [(i, count - 1 - i) for i in range(count)])
 
 
-REDUCE_ORDER = (
-    ("lon", 0), ("lat", None), ("ens", None), ("lon", 1), ("lon", 4), ("lon", 2), ("lon", 3),
-)
+LON = ("lon_z", "lon_y", "lon_c")
+REDUCE_ORDER = (("lon_c", 0), ("lat", None), ("ens", None), ("lon_y", None), ("lon_z", 0))
 
 
 def spread(array, axis):
@@ -148,12 +147,12 @@
     margin = KS // 2
     mask_bf = ocean_mask.astype(jnp.bfloat16)
     masked = state_tile * mask_bf[None]
-    padded = with_halo(masked, (("lon", 2), ("lat", 1)), margin)
+    padded = with_halo(masked, ((LON, 2), ("lat", 1)), margin)
     lat_now = lax.axis_index("lat")
     lat_count = lax.axis_size("lat")
-    lon_count = lax.axis_size("lon")
+    lon_count = lax.axis_size(LON)
     top_strip = padded[:, tile_rows : tile_rows + margin, :][:, ::-1, ::-1]
-    mirrored = mirrored_across(top_strip, "lon")
+    mirrored = mirrored_across(top_strip, LON)
     north_rows = jnp.where(lat_now == lat_count - 1, mirrored, padded[:, tile_rows + margin :, :])
     south_rows = jnp.where(lat_now == 0, jnp.zeros_like(top_strip), padded[:, :margin, :])
     padded = jnp.concatenate(
@@ -185,11 +184,7 @@
     small_rows += -small_rows % 8
     small = jnp.pad(small, (0, small_rows * width - small.shape[0])).reshape(small_rows, width)
     packed = jnp.concatenate([grad_expand, grad_reduce.T, small], axis=0)
-    steps = list(REDUCE_ORDER)
-    for bit in range(lax.axis_size("lon").bit_length() - 1):
-        if ("lon", bit) not in steps:
-            steps.append(("lon", bit))
-    packed = tree_psum(packed, steps, jnp.float32)
+    packed = tree_psum(packed, REDUCE_ORDER, jnp.float32)
     grad_expand = packed[:channels]
     grad_reduce = packed[channels : 2 * channels].T
     small = packed[2 * channels :].reshape(-1)[: channels * (KS * KS + 1)].reshape(-1, channels)
@@ -200,18 +195,20 @@
 
 
 def solution(mesh):
+    ens, lon, lat = (mesh.shape[name] for name in ("ens", "lon", "lat"))
+    fine = Mesh(mesh.devices.reshape(ens, 2, lon // 4, 2, lat), ("ens",) + LON + ("lat",))
     return jax.shard_map(
         body,
-        mesh=mesh,
+        mesh=fine,
         in_specs=(
-            P("ens", None, "lat", "lon"),
-            P("lat", "lon"),
-            P(),
-            P(),
-            P(),
-            P(),
-            P("ens", None, "lat", "lon"),
+            P("ens", None, "lat", LON),
+            P("lat", LON),
+            P(),
+            P(),
+            P(),
+            P(),
+            P("ens", None, "lat", LON),
         ),
-        out_specs=(P("ens", None, "lat", "lon"), P(), P(), P(), P()),
+        out_specs=(P("ens", None, "lat", LON), P(), P(), P(), P()),
         check_vma=False,
     )

time: 178 us -> 175 us (0.983)
  blocking collectives: 54 us -> 73.1 us
  starting transfers between devices: 52.2 us -> 38.8 us
  waiting for transfers between devices: 19.5 us -> 11 us
    all_to_all x2 -> x3, blocking collectives: 22.5 us -> 41.5 us  [spread(): return lax.all_to_all(copies, axis, 0, 0, tiled=False)]
    ppermute x6 -> x3, starting transfers between devices: 29.1 us -> 15.8 us  [swapped(): lax.ppermute(array, axis, [(i, i ^ 1 << stride) for i in range(lax.axis_s...]
    ppermute x6 -> x3, waiting for transfers between devices: 13.2 us -> 4.65 us  [swapped(): lax.ppermute(array, axis, [(i, i ^ 1 << stride) for i in range(lax.axis_s...]
  transfers between devices with their start and end apart: 11 -> 8, of which waited for: 7 -> 4; matrix products, arithmetic and copies ran while one was open for 2% -> 2% of each run, Pallas kernels for 0% -> 0%
where the time goes in v5:
time: 175 us; the launch traced here: 174 us
  blocking collectives  73.1 us (42%)
  starting transfers between devices  38.8 us (22%)
  other arithmetic  25.5 us (15%)
  local copies, waits for them, and re-layouts  14.4 us (8%)
  waiting for transfers between devices  11 us (6%)
  matrix products  10.3 us (6%)
    all_to_all x3, blocking collectives, spread(): return lax.all_to_all(copies, axis, 0, 0, tiled=False)  41.5 us
    all_to_all x2, blocking collectives, tree_psum(): flat = lax.all_to_all(chunks, axis, 0, 0, tiled=False).sum(0)  31.6 us
    ppermute x3, starting transfers between devices, swapped(): lax.ppermute(array, axis, [(i, i ^ 1 << stride) for i in range(lax.axis_s...  15.8 us
    reduce_sum x4, other arithmetic, depthwise_grad(): columns.append(jnp.sum(d_conv * window, axis=(1, 2)))  11.9 us
    ppermute x2, starting transfers between devices, with_halo(): lax.ppermute(head, axis, [((i + 1) % count, i) for i in range(count)])  11 us
    reduce_sum x1, other arithmetic, cell_pass(): chan_mean = jnp.mean(conv_blk, axis=0, keepdims=True)  8.26 us
    ppermute x2, starting transfers between devices, with_halo(): lax.ppermute(tail, axis, [(i, (i + 1) % count) for i in range(count)])  6.52 us
    ppermute x1, starting transfers between devices, mirrored_across(): return lax.ppermute(array, axis, [(i, count - 1 - i) for i in range(count)])  5.6 us
  transfers between devices with their start and end apart: 8, of which 4 were waited for; matrix products, arithmetic and copies ran while one was open for 2% of the time, Pallas kernels for 0%

profile of v5, /device:TPU:1, one launch (start us, length us, event | category | flops | bytes accessed | tf_op | source)
XLA Modules:
  0.0 174.2 jit_solution(10026667024181465023)
XLA Ops:
  3.5 4.6 %collective-permute-start = (bf16[200,8,3]{0,2,1:T(4,128)(2,1)S(1)}, bf16[200,8,3]{0,2,1:T(4,128)(2,1)S(1)}, u32[]{:S(2)}, u32[]{:S(2)}) collective-permute-start(bf16[200,8,3]{0,2,1:T(4,128)(2,1)S(1)} %get-tuple-element.78), channel_id=1, source_target_pairs={{0,4},{4,8},{8,12},{12,16},{16,20},{20,24},{24,28},{28,32},{32,36}... | collective-permute-start | bytes 28808 | tf_op jit(solution)/shard_map/ppermute | solution.py:23
  8.1 6.1 %collective-permute-start.1 = (bf16[200,8,3]{0,2,1:T(4,128)(2,1)S(1)}, bf16[200,8,3]{0,2,1:T(4,128)(2,1)S(1)}, u32[]{:S(2)}, u32[]{:S(2)}) collective-permute-start(bf16[200,8,3]{0,2,1:T(4,128)(2,1)S(1)} %get-tuple-element.79), channel_id=1, source_target_pairs={{4,0},{8,4},{12,8},{16,12},{20,16},{24,20},{28,24},{32,28},{36,32}... | collective-permute-start | bytes 28808 | tf_op jit(solution)/shard_map/ppermute | solution.py:25
  15.2 1.9 %collective-permute-start.2 = (bf16[200,3,134]{0,2,1:T(8,128)(2,1)S(1)}, bf16[200,3,134]{0,2,1:T(8,128)(2,1)S(1)}, u32[]{:S(2)}, u32[]{:S(2)}) collective-permute-start(bf16[200,3,134]{0,2,1:T(8,128)(2,1)S(1)} %get-tuple-element.77), channel_id=1, source_target_pairs={{0,1},{1,2},{2,3},{3,0},{4,5},{5,6},{6,7},{7,4},{8,9},{9,10},{10,1... | collective-permute-start | bytes 482408 | tf_op jit(solution)/shard_map/ppermute | solution.py:23
  18.1 5.6 %collective-permute-start.3 = (bf16[200,3,134]{0,2,1:T(8,128)(2,1)S(1)}, bf16[200,3,134]{0,2,1:T(8,128)(2,1)S(1)}, u32[]{:S(2)}, u32[]{:S(2)}) collective-permute-start(bf16[200,3,134]{0,2,1:T(8,128)(2,1)S(1)} %rev.3), channel_id=1, source_target_pairs={{0,124},{4,120},{8,116},{12,112},{16,108},{20,104},{24,100},{28,96... | collective-permute-start | bytes 482408 | tf_op jit(solution)/shard_map/ppermute | solution.py:38
  23.7 4.9 %collective-permute-start.4 = (bf16[200,3,134]{0,2,1:T(8,128)(2,1)S(1)}, bf16[200,3,134]{0,2,1:T(8,128)(2,1)S(1)}, u32[]{:S(2)}, u32[]{:S(2)}) collective-permute-start(bf16[200,3,134]{0,2,1:T(8,128)(2,1)S(1)} %get-tuple-element.76), channel_id=1, source_target_pairs={{1,0},{2,1},{3,2},{0,3},{5,4},{6,5},{7,6},{4,7},{9,8},{10,9},{11,1... | collective-permute-start | bytes 482408 | tf_op jit(solution)/shard_map/ppermute | solution.py:25
  28.6 5.6 %collective-permute-done.3 = bf16[200,3,134]{0,2,1:T(8,128)(2,1)S(1)} collective-permute-done((bf16[200,3,134]{0,2,1:T(8,128)(2,1)S(1)}, bf16[200,3,134]{0,2,1:T(8,128)(2,1)S(1)}, u32[]{:S(2)}, u32[]{:S(2)}) %collective-permute-start.3) | collective-permute-done | bytes 160832 | tf_op jit(solution)/shard_map/ppermute | solution.py:38
  34.5 8.3 %fusion.119 = (f32[8,128]{1,0:T(8,128)S(1)}, f32[200,8,128]{0,2,1:T(8,128)S(1)}) fusion(bf16[200,11,134]{0,2,1:T(8,128)(2,1)S(1)} %get-tuple-element.75, f32[200]{0:T(256)S(1)} %bitcast.308, f32[200]{0:T(256)S(1)} %bitcast.309, f32[200]{0:T(256)S(1)} %bitcast.262, f32[200]{0:T(256)S(1)} %bitcast.263, f32[200]{0:T(256)S(1)} %bitcast.264, ...), kind=kLoop, calls=%fused_computation.260 | loop fusion | flops 33790976 | bytes 18494496 | tf_op jit(solution)/shard_map/reduce_sum | solution.py:114
  45.3 2.2 %fusion.9 = (bf16[800,1024]{1,0:T(8,128)(2,1)}, f32[1024,800]{0,1:T(8,128)S(1)}) fusion(bf16[200,800]{1,0:T(8,128)(2,1)S(1)} %copy-done, f32[200,1024]{1,0:T(8,128)S(1)} %copy.163, f32[200]{0:T(256)S(1)} %copy-done.8, f32[1024]{0:T(1024)S(1)} %rsqrt_bitcast_fusion, f32[1024]{0:T(1024)S(1)} %get-tuple-element.131), kind=kOutput, calls=%fused_computation.12 | convolution fusion | flops 332595200 | bytes 6063392 | tf_op jit(solution)/shard_map/dot_general | solution.py:120
  47.5 1.7 fusion.5
  49.2 1.7 convolution_multiply_fusion.1
  55.0 3.8 %fusion.59 = (f32[200]{0:T(256)S(1)}, f32[200]{0:T(256)S(1)}, f32[200]{0:T(256)S(1)}, f32[200]{0:T(256)S(1)}, f32[200]{0:T(256)S(1)}, /*index=5*/f32[200]{0:T(25...) fusion(bf16[200,11,134]{0,2,1:T(8,128)(2,1)S(1)} %get-tuple-ele, ...), kind=kLoop, calls=%fused_computation.163 | loop fusion | flops 11055600 | bytes 8206400 | tf_op jit(solution)/shard_map/reduce_sum | solution.py:109
  58.8 3.8 %fusion.109 = (f32[200]{0:T(256)}, f32[200]{0:T(256)}, f32[200]{0:T(256)}, f32[200]{0:T(256)}, f32[200]{0:T(256)}, /*index=5*/f32[200]{0:T(256)}, f32[200]{0:T(2...) fusion(bf16[200,11,134]{0,2,1:T(8,128)(2,1)S(1)} %get-tuple-ele, ...), kind=kLoop, calls=%fused_computation.213 | loop fusion | flops 11055600 | bytes 8206400 | tf_op jit(solution)/shard_map/reduce_sum | solution.py:109
  64.8 3.0 %fusion.91 = (f32[200]{0:T(256)}, f32[200]{0:T(256)}, f32[200]{0:T(256)}, f32[200]{0:T(256)}, f32[200]{0:T(256)}, /*index=5*/f32[200]{0:T(256)}, f32[200]{0:T(25...) fusion(bf16[200,11,134]{0,2,1:T(8,128)(2,1)S(1)} %get-tuple-element.75, ...), kind=kLoop, calls=%fused_computation.195 | loop fusion | flops 11056800 | bytes 3715200 | tf_op jit(solution)/shard_map/reduce_sum | solution.py:109
  67.9 4.4 %stack.199 = f32[49,200]{1,0:T(8,128)S(1)} concatenate(f32[1,200]{1,0:T(1,128)} %bitcast.314, f32[1,200]{1,0:T(1,128)} %bitcast.315, f32[1,200]{1,0:T(1,128)} %bitcast.316, f32[1,200]{1,0:T(1,128)} %bitcast.242, f32[1,200]{1,0:T(1,128)} %bitcast.241, f32[1,200]{1,0:T(1,128)} %bitcast.240, f32[1,200]{1,0:T(1,128)} %bitcast.239, f32[1,200]{1,0:T(1,128)} %bitcast.238, ...), dimensions={0} | concatenate | bytes 78400 | tf_op jit(solution)/shard_map/stack | solution.py:110
  74.6 4.4 %collective-permute-start.5 = (f32[208,800]{1,0:T(8,128)S(1)}, f32[208,800]{1,0:T(8,128)S(1)}, u32[]{:S(2)}, u32[]{:S(2)}) collective-permute-start(f32[208,800]{1,0:T(8,128)S(1)} %fusion.110), channel_id=1, source_target_pairs={{0,4},{4,0},{1,5},{5,1},{2,6},{6,2},{3,7},{7,3},{8,12},{12,8},{9,1... | collective-permute-start | bytes 1996808 | tf_op jit(solution)/shard_map/ppermute | solution.py:33
  80.9 16.4 %all_to_all.25 = f32[4,52,800]{2,1,0:T(8,128)S(1)} all-to-all(f32[4,52,800]{2,1,0:T(8,128)S(1)} %reshape.154), channel_id=1, replica_groups=mesh['ens'=4,'lon_z'=2,'lon_y'=8,'lon_c'=2,'lat'=4] {'lat'}, dimensions={0} | all-to-all | bytes 1331200 | tf_op jit(solution)/shard_map/all_to_all | solution.py:59
  97.4 15.2 %all_to_all.26 = f32[4,13,800]{2,1,0:T(8,128)S(1)} all-to-all(f32[4,13,800]{2,1,0:T(8,128)S(1)} %reshape.155), channel_id=1, replica_groups=mesh['ens'=4,'lon_z'=2,'lon_y'=8,'lon_c'=2,'lat'=4] {'ens'}, dimensions={0} | all-to-all | bytes 332800 | tf_op jit(solution)/shard_map/all_to_all | solution.py:59
  112.6 17.7 %all_to_all.27 = f32[8,13,800]{2,1,0:T(8,128)S(1)} all-to-all(f32[8,13,800]{2,1,0:T(8,128)S(1)} %broadcast_in_dim.11), channel_id=1, replica_groups=mesh['ens'=4,'lon_z'=2,'lon_y'=8,'lon_c'=2,'lat'=4] {'lon_y'}, dimensions={0} | all-to-all | bytes 665600 | tf_op jit(solution)/shard_map/all_to_all | solution.py:48
  130.4 1.9 %collective-permute-start.6 = (f32[13,800]{1,0:T(8,128)S(1)}, f32[13,800]{1,0:T(8,128)S(1)}, u32[]{:S(2)}, u32[]{:S(2)}) collective-permute-start(f32[13,800]{1,0:T(8,128)S(1)} %reduce_sum.569), channel_id=1, source_target_pairs={{0,64},{64,0},{1,65},{65,1},{2,66},{66,2},{3,67},{67,3},{4,68},{68... | collective-permute-start | bytes 124808 | tf_op jit(solution)/shard_map/ppermute | solution.py:33
  132.3 3.0 %collective-permute-done.6 = f32[13,800]{1,0:T(8,128)S(1)} collective-permute-done((f32[13,800]{1,0:T(8,128)S(1)}, f32[13,800]{1,0:T(8,128)S(1)}, u32[]{:S(2)}, u32[]{:S(2)}) %collective-permute-start.6) | collective-permute-done | bytes 41632 | tf_op jit(solution)/shard_map/ppermute | solution.py:33
  135.3 12.9 %all_to_all.28 = f32[4,13,800]{2,1,0:T(8,128)S(1)} all-to-all(f32[4,13,800]{2,1,0:T(8,128)S(1)} %broadcast_in_dim.12), channel_id=1, replica_groups=mesh['ens'=4,'lon_z'=2,'lon_y'=8,'lon_c'=2,'lat'=4] {'ens'}, dimensions={0} | all-to-all | bytes 332800 | tf_op jit(solution)/shard_map/all_to_all | solution.py:48
  148.3 10.9 %all_to_all.29 = f32[4,52,800]{2,1,0:T(8,128)S(1)} all-to-all(f32[4,52,800]{2,1,0:T(8,128)S(1)} %broadcast_in_dim.14), channel_id=1, replica_groups=mesh['ens'=4,'lon_z'=2,'lon_y'=8,'lon_c'=2,'lat'=4] {'lat'}, dimensions={0} | all-to-all | bytes 1331200 | tf_op jit(solution)/shard_map/all_to_all | solution.py:48
  159.4 9.5 %collective-permute-start.7 = (f32[208,800]{1,0:T(8,128)S(1)}, f32[208,800]{1,0:T(8,128)S(1)}, u32[]{:S(2)}, u32[]{:S(2)}) collective-permute-start(f32[208,800]{1,0:T(8,128)S(1)} %reshape.156), channel_id=1, source_target_pairs={{0,4},{4,0},{1,5},{5,1},{2,6},{6,2},{3,7},{7,3},{8,12},{12,8},{9,1... | collective-permute-start | bytes 1996808 | tf_op jit(solution)/shard_map/ppermute | solution.py:33
  168.9 1.7 fusion.13
  (84 shorter events, 22.0 us)
Async XLA Ops:
  0.6 44.7 %copy-start = (bf16[200,800]{1,0:T(8,128)(2,1)S(1)}, bf16[200,800]{1,0:T(8,128)(2,1)}, u32[]{:S(2)}) copy-start(bf16[200,800]{1,0:T(8,128)(2,1)} %param.11) | copy-start | bytes 960004
  0.6 13.6 %copy-start.7 = (f32[200,49]{0,1:T(8,128)S(1)}, f32[200,49]{0,1:T(8,128)}, u32[]{:S(2)}) copy-start(f32[200,49]{0,1:T(8,128)} %param.9) | copy-start | bytes 117604
  3.5 10.8 %collective-permute-start = (bf16[200,8,3]{0,2,1:T(4,128)(2,1)S(1)}, bf16[200,8,3]{0,2,1:T(4,128)(2,1)S(1)}, u32[]{:S(2)}, u32[]{:S(2)}) collective-permute-start(bf16[200,8,3]{0,2,1:T(4,128)(2,1)S(1)} %get-tuple-element.78), channel_id=1, source_target_pairs={{0,4},{4,8},{8,12},{12,16},{16,20},{20,24},{24,28},{28,32},{32,36}... | collective-permute-start | bytes 28808 | tf_op jit(solution)/shard_map/ppermute | solution.py:23
  8.1 6.9 %collective-permute-start.1 = (bf16[200,8,3]{0,2,1:T(4,128)(2,1)S(1)}, bf16[200,8,3]{0,2,1:T(4,128)(2,1)S(1)}, u32[]{:S(2)}, u32[]{:S(2)}) collective-permute-start(bf16[200,8,3]{0,2,1:T(4,128)(2,1)S(1)} %get-tuple-element.79), channel_id=1, source_target_pairs={{4,0},{8,4},{12,8},{16,12},{20,16},{24,20},{28,24},{32,28},{36,32}... | collective-permute-start | bytes 28808 | tf_op jit(solution)/shard_map/ppermute | solution.py:25
  15.2 13.4 %collective-permute-start.2 = (bf16[200,3,134]{0,2,1:T(8,128)(2,1)S(1)}, bf16[200,3,134]{0,2,1:T(8,128)(2,1)S(1)}, u32[]{:S(2)}, u32[]{:S(2)}) collective-permute-start(bf16[200,3,134]{0,2,1:T(8,128)(2,1)S(1)} %get-tuple-element.77), channel_id=1, source_target_pairs={{0,1},{1,2},{2,3},{3,0},{4,5},{5,6},{6,7},{7,4},{8,9},{9,10},{10,1... | collective-permute-start | bytes 482408 | tf_op jit(solution)/shard_map/ppermute | solution.py:23
  18.1 16.1 %collective-permute-start.3 = (bf16[200,3,134]{0,2,1:T(8,128)(2,1)S(1)}, bf16[200,3,134]{0,2,1:T(8,128)(2,1)S(1)}, u32[]{:S(2)}, u32[]{:S(2)}) collective-permute-start(bf16[200,3,134]{0,2,1:T(8,128)(2,1)S(1)} %rev.3), channel_id=1, source_target_pairs={{0,124},{4,120},{8,116},{12,112},{16,108},{20,104},{24,100},{28,96... | collective-permute-start | bytes 482408 | tf_op jit(solution)/shard_map/ppermute | solution.py:38
  23.7 10.5 %collective-permute-start.4 = (bf16[200,3,134]{0,2,1:T(8,128)(2,1)S(1)}, bf16[200,3,134]{0,2,1:T(8,128)(2,1)S(1)}, u32[]{:S(2)}, u32[]{:S(2)}) collective-permute-start(bf16[200,3,134]{0,2,1:T(8,128)(2,1)S(1)} %get-tuple-element.76), channel_id=1, source_target_pairs={{1,0},{2,1},{3,2},{0,3},{5,4},{6,5},{7,6},{4,7},{9,8},{10,9},{11,1... | collective-permute-start | bytes 482408 | tf_op jit(solution)/shard_map/ppermute | solution.py:25
  42.8 1.0 copy-start.1
  42.8 2.5 %copy-start.8 = (f32[200]{0:T(256)S(1)}, f32[200]{0:T(256)}, u32[]{:S(2)}) copy-start(f32[200]{0:T(256)} %param.10) | copy-start | bytes 2404
  45.3 2.2 %copy-start.12 = (bf16[1,200,8,128]{3,2,1,0:T(8,128)(2,1)S(1)}, bf16[1,200,8,128]{3,2,1,0:T(8,128)(2,1)}, u32[]{:S(2)}) copy-start(bf16[1,200,8,128]{3,2,1,0:T(8,128)(2,1)} %param.13) | copy-start | bytes 1228804
  45.3 2.2 %copy-start.14 = (bf16[800,200]{0,1:T(8,128)(2,1)S(1)}, bf16[800,200]{0,1:T(8,128)(2,1)}, u32[]{:S(2)}) copy-start(bf16[800,200]{0,1:T(8,128)(2,1)} %param.12) | copy-start | bytes 960004
  50.9 1.4 copy-start.6
  58.8 3.8 %copy-start.4 = (bf16[800,1024]{1,0:T(8,128)(2,1)S(1)}, bf16[800,1024]{1,0:T(8,128)(2,1)}, u32[]{:S(2)}) copy-start(bf16[800,1024]{1,0:T(8,128)(2,1)} %get-tuple-element.133) | copy-start | bytes 4915204
  58.8 3.8 %copy-start.13 = (bf16[1,200,8,128]{3,2,1,0:T(8,128)(2,1)S(1)}, bf16[1,200,8,128]{3,2,1,0:T(8,128)(2,1)}, u32[]{:S(2)}) copy-start(bf16[1,200,8,128]{3,2,1,0:T(8,128)(2,1)} %param.13) | copy-start | bytes 1228804
  62.6 1.6 copy-start.11
  64.8 3.0 %copy-start.9 = (f32[200]{0:T(256)S(1)}, f32[200]{0:T(256)}, u32[]{:S(2)}) copy-start(f32[200]{0:T(256)} %get-tuple-element.38) | copy-start | bytes 2404
  67.8 12.8 %copy-start.2 = (f32[200,800]{1,0:T(8,128)S(1)}, f32[200,800]{1,0:T(8,128)}, u32[]{:S(2)}) copy-start(f32[200,800]{1,0:T(8,128)} %convolution_multiply_fusion.1) | copy-start | bytes 1920004
  67.8 12.8 %copy-start.3 = (f32[200,800]{1,0:T(8,128)S(1)}, f32[200,800]{1,0:T(8,128)}, u32[]{:S(2)}) copy-start(f32[200,800]{1,0:T(8,128)} %convolution_multiply_fusion) | copy-start | bytes 1920004
  74.6 6.0 %collective-permute-start.5 = (f32[208,800]{1,0:T(8,128)S(1)}, f32[208,800]{1,0:T(8,128)S(1)}, u32[]{:S(2)}, u32[]{:S(2)}) collective-permute-start(f32[208,800]{1,0:T(8,128)S(1)} %fusion.110), channel_id=1, source_target_pairs={{0,4},{4,0},{1,5},{5,1},{2,6},{6,2},{3,7},{7,3},{8,12},{12,8},{9,1... | collective-permute-start | bytes 1996808 | tf_op jit(solution)/shard_map/ppermute | solution.py:33
  130.4 4.9 %collective-permute-start.6 = (f32[13,800]{1,0:T(8,128)S(1)}, f32[13,800]{1,0:T(8,128)S(1)}, u32[]{:S(2)}, u32[]{:S(2)}) collective-permute-start(f32[13,800]{1,0:T(8,128)S(1)} %reduce_sum.569), channel_id=1, source_target_pairs={{0,64},{64,0},{1,65},{65,1},{2,66},{66,2},{3,67},{67,3},{4,68},{68... | collective-permute-start | bytes 124808 | tf_op jit(solution)/shard_map/ppermute | solution.py:33
  148.3 20.5 %copy-start.5 = (bf16[800,1024]{1,0:T(8,128)(2,1)S(1)}, bf16[800,1024]{1,0:T(8,128)(2,1)}, u32[]{:S(2)}) copy-start(bf16[800,1024]{1,0:T(8,128)(2,1)} %get-tuple-element.133) | copy-start | bytes 4915204
  148.3 20.5 %copy-start.10 = (f32[1024]{0:T(1024)S(1)}, f32[1024]{0:T(1024)}, u32[]{:S(2)}) copy-start(f32[1024]{0:T(1024)} %get-tuple-element.129) | copy-start | bytes 12292
  159.4 12.1 %collective-permute-start.7 = (f32[208,800]{1,0:T(8,128)S(1)}, f32[208,800]{1,0:T(8,128)S(1)}, u32[]{:S(2)}, u32[]{:S(2)}) collective-permute-start(f32[208,800]{1,0:T(8,128)S(1)} %reshape.156), channel_id=1, source_target_pairs={{0,4},{4,0},{1,5},{5,1},{2,6},{6,2},{3,7},{7,3},{8,12},{12,8},{9,1... | collective-permute-start | bytes 1996808 | tf_op jit(solution)/shard_map/ppermute | solution.py:33

commit v6 on v5

--- a/solution.py
+++ b/solution.py
@@ -184,7 +184,7 @@
     small_rows += -small_rows % 8
     small = jnp.pad(small, (0, small_rows * width - small.shape[0])).reshape(small_rows, width)
     packed = jnp.concatenate([grad_expand, grad_reduce.T, small], axis=0)
-    packed = tree_psum(packed, REDUCE_ORDER, jnp.float32)
+    packed = tree_psum(packed, REDUCE_ORDER, jnp.bfloat16)
     grad_expand = packed[:channels]
     grad_reduce = packed[channels : 2 * channels].T
     small = packed[2 * channels :].reshape(-1)[: channels * (KS * KS + 1)].reshape(-1, channels)

time: 175 us -> 172 us (0.983)
  blocking collectives: 73.1 us -> 69.9 us
    all_to_all x3, blocking collectives: 41.5 us -> 38.3 us  [spread(): return lax.all_to_all(copies, axis, 0, 0, tiled=False)]
where the time goes in v6:
time: 172 us; the launch traced here: 171 us
  blocking collectives  69.9 us (41%)
  starting transfers between devices  38.8 us (23%)
  other arithmetic  25.6 us (15%)
  local copies, waits for them, and re-layouts  14.4 us (8%)
  waiting for transfers between devices  11 us (6%)
  matrix products  10.1 us (6%)
    all_to_all x3, blocking collectives, spread(): return lax.all_to_all(copies, axis, 0, 0, tiled=False)  38.3 us
    all_to_all x2, blocking collectives, tree_psum(): flat = lax.all_to_all(chunks, axis, 0, 0, tiled=False).sum(0)  31.6 us
    ppermute x3, starting transfers between devices, swapped(): lax.ppermute(array, axis, [(i, i ^ 1 << stride) for i in range(lax.axis_s...  15.7 us
    reduce_sum x4, other arithmetic, depthwise_grad(): columns.append(jnp.sum(d_conv * window, axis=(1, 2)))  11.9 us
    ppermute x2, starting transfers between devices, with_halo(): lax.ppermute(head, axis, [((i + 1) % count, i) for i in range(count)])  11 us
    reduce_sum x1, other arithmetic, cell_pass(): chan_mean = jnp.mean(conv_blk, axis=0, keepdims=True)  8.26 us
    ppermute x2, starting transfers between devices, with_halo(): lax.ppermute(tail, axis, [(i, (i + 1) % count) for i in range(count)])  6.52 us
    ppermute x1, starting transfers between devices, mirrored_across(): return lax.ppermute(array, axis, [(i, count - 1 - i) for i in range(count)])  5.6 us
  transfers between devices with their start and end apart: 8, of which 4 were waited for; matrix products, arithmetic and copies ran while one was open for 2% of the time, Pallas kernels for 0%

profile of v6, /device:TPU:1, one launch (start us, length us, event | category | flops | bytes accessed | tf_op | source)
XLA Modules:
  0.0 170.9 jit_solution(10600984772799129898)
XLA Ops:
  3.5 4.6 %collective-permute-start = (bf16[200,8,3]{0,2,1:T(4,128)(2,1)S(1)}, bf16[200,8,3]{0,2,1:T(4,128)(2,1)S(1)}, u32[]{:S(2)}, u32[]{:S(2)}) collective-permute-start(bf16[200,8,3]{0,2,1:T(4,128)(2,1)S(1)} %get-tuple-element.78), channel_id=1, source_target_pairs={{0,4},{4,8},{8,12},{12,16},{16,20},{20,24},{24,28},{28,32},{32,36}... | collective-permute-start | bytes 28808 | tf_op jit(solution)/shard_map/ppermute | solution.py:23
  8.1 6.1 %collective-permute-start.1 = (bf16[200,8,3]{0,2,1:T(4,128)(2,1)S(1)}, bf16[200,8,3]{0,2,1:T(4,128)(2,1)S(1)}, u32[]{:S(2)}, u32[]{:S(2)}) collective-permute-start(bf16[200,8,3]{0,2,1:T(4,128)(2,1)S(1)} %get-tuple-element.79), channel_id=1, source_target_pairs={{4,0},{8,4},{12,8},{16,12},{20,16},{24,20},{28,24},{32,28},{36,32}... | collective-permute-start | bytes 28808 | tf_op jit(solution)/shard_map/ppermute | solution.py:25
  15.2 1.9 %collective-permute-start.2 = (bf16[200,3,134]{0,2,1:T(8,128)(2,1)S(1)}, bf16[200,3,134]{0,2,1:T(8,128)(2,1)S(1)}, u32[]{:S(2)}, u32[]{:S(2)}) collective-permute-start(bf16[200,3,134]{0,2,1:T(8,128)(2,1)S(1)} %get-tuple-element.77), channel_id=1, source_target_pairs={{0,1},{1,2},{2,3},{3,0},{4,5},{5,6},{6,7},{7,4},{8,9},{9,10},{10,1... | collective-permute-start | bytes 482408 | tf_op jit(solution)/shard_map/ppermute | solution.py:23
  18.1 5.6 %collective-permute-start.3 = (bf16[200,3,134]{0,2,1:T(8,128)(2,1)S(1)}, bf16[200,3,134]{0,2,1:T(8,128)(2,1)S(1)}, u32[]{:S(2)}, u32[]{:S(2)}) collective-permute-start(bf16[200,3,134]{0,2,1:T(8,128)(2,1)S(1)} %rev.3), channel_id=1, source_target_pairs={{0,124},{4,120},{8,116},{12,112},{16,108},{20,104},{24,100},{28,96... | collective-permute-start | bytes 482408 | tf_op jit(solution)/shard_map/ppermute | solution.py:38
  23.7 4.9 %collective-permute-start.4 = (bf16[200,3,134]{0,2,1:T(8,128)(2,1)S(1)}, bf16[200,3,134]{0,2,1:T(8,128)(2,1)S(1)}, u32[]{:S(2)}, u32[]{:S(2)}) collective-permute-start(bf16[200,3,134]{0,2,1:T(8,128)(2,1)S(1)} %get-tuple-element.76), channel_id=1, source_target_pairs={{1,0},{2,1},{3,2},{0,3},{5,4},{6,5},{7,6},{4,7},{9,8},{10,9},{11,1... | collective-permute-start | bytes 482408 | tf_op jit(solution)/shard_map/ppermute | solution.py:25
  28.6 5.6 %collective-permute-done.3 = bf16[200,3,134]{0,2,1:T(8,128)(2,1)S(1)} collective-permute-done((bf16[200,3,134]{0,2,1:T(8,128)(2,1)S(1)}, bf16[200,3,134]{0,2,1:T(8,128)(2,1)S(1)}, u32[]{:S(2)}, u32[]{:S(2)}) %collective-permute-start.3) | collective-permute-done | bytes 160832 | tf_op jit(solution)/shard_map/ppermute | solution.py:38
  34.5 8.3 %fusion.120 = (f32[8,128]{1,0:T(8,128)S(1)}, f32[200,8,128]{0,2,1:T(8,128)S(1)}) fusion(bf16[200,11,134]{0,2,1:T(8,128)(2,1)S(1)} %get-tuple-element.75, f32[200]{0:T(256)S(1)} %bitcast.308, f32[200]{0:T(256)S(1)} %bitcast.309, f32[200]{0:T(256)S(1)} %bitcast.262, f32[200]{0:T(256)S(1)} %bitcast.263, f32[200]{0:T(256)S(1)} %bitcast.264, ...), kind=kLoop, calls=%fused_computation.262 | loop fusion | flops 33790976 | bytes 18494496 | tf_op jit(solution)/shard_map/reduce_sum | solution.py:114
  45.3 2.2 %fusion.9 = (bf16[800,1024]{1,0:T(8,128)(2,1)}, f32[1024,800]{0,1:T(8,128)S(1)}) fusion(bf16[200,800]{1,0:T(8,128)(2,1)S(1)} %copy-done, f32[200,1024]{1,0:T(8,128)S(1)} %copy.163, f32[200]{0:T(256)S(1)} %copy-done.9, f32[1024]{0:T(1024)S(1)} %rsqrt_bitcast_fusion, f32[1024]{0:T(1024)S(1)} %get-tuple-element.131), kind=kOutput, calls=%fused_computation.12 | convolution fusion | flops 332595200 | bytes 6063392 | tf_op jit(solution)/shard_map/dot_general | solution.py:120
  47.5 1.7 fusion.5
  49.2 1.7 %convolution_multiply_fusion.1 = f32[200,800]{1,0:T(8,128)} fusion(bf16[800,1024]{1,0:T(8,128)(2,1)S(1)} %fusion.5, f32[200,1024]{1,0:T(8,128)S(1)} %copy.163, f32[200]{0:T(256)S(1)} %copy-done.9, f32[1024]{0:T(1024)S(1)} %rsqrt_bitcast_fusion, f32[1024]{0:T(1024)S(1)} %get-tuple-element.131), kind=kOutput, calls=%fused_computation.114 | convolution fusion | flops 328659200 | bytes 3106592 | tf_op jit(solution)/shard_map/dot_general | solution.py:130
  55.0 3.8 %fusion.59 = (f32[200]{0:T(256)S(1)}, f32[200]{0:T(256)S(1)}, f32[200]{0:T(256)S(1)}, f32[200]{0:T(256)S(1)}, f32[200]{0:T(256)S(1)}, /*index=5*/f32[200]{0:T(25...) fusion(bf16[200,11,134]{0,2,1:T(8,128)(2,1)S(1)} %get-tuple-ele, ...), kind=kLoop, calls=%fused_computation.162 | loop fusion | flops 11055600 | bytes 8206400 | tf_op jit(solution)/shard_map/reduce_sum | solution.py:109
  58.8 3.8 %fusion.109 = (f32[200]{0:T(256)}, f32[200]{0:T(256)}, f32[200]{0:T(256)}, f32[200]{0:T(256)}, f32[200]{0:T(256)}, /*index=5*/f32[200]{0:T(256)}, f32[200]{0:T(2...) fusion(bf16[200,11,134]{0,2,1:T(8,128)(2,1)S(1)} %get-tuple-ele, ...), kind=kLoop, calls=%fused_computation.212 | loop fusion | flops 11055600 | bytes 8206400 | tf_op jit(solution)/shard_map/reduce_sum | solution.py:109
  64.8 3.0 %fusion.91 = (f32[200]{0:T(256)}, f32[200]{0:T(256)}, f32[200]{0:T(256)}, f32[200]{0:T(256)}, f32[200]{0:T(256)}, /*index=5*/f32[200]{0:T(256)}, f32[200]{0:T(25...) fusion(bf16[200,11,134]{0,2,1:T(8,128)(2,1)S(1)} %get-tuple-element.75, ...), kind=kLoop, calls=%fused_computation.194 | loop fusion | flops 11056800 | bytes 3715200 | tf_op jit(solution)/shard_map/reduce_sum | solution.py:109
  67.9 4.4 %stack.199 = f32[49,200]{1,0:T(8,128)S(1)} concatenate(f32[1,200]{1,0:T(1,128)} %bitcast.314, f32[1,200]{1,0:T(1,128)} %bitcast.315, f32[1,200]{1,0:T(1,128)} %bitcast.316, f32[1,200]{1,0:T(1,128)} %bitcast.242, f32[1,200]{1,0:T(1,128)} %bitcast.241, f32[1,200]{1,0:T(1,128)} %bitcast.240, f32[1,200]{1,0:T(1,128)} %bitcast.239, f32[1,200]{1,0:T(1,128)} %bitcast.238, ...), dimensions={0} | concatenate | bytes 78400 | tf_op jit(solution)/shard_map/stack | solution.py:110
  74.6 4.4 %collective-permute-start.5 = (f32[208,800]{1,0:T(8,128)S(1)}, f32[208,800]{1,0:T(8,128)S(1)}, u32[]{:S(2)}, u32[]{:S(2)}) collective-permute-start(f32[208,800]{1,0:T(8,128)S(1)} %fusion.111), channel_id=1, source_target_pairs={{0,4},{4,0},{1,5},{5,1},{2,6},{6,2},{3,7},{7,3},{8,12},{12,8},{9,1... | collective-permute-start | bytes 1996808 | tf_op jit(solution)/shard_map/ppermute | solution.py:33
  79.0 1.7 collective-permute-done.5
  80.9 16.4 %all_to_all.25 = f32[4,52,800]{2,1,0:T(8,128)S(1)} all-to-all(f32[4,52,800]{2,1,0:T(8,128)S(1)} %reshape.154), channel_id=1, replica_groups=mesh['ens'=4,'lon_z'=2,'lon_y'=8,'lon_c'=2,'lat'=4] {'lat'}, dimensions={0} | all-to-all | bytes 1331200 | tf_op jit(solution)/shard_map/all_to_all | solution.py:59
  97.4 15.2 %all_to_all.26 = f32[4,13,800]{2,1,0:T(8,128)S(1)} all-to-all(f32[4,13,800]{2,1,0:T(8,128)S(1)} %reshape.155), channel_id=1, replica_groups=mesh['ens'=4,'lon_z'=2,'lon_y'=8,'lon_c'=2,'lat'=4] {'ens'}, dimensions={0} | all-to-all | bytes 332800 | tf_op jit(solution)/shard_map/all_to_all | solution.py:59
  112.6 17.7 %all_to_all.27 = f32[8,13,800]{2,1,0:T(8,128)S(1)} all-to-all(f32[8,13,800]{2,1,0:T(8,128)S(1)} %broadcast_in_dim.11), channel_id=1, replica_groups=mesh['ens'=4,'lon_z'=2,'lon_y'=8,'lon_c'=2,'lat'=4] {'lon_y'}, dimensions={0} | all-to-all | bytes 665600 | tf_op jit(solution)/shard_map/all_to_all | solution.py:48
  130.4 2.1 %collective-permute-start.6 = (f32[13,800]{1,0:T(8,128)S(1)}, f32[13,800]{1,0:T(8,128)S(1)}, u32[]{:S(2)}, u32[]{:S(2)}) collective-permute-start(f32[13,800]{1,0:T(8,128)S(1)} %reduce_sum.569), channel_id=1, source_target_pairs={{0,64},{64,0},{1,65},{65,1},{2,66},{66,2},{3,67},{67,3},{4,68},{68... | collective-permute-start | bytes 124808 | tf_op jit(solution)/shard_map/ppermute | solution.py:33
  132.4 3.0 %collective-permute-done.6 = f32[13,800]{1,0:T(8,128)S(1)} collective-permute-done((f32[13,800]{1,0:T(8,128)S(1)}, f32[13,800]{1,0:T(8,128)S(1)}, u32[]{:S(2)}, u32[]{:S(2)}) %collective-permute-start.6) | collective-permute-done | bytes 41632 | tf_op jit(solution)/shard_map/ppermute | solution.py:33
  135.5 11.9 %all_to_all.28 = bf16[4,13,800]{2,1,0:T(8,128)(2,1)S(1)} all-to-all(bf16[4,13,800]{2,1,0:T(8,128)(2,1)S(1)} %broadcast_in_dim.12), channel_id=1, replica_groups=mesh['ens'=4,'lon_z'=2,'lon_y'=8,'lon_c'=2,'lat'=4] {'ens'}, dimensions={0} | all-to-all | bytes 166400 | tf_op jit(solution)/shard_map/all_to_all | solution.py:48
  147.5 8.7 %all_to_all.29 = bf16[4,52,800]{2,1,0:T(8,128)(2,1)S(1)} all-to-all(bf16[4,52,800]{2,1,0:T(8,128)(2,1)S(1)} %broadcast_in_dim.14), channel_id=1, replica_groups=mesh['ens'=4,'lon_z'=2,'lon_y'=8,'lon_c'=2,'lat'=4] {'lat'}, dimensions={0} | all-to-all | bytes 665600 | tf_op jit(solution)/shard_map/all_to_all | solution.py:48
  156.3 9.3 %collective-permute-start.7 = (bf16[208,800]{1,0:T(8,128)(2,1)S(1)}, bf16[208,800]{1,0:T(8,128)(2,1)S(1)}, u32[]{:S(2)}, u32[]{:S(2)}) collective-permute-start(bf16[208,800]{1,0:T(8,128)(2,1)S(1)} %reshape.156), channel_id=1, source_target_pairs={{0,4},{4,0},{1,5},{5,1},{2,6},{6,2},{3,7},{7,3},{8,12},{12,8},{9,1... | collective-permute-start | bytes 998408 | tf_op jit(solution)/shard_map/ppermute | solution.py:33
  (86 shorter events, 22.0 us)
Async XLA Ops:
  0.6 44.7 %copy-start = (bf16[200,800]{1,0:T(8,128)(2,1)S(1)}, bf16[200,800]{1,0:T(8,128)(2,1)}, u32[]{:S(2)}) copy-start(bf16[200,800]{1,0:T(8,128)(2,1)} %param.11) | copy-start | bytes 960004
  0.6 13.6 %copy-start.8 = (f32[200,49]{0,1:T(8,128)S(1)}, f32[200,49]{0,1:T(8,128)}, u32[]{:S(2)}) copy-start(f32[200,49]{0,1:T(8,128)} %param.9) | copy-start | bytes 117604
  3.5 10.8 %collective-permute-start = (bf16[200,8,3]{0,2,1:T(4,128)(2,1)S(1)}, bf16[200,8,3]{0,2,1:T(4,128)(2,1)S(1)}, u32[]{:S(2)}, u32[]{:S(2)}) collective-permute-start(bf16[200,8,3]{0,2,1:T(4,128)(2,1)S(1)} %get-tuple-element.78), channel_id=1, source_target_pairs={{0,4},{4,8},{8,12},{12,16},{16,20},{20,24},{24,28},{28,32},{32,36}... | collective-permute-start | bytes 28808 | tf_op jit(solution)/shard_map/ppermute | solution.py:23
  8.1 6.9 %collective-permute-start.1 = (bf16[200,8,3]{0,2,1:T(4,128)(2,1)S(1)}, bf16[200,8,3]{0,2,1:T(4,128)(2,1)S(1)}, u32[]{:S(2)}, u32[]{:S(2)}) collective-permute-start(bf16[200,8,3]{0,2,1:T(4,128)(2,1)S(1)} %get-tuple-element.79), channel_id=1, source_target_pairs={{4,0},{8,4},{12,8},{16,12},{20,16},{24,20},{28,24},{32,28},{36,32}... | collective-permute-start | bytes 28808 | tf_op jit(solution)/shard_map/ppermute | solution.py:25
  15.2 13.4 %collective-permute-start.2 = (bf16[200,3,134]{0,2,1:T(8,128)(2,1)S(1)}, bf16[200,3,134]{0,2,1:T(8,128)(2,1)S(1)}, u32[]{:S(2)}, u32[]{:S(2)}) collective-permute-start(bf16[200,3,134]{0,2,1:T(8,128)(2,1)S(1)} %get-tuple-element.77), channel_id=1, source_target_pairs={{0,1},{1,2},{2,3},{3,0},{4,5},{5,6},{6,7},{7,4},{8,9},{9,10},{10,1... | collective-permute-start | bytes 482408 | tf_op jit(solution)/shard_map/ppermute | solution.py:23
  18.1 16.1 %collective-permute-start.3 = (bf16[200,3,134]{0,2,1:T(8,128)(2,1)S(1)}, bf16[200,3,134]{0,2,1:T(8,128)(2,1)S(1)}, u32[]{:S(2)}, u32[]{:S(2)}) collective-permute-start(bf16[200,3,134]{0,2,1:T(8,128)(2,1)S(1)} %rev.3), channel_id=1, source_target_pairs={{0,124},{4,120},{8,116},{12,112},{16,108},{20,104},{24,100},{28,96... | collective-permute-start | bytes 482408 | tf_op jit(solution)/shard_map/ppermute | solution.py:38
  23.7 10.5 %collective-permute-start.4 = (bf16[200,3,134]{0,2,1:T(8,128)(2,1)S(1)}, bf16[200,3,134]{0,2,1:T(8,128)(2,1)S(1)}, u32[]{:S(2)}, u32[]{:S(2)}) collective-permute-start(bf16[200,3,134]{0,2,1:T(8,128)(2,1)S(1)} %get-tuple-element.76), channel_id=1, source_target_pairs={{1,0},{2,1},{3,2},{0,3},{5,4},{6,5},{7,6},{4,7},{9,8},{10,9},{11,1... | collective-permute-start | bytes 482408 | tf_op jit(solution)/shard_map/ppermute | solution.py:25
  42.8 1.0 copy-start.1
  42.8 2.5 %copy-start.9 = (f32[200]{0:T(256)S(1)}, f32[200]{0:T(256)}, u32[]{:S(2)}) copy-start(f32[200]{0:T(256)} %param.10) | copy-start | bytes 2404
  45.3 2.2 %copy-start.13 = (bf16[1,200,8,128]{3,2,1,0:T(8,128)(2,1)S(1)}, bf16[1,200,8,128]{3,2,1,0:T(8,128)(2,1)}, u32[]{:S(2)}) copy-start(bf16[1,200,8,128]{3,2,1,0:T(8,128)(2,1)} %param.13) | copy-start | bytes 1228804
  45.3 2.2 %copy-start.15 = (bf16[800,200]{0,1:T(8,128)(2,1)S(1)}, bf16[800,200]{0,1:T(8,128)(2,1)}, u32[]{:S(2)}) copy-start(bf16[800,200]{0,1:T(8,128)(2,1)} %param.12) | copy-start | bytes 960004
  50.9 1.4 copy-start.6
  58.8 3.8 %copy-start.4 = (bf16[800,1024]{1,0:T(8,128)(2,1)S(1)}, bf16[800,1024]{1,0:T(8,128)(2,1)}, u32[]{:S(2)}) copy-start(bf16[800,1024]{1,0:T(8,128)(2,1)} %get-tuple-element.133) | copy-start | bytes 4915204
  58.8 3.8 %copy-start.14 = (bf16[1,200,8,128]{3,2,1,0:T(8,128)(2,1)S(1)}, bf16[1,200,8,128]{3,2,1,0:T(8,128)(2,1)}, u32[]{:S(2)}) copy-start(bf16[1,200,8,128]{3,2,1,0:T(8,128)(2,1)} %param.13) | copy-start | bytes 1228804
  62.6 1.6 copy-start.12
  64.8 3.0 %copy-start.10 = (f32[200]{0:T(256)S(1)}, f32[200]{0:T(256)}, u32[]{:S(2)}) copy-start(f32[200]{0:T(256)} %get-tuple-element.38) | copy-start | bytes 2404
  67.8 12.8 %copy-start.2 = (f32[200,800]{1,0:T(8,128)S(1)}, f32[200,800]{1,0:T(8,128)}, u32[]{:S(2)}) copy-start(f32[200,800]{1,0:T(8,128)} %convolution_multiply_fusion.1) | copy-start | bytes 1920004
  67.8 12.8 %copy-start.3 = (f32[200,800]{1,0:T(8,128)S(1)}, f32[200,800]{1,0:T(8,128)}, u32[]{:S(2)}) copy-start(f32[200,800]{1,0:T(8,128)} %convolution_multiply_fusion) | copy-start | bytes 1920004
  74.6 6.0 %collective-permute-start.5 = (f32[208,800]{1,0:T(8,128)S(1)}, f32[208,800]{1,0:T(8,128)S(1)}, u32[]{:S(2)}, u32[]{:S(2)}) collective-permute-start(f32[208,800]{1,0:T(8,128)S(1)} %fusion.111), channel_id=1, source_target_pairs={{0,4},{4,0},{1,5},{5,1},{2,6},{6,2},{3,7},{7,3},{8,12},{12,8},{9,1... | collective-permute-start | bytes 1996808 | tf_op jit(solution)/shard_map/ppermute | solution.py:33
  130.3 35.3 %copy-start.5 = (bf16[800,1024]{1,0:T(8,128)(2,1)S(1)}, bf16[800,1024]{1,0:T(8,128)(2,1)}, u32[]{:S(2)}) copy-start(bf16[800,1024]{1,0:T(8,128)(2,1)} %get-tuple-element.133) | copy-start | bytes 4915204
  130.3 35.3 %copy-start.7 = (bf16[1,200,8,128]{3,2,1,0:T(8,128)(2,1)S(1)}, bf16[1,200,8,128]{3,2,1,0:T(8,128)(2,1)}, u32[]{:S(2)}) copy-start(bf16[1,200,8,128]{3,2,1,0:T(8,128)(2,1)} %param.7) | copy-start | bytes 1228804
  130.3 35.3 %copy-start.11 = (f32[1024]{0:T(1024)S(1)}, f32[1024]{0:T(1024)}, u32[]{:S(2)}) copy-start(f32[1024]{0:T(1024)} %get-tuple-element.129) | copy-start | bytes 12292
  130.4 5.1 %collective-permute-start.6 = (f32[13,800]{1,0:T(8,128)S(1)}, f32[13,800]{1,0:T(8,128)S(1)}, u32[]{:S(2)}, u32[]{:S(2)}) collective-permute-start(f32[13,800]{1,0:T(8,128)S(1)} %reduce_sum.569), channel_id=1, source_target_pairs={{0,64},{64,0},{1,65},{65,1},{2,66},{66,2},{3,67},{67,3},{4,68},{68... | collective-permute-start | bytes 124808 | tf_op jit(solution)/shard_map/ppermute | solution.py:33
  156.3 11.8 %collective-permute-start.7 = (bf16[208,800]{1,0:T(8,128)(2,1)S(1)}, bf16[208,800]{1,0:T(8,128)(2,1)S(1)}, u32[]{:S(2)}, u32[]{:S(2)}) collective-permute-start(bf16[208,800]{1,0:T(8,128)(2,1)S(1)} %reshape.156), channel_id=1, source_target_pairs={{0,4},{4,0},{1,5},{5,1},{2,6},{6,2},{3,7},{7,3},{8,12},{12,8},{9,1... | collective-permute-start | bytes 998408 | tf_op jit(solution)/shard_map/ppermute | solution.py:33

commit v7 on v6

--- a/solution.py
+++ b/solution.py
@@ -39,7 +39,7 @@
 
 
 LON = ("lon_z", "lon_y", "lon_c")
-REDUCE_ORDER = (("lon_c", 0), ("lat", None), ("ens", None), ("lon_y", None), ("lon_z", 0))
+REDUCE_ORDER = (("lon_c", 0), ("lat", None), ("ens", None), ("lon_z", 0), ("lon_y", None))
 
 
 def spread(array, axis):

time: 172 us -> 171 us (level)
  no operation moved by 1% of the time
where the time goes in v7:
time: 171 us; the launch traced here: 170 us
  blocking collectives  68.5 us (40%)
  starting transfers between devices  39.3 us (23%)
  other arithmetic  25.6 us (15%)
  local copies, waits for them, and re-layouts  14.4 us (8%)
  waiting for transfers between devices  10.7 us (6%)
  matrix products  10.1 us (6%)
    all_to_all x3, blocking collectives, spread(): return lax.all_to_all(copies, axis, 0, 0, tiled=False)  36.9 us
    all_to_all x2, blocking collectives, tree_psum(): flat = lax.all_to_all(chunks, axis, 0, 0, tiled=False).sum(0)  31.6 us
    ppermute x3, starting transfers between devices, swapped(): lax.ppermute(array, axis, [(i, i ^ 1 << stride) for i in range(lax.axis_s...  16.2 us
    reduce_sum x4, other arithmetic, depthwise_grad(): columns.append(jnp.sum(d_conv * window, axis=(1, 2)))  11.9 us
    ppermute x2, starting transfers between devices, with_halo(): lax.ppermute(head, axis, [((i + 1) % count, i) for i in range(count)])  11 us
    reduce_sum x1, other arithmetic, cell_pass(): chan_mean = jnp.mean(conv_blk, axis=0, keepdims=True)  8.26 us
    ppermute x2, starting transfers between devices, with_halo(): lax.ppermute(tail, axis, [(i, (i + 1) % count) for i in range(count)])  6.52 us
    ppermute x1, starting transfers between devices, mirrored_across(): return lax.ppermute(array, axis, [(i, count - 1 - i) for i in range(count)])  5.6 us
  transfers between devices with their start and end apart: 8, of which 4 were waited for; matrix products, arithmetic and copies ran while one was open for 2% of the time, Pallas kernels for 0%

profile of v7, /device:TPU:1, one launch (start us, length us, event | category | flops | bytes accessed | tf_op | source)
XLA Modules:
  0.0 169.7 jit_solution(8039346553216421466)
XLA Ops:
  3.5 4.6 %collective-permute-start = (bf16[200,8,3]{0,2,1:T(4,128)(2,1)S(1)}, bf16[200,8,3]{0,2,1:T(4,128)(2,1)S(1)}, u32[]{:S(2)}, u32[]{:S(2)}) collective-permute-start(bf16[200,8,3]{0,2,1:T(4,128)(2,1)S(1)} %get-tuple-element.78), channel_id=1, source_target_pairs={{0,4},{4,8},{8,12},{12,16},{16,20},{20,24},{24,28},{28,32},{32,36}... | collective-permute-start | bytes 28808 | tf_op jit(solution)/shard_map/ppermute | solution.py:23
  8.1 6.1 %collective-permute-start.1 = (bf16[200,8,3]{0,2,1:T(4,128)(2,1)S(1)}, bf16[200,8,3]{0,2,1:T(4,128)(2,1)S(1)}, u32[]{:S(2)}, u32[]{:S(2)}) collective-permute-start(bf16[200,8,3]{0,2,1:T(4,128)(2,1)S(1)} %get-tuple-element.79), channel_id=1, source_target_pairs={{4,0},{8,4},{12,8},{16,12},{20,16},{24,20},{28,24},{32,28},{36,32}... | collective-permute-start | bytes 28808 | tf_op jit(solution)/shard_map/ppermute | solution.py:25
  15.2 1.9 %collective-permute-start.2 = (bf16[200,3,134]{0,2,1:T(8,128)(2,1)S(1)}, bf16[200,3,134]{0,2,1:T(8,128)(2,1)S(1)}, u32[]{:S(2)}, u32[]{:S(2)}) collective-permute-start(bf16[200,3,134]{0,2,1:T(8,128)(2,1)S(1)} %get-tuple-element.77), channel_id=1, source_target_pairs={{0,1},{1,2},{2,3},{3,0},{4,5},{5,6},{6,7},{7,4},{8,9},{9,10},{10,1... | collective-permute-start | bytes 482408 | tf_op jit(solution)/shard_map/ppermute | solution.py:23
  18.1 5.6 %collective-permute-start.3 = (bf16[200,3,134]{0,2,1:T(8,128)(2,1)S(1)}, bf16[200,3,134]{0,2,1:T(8,128)(2,1)S(1)}, u32[]{:S(2)}, u32[]{:S(2)}) collective-permute-start(bf16[200,3,134]{0,2,1:T(8,128)(2,1)S(1)} %rev.3), channel_id=1, source_target_pairs={{0,124},{4,120},{8,116},{12,112},{16,108},{20,104},{24,100},{28,96... | collective-permute-start | bytes 482408 | tf_op jit(solution)/shard_map/ppermute | solution.py:38
  23.7 4.9 %collective-permute-start.4 = (bf16[200,3,134]{0,2,1:T(8,128)(2,1)S(1)}, bf16[200,3,134]{0,2,1:T(8,128)(2,1)S(1)}, u32[]{:S(2)}, u32[]{:S(2)}) collective-permute-start(bf16[200,3,134]{0,2,1:T(8,128)(2,1)S(1)} %get-tuple-element.76), channel_id=1, source_target_pairs={{1,0},{2,1},{3,2},{0,3},{5,4},{6,5},{7,6},{4,7},{9,8},{10,9},{11,1... | collective-permute-start | bytes 482408 | tf_op jit(solution)/shard_map/ppermute | solution.py:25
  28.6 5.6 %collective-permute-done.3 = bf16[200,3,134]{0,2,1:T(8,128)(2,1)S(1)} collective-permute-done((bf16[200,3,134]{0,2,1:T(8,128)(2,1)S(1)}, bf16[200,3,134]{0,2,1:T(8,128)(2,1)S(1)}, u32[]{:S(2)}, u32[]{:S(2)}) %collective-permute-start.3) | collective-permute-done | bytes 160832 | tf_op jit(solution)/shard_map/ppermute | solution.py:38
  34.5 8.3 %fusion.120 = (f32[8,128]{1,0:T(8,128)S(1)}, f32[200,8,128]{0,2,1:T(8,128)S(1)}) fusion(bf16[200,11,134]{0,2,1:T(8,128)(2,1)S(1)} %get-tuple-element.75, f32[200]{0:T(256)S(1)} %bitcast.308, f32[200]{0:T(256)S(1)} %bitcast.309, f32[200]{0:T(256)S(1)} %bitcast.262, f32[200]{0:T(256)S(1)} %bitcast.263, f32[200]{0:T(256)S(1)} %bitcast.264, ...), kind=kLoop, calls=%fused_computation.261 | loop fusion | flops 33790976 | bytes 18494496 | tf_op jit(solution)/shard_map/reduce_sum | solution.py:114
  45.3 2.2 %fusion.9 = (bf16[800,1024]{1,0:T(8,128)(2,1)}, f32[1024,800]{0,1:T(8,128)S(1)}) fusion(bf16[200,800]{1,0:T(8,128)(2,1)S(1)} %copy-done, f32[200,1024]{1,0:T(8,128)S(1)} %copy.163, f32[200]{0:T(256)S(1)} %copy-done.9, f32[1024]{0:T(1024)S(1)} %rsqrt_bitcast_fusion, f32[1024]{0:T(1024)S(1)} %get-tuple-element.131), kind=kOutput, calls=%fused_computation.12 | convolution fusion | flops 332595200 | bytes 6063392 | tf_op jit(solution)/shard_map/dot_general | solution.py:120
  47.5 1.7 fusion.5
  49.2 1.7 %convolution_multiply_fusion.1 = f32[200,800]{1,0:T(8,128)} fusion(bf16[800,1024]{1,0:T(8,128)(2,1)S(1)} %fusion.5, f32[200,1024]{1,0:T(8,128)S(1)} %copy.163, f32[200]{0:T(256)S(1)} %copy-done.9, f32[1024]{0:T(1024)S(1)} %rsqrt_bitcast_fusion, f32[1024]{0:T(1024)S(1)} %get-tuple-element.131), kind=kOutput, calls=%fused_computation.114 | convolution fusion | flops 328659200 | bytes 3106592 | tf_op jit(solution)/shard_map/dot_general | solution.py:130
  55.0 3.8 %fusion.59 = (f32[200]{0:T(256)S(1)}, f32[200]{0:T(256)S(1)}, f32[200]{0:T(256)S(1)}, f32[200]{0:T(256)S(1)}, f32[200]{0:T(256)S(1)}, /*index=5*/f32[200]{0:T(25...) fusion(bf16[200,11,134]{0,2,1:T(8,128)(2,1)S(1)} %get-tuple-ele, ...), kind=kLoop, calls=%fused_computation.162 | loop fusion | flops 11055600 | bytes 8206400 | tf_op jit(solution)/shard_map/reduce_sum | solution.py:109
  58.8 3.8 %fusion.109 = (f32[200]{0:T(256)}, f32[200]{0:T(256)}, f32[200]{0:T(256)}, f32[200]{0:T(256)}, f32[200]{0:T(256)}, /*index=5*/f32[200]{0:T(256)}, f32[200]{0:T(2...) fusion(bf16[200,11,134]{0,2,1:T(8,128)(2,1)S(1)} %get-tuple-ele, ...), kind=kLoop, calls=%fused_computation.212 | loop fusion | flops 11055600 | bytes 8206400 | tf_op jit(solution)/shard_map/reduce_sum | solution.py:109
  64.8 3.0 %fusion.91 = (f32[200]{0:T(256)}, f32[200]{0:T(256)}, f32[200]{0:T(256)}, f32[200]{0:T(256)}, f32[200]{0:T(256)}, /*index=5*/f32[200]{0:T(256)}, f32[200]{0:T(25...) fusion(bf16[200,11,134]{0,2,1:T(8,128)(2,1)S(1)} %get-tuple-element.75, ...), kind=kLoop, calls=%fused_computation.194 | loop fusion | flops 11056800 | bytes 3715200 | tf_op jit(solution)/shard_map/reduce_sum | solution.py:109
  67.9 4.4 %stack.199 = f32[49,200]{1,0:T(8,128)S(1)} concatenate(f32[1,200]{1,0:T(1,128)} %bitcast.314, f32[1,200]{1,0:T(1,128)} %bitcast.315, f32[1,200]{1,0:T(1,128)} %bitcast.316, f32[1,200]{1,0:T(1,128)} %bitcast.242, f32[1,200]{1,0:T(1,128)} %bitcast.241, f32[1,200]{1,0:T(1,128)} %bitcast.240, f32[1,200]{1,0:T(1,128)} %bitcast.239, f32[1,200]{1,0:T(1,128)} %bitcast.238, ...), dimensions={0} | concatenate | bytes 78400 | tf_op jit(solution)/shard_map/stack | solution.py:110
  74.6 4.4 %collective-permute-start.5 = (f32[208,800]{1,0:T(8,128)S(1)}, f32[208,800]{1,0:T(8,128)S(1)}, u32[]{:S(2)}, u32[]{:S(2)}) collective-permute-start(f32[208,800]{1,0:T(8,128)S(1)} %fusion.111), channel_id=1, source_target_pairs={{0,4},{4,0},{1,5},{5,1},{2,6},{6,2},{3,7},{7,3},{8,12},{12,8},{9,1... | collective-permute-start | bytes 1996808 | tf_op jit(solution)/shard_map/ppermute | solution.py:33
  79.0 1.7 collective-permute-done.5
  80.9 16.4 %all_to_all.25 = f32[4,52,800]{2,1,0:T(8,128)S(1)} all-to-all(f32[4,52,800]{2,1,0:T(8,128)S(1)} %reshape.156), channel_id=1, replica_groups=mesh['ens'=4,'lon_z'=2,'lon_y'=8,'lon_c'=2,'lat'=4] {'lat'}, dimensions={0} | all-to-all | bytes 1331200 | tf_op jit(solution)/shard_map/all_to_all | solution.py:59
  97.4 15.2 %all_to_all.26 = f32[4,13,800]{2,1,0:T(8,128)S(1)} all-to-all(f32[4,13,800]{2,1,0:T(8,128)S(1)} %reshape.157), channel_id=1, replica_groups=mesh['ens'=4,'lon_z'=2,'lon_y'=8,'lon_c'=2,'lat'=4] {'ens'}, dimensions={0} | all-to-all | bytes 332800 | tf_op jit(solution)/shard_map/all_to_all | solution.py:59
  112.6 2.1 %collective-permute-start.6 = (f32[13,800]{1,0:T(8,128)S(1)}, f32[13,800]{1,0:T(8,128)S(1)}, u32[]{:S(2)}, u32[]{:S(2)}) collective-permute-start(f32[13,800]{1,0:T(8,128)S(1)} %reduce_sum.568), channel_id=1, source_target_pairs={{0,64},{64,0},{1,65},{65,1},{2,66},{66,2},{3,67},{67,3},{4,68},{68... | collective-permute-start | bytes 124808 | tf_op jit(solution)/shard_map/ppermute | solution.py:33
  114.7 2.8 %collective-permute-done.6 = f32[13,800]{1,0:T(8,128)S(1)} collective-permute-done((f32[13,800]{1,0:T(8,128)S(1)}, f32[13,800]{1,0:T(8,128)S(1)}, u32[]{:S(2)}, u32[]{:S(2)}) %collective-permute-start.6) | collective-permute-done | bytes 41632 | tf_op jit(solution)/shard_map/ppermute | solution.py:33
  117.6 17.2 %all_to_all.27 = f32[8,13,800]{2,1,0:T(8,128)S(1)} all-to-all(f32[8,13,800]{2,1,0:T(8,128)S(1)} %broadcast_in_dim.11), channel_id=1, replica_groups=mesh['ens'=4,'lon_z'=2,'lon_y'=8,'lon_c'=2,'lat'=4] {'lon_y'}, dimensions={0} | all-to-all | bytes 665600 | tf_op jit(solution)/shard_map/all_to_all | solution.py:48
  134.8 11.0 %all_to_all.28 = bf16[4,13,800]{2,1,0:T(8,128)(2,1)S(1)} all-to-all(bf16[4,13,800]{2,1,0:T(8,128)(2,1)S(1)} %broadcast_in_dim.12), channel_id=1, replica_groups=mesh['ens'=4,'lon_z'=2,'lon_y'=8,'lon_c'=2,'lat'=4] {'ens'}, dimensions={0} | all-to-all | bytes 166400 | tf_op jit(solution)/shard_map/all_to_all | solution.py:48
  145.9 8.7 %all_to_all.29 = bf16[4,52,800]{2,1,0:T(8,128)(2,1)S(1)} all-to-all(bf16[4,52,800]{2,1,0:T(8,128)(2,1)S(1)} %broadcast_in_dim.14), channel_id=1, replica_groups=mesh['ens'=4,'lon_z'=2,'lon_y'=8,'lon_c'=2,'lat'=4] {'lat'}, dimensions={0} | all-to-all | bytes 665600 | tf_op jit(solution)/shard_map/all_to_all | solution.py:48
  154.7 9.7 %collective-permute-start.7 = (bf16[208,800]{1,0:T(8,128)(2,1)S(1)}, bf16[208,800]{1,0:T(8,128)(2,1)S(1)}, u32[]{:S(2)}, u32[]{:S(2)}) collective-permute-start(bf16[208,800]{1,0:T(8,128)(2,1)S(1)} %reshape.158), channel_id=1, source_target_pairs={{0,4},{4,0},{1,5},{5,1},{2,6},{6,2},{3,7},{7,3},{8,12},{12,8},{9,1... | collective-permute-start | bytes 998408 | tf_op jit(solution)/shard_map/ppermute | solution.py:33
  (86 shorter events, 22.0 us)
Async XLA Ops:
  0.6 44.7 %copy-start = (bf16[200,800]{1,0:T(8,128)(2,1)S(1)}, bf16[200,800]{1,0:T(8,128)(2,1)}, u32[]{:S(2)}) copy-start(bf16[200,800]{1,0:T(8,128)(2,1)} %param.11) | copy-start | bytes 960004
  0.6 13.6 %copy-start.8 = (f32[200,49]{0,1:T(8,128)S(1)}, f32[200,49]{0,1:T(8,128)}, u32[]{:S(2)}) copy-start(f32[200,49]{0,1:T(8,128)} %param.9) | copy-start | bytes 117604
  3.5 10.8 %collective-permute-start = (bf16[200,8,3]{0,2,1:T(4,128)(2,1)S(1)}, bf16[200,8,3]{0,2,1:T(4,128)(2,1)S(1)}, u32[]{:S(2)}, u32[]{:S(2)}) collective-permute-start(bf16[200,8,3]{0,2,1:T(4,128)(2,1)S(1)} %get-tuple-element.78), channel_id=1, source_target_pairs={{0,4},{4,8},{8,12},{12,16},{16,20},{20,24},{24,28},{28,32},{32,36}... | collective-permute-start | bytes 28808 | tf_op jit(solution)/shard_map/ppermute | solution.py:23
  8.1 6.9 %collective-permute-start.1 = (bf16[200,8,3]{0,2,1:T(4,128)(2,1)S(1)}, bf16[200,8,3]{0,2,1:T(4,128)(2,1)S(1)}, u32[]{:S(2)}, u32[]{:S(2)}) collective-permute-start(bf16[200,8,3]{0,2,1:T(4,128)(2,1)S(1)} %get-tuple-element.79), channel_id=1, source_target_pairs={{4,0},{8,4},{12,8},{16,12},{20,16},{24,20},{28,24},{32,28},{36,32}... | collective-permute-start | bytes 28808 | tf_op jit(solution)/shard_map/ppermute | solution.py:25
  15.2 13.4 %collective-permute-start.2 = (bf16[200,3,134]{0,2,1:T(8,128)(2,1)S(1)}, bf16[200,3,134]{0,2,1:T(8,128)(2,1)S(1)}, u32[]{:S(2)}, u32[]{:S(2)}) collective-permute-start(bf16[200,3,134]{0,2,1:T(8,128)(2,1)S(1)} %get-tuple-element.77), channel_id=1, source_target_pairs={{0,1},{1,2},{2,3},{3,0},{4,5},{5,6},{6,7},{7,4},{8,9},{9,10},{10,1... | collective-permute-start | bytes 482408 | tf_op jit(solution)/shard_map/ppermute | solution.py:23
  18.1 16.1 %collective-permute-start.3 = (bf16[200,3,134]{0,2,1:T(8,128)(2,1)S(1)}, bf16[200,3,134]{0,2,1:T(8,128)(2,1)S(1)}, u32[]{:S(2)}, u32[]{:S(2)}) collective-permute-start(bf16[200,3,134]{0,2,1:T(8,128)(2,1)S(1)} %rev.3), channel_id=1, source_target_pairs={{0,124},{4,120},{8,116},{12,112},{16,108},{20,104},{24,100},{28,96... | collective-permute-start | bytes 482408 | tf_op jit(solution)/shard_map/ppermute | solution.py:38
  23.7 10.5 %collective-permute-start.4 = (bf16[200,3,134]{0,2,1:T(8,128)(2,1)S(1)}, bf16[200,3,134]{0,2,1:T(8,128)(2,1)S(1)}, u32[]{:S(2)}, u32[]{:S(2)}) collective-permute-start(bf16[200,3,134]{0,2,1:T(8,128)(2,1)S(1)} %get-tuple-element.76), channel_id=1, source_target_pairs={{1,0},{2,1},{3,2},{0,3},{5,4},{6,5},{7,6},{4,7},{9,8},{10,9},{11,1... | collective-permute-start | bytes 482408 | tf_op jit(solution)/shard_map/ppermute | solution.py:25
  42.8 1.0 copy-start.1
  42.8 2.5 %copy-start.9 = (f32[200]{0:T(256)S(1)}, f32[200]{0:T(256)}, u32[]{:S(2)}) copy-start(f32[200]{0:T(256)} %param.10) | copy-start | bytes 2404
  45.3 2.2 %copy-start.13 = (bf16[1,200,8,128]{3,2,1,0:T(8,128)(2,1)S(1)}, bf16[1,200,8,128]{3,2,1,0:T(8,128)(2,1)}, u32[]{:S(2)}) copy-start(bf16[1,200,8,128]{3,2,1,0:T(8,128)(2,1)} %param.13) | copy-start | bytes 1228804
  45.3 2.2 %copy-start.15 = (bf16[800,200]{0,1:T(8,128)(2,1)S(1)}, bf16[800,200]{0,1:T(8,128)(2,1)}, u32[]{:S(2)}) copy-start(bf16[800,200]{0,1:T(8,128)(2,1)} %param.12) | copy-start | bytes 960004
  50.9 1.4 copy-start.6
  58.8 3.8 %copy-start.4 = (bf16[800,1024]{1,0:T(8,128)(2,1)S(1)}, bf16[800,1024]{1,0:T(8,128)(2,1)}, u32[]{:S(2)}) copy-start(bf16[800,1024]{1,0:T(8,128)(2,1)} %get-tuple-element.133) | copy-start | bytes 4915204
  58.8 3.8 %copy-start.14 = (bf16[1,200,8,128]{3,2,1,0:T(8,128)(2,1)S(1)}, bf16[1,200,8,128]{3,2,1,0:T(8,128)(2,1)}, u32[]{:S(2)}) copy-start(bf16[1,200,8,128]{3,2,1,0:T(8,128)(2,1)} %param.13) | copy-start | bytes 1228804
  62.6 1.6 copy-start.12
  64.8 3.0 %copy-start.10 = (f32[200]{0:T(256)S(1)}, f32[200]{0:T(256)}, u32[]{:S(2)}) copy-start(f32[200]{0:T(256)} %get-tuple-element.38) | copy-start | bytes 2404
  67.8 12.8 %copy-start.2 = (f32[200,800]{1,0:T(8,128)S(1)}, f32[200,800]{1,0:T(8,128)}, u32[]{:S(2)}) copy-start(f32[200,800]{1,0:T(8,128)} %convolution_multiply_fusion.1) | copy-start | bytes 1920004
  67.8 12.8 %copy-start.3 = (f32[200,800]{1,0:T(8,128)S(1)}, f32[200,800]{1,0:T(8,128)}, u32[]{:S(2)}) copy-start(f32[200,800]{1,0:T(8,128)} %convolution_multiply_fusion) | copy-start | bytes 1920004
  74.6 6.0 %collective-permute-start.5 = (f32[208,800]{1,0:T(8,128)S(1)}, f32[208,800]{1,0:T(8,128)S(1)}, u32[]{:S(2)}, u32[]{:S(2)}) collective-permute-start(f32[208,800]{1,0:T(8,128)S(1)} %fusion.111), channel_id=1, source_target_pairs={{0,4},{4,0},{1,5},{5,1},{2,6},{6,2},{3,7},{7,3},{8,12},{12,8},{9,1... | collective-permute-start | bytes 1996808 | tf_op jit(solution)/shard_map/ppermute | solution.py:33
  112.6 4.9 %collective-permute-start.6 = (f32[13,800]{1,0:T(8,128)S(1)}, f32[13,800]{1,0:T(8,128)S(1)}, u32[]{:S(2)}, u32[]{:S(2)}) collective-permute-start(f32[13,800]{1,0:T(8,128)S(1)} %reduce_sum.568), channel_id=1, source_target_pairs={{0,64},{64,0},{1,65},{65,1},{2,66},{66,2},{3,67},{67,3},{4,68},{68... | collective-permute-start | bytes 124808 | tf_op jit(solution)/shard_map/ppermute | solution.py:33
  134.8 29.7 %copy-start.5 = (bf16[800,1024]{1,0:T(8,128)(2,1)S(1)}, bf16[800,1024]{1,0:T(8,128)(2,1)}, u32[]{:S(2)}) copy-start(bf16[800,1024]{1,0:T(8,128)(2,1)} %get-tuple-element.133) | copy-start | bytes 4915204
  134.8 29.7 %copy-start.7 = (bf16[1,200,8,128]{3,2,1,0:T(8,128)(2,1)S(1)}, bf16[1,200,8,128]{3,2,1,0:T(8,128)(2,1)}, u32[]{:S(2)}) copy-start(bf16[1,200,8,128]{3,2,1,0:T(8,128)(2,1)} %param.7) | copy-start | bytes 1228804
  134.8 29.7 %copy-start.11 = (f32[1024]{0:T(1024)S(1)}, f32[1024]{0:T(1024)}, u32[]{:S(2)}) copy-start(f32[1024]{0:T(1024)} %get-tuple-element.129) | copy-start | bytes 12292
  154.7 12.2 %collective-permute-start.7 = (bf16[208,800]{1,0:T(8,128)(2,1)S(1)}, bf16[208,800]{1,0:T(8,128)(2,1)S(1)}, u32[]{:S(2)}, u32[]{:S(2)}) collective-permute-start(bf16[208,800]{1,0:T(8,128)(2,1)S(1)} %reshape.158), channel_id=1, source_target_pairs={{0,4},{4,0},{1,5},{5,1},{2,6},{6,2},{3,7},{7,3},{8,12},{12,8},{9,1... | collective-permute-start | bytes 998408 | tf_op jit(solution)/shard_map/ppermute | solution.py:33

commit v8 on v7

--- a/solution.py
+++ b/solution.py
@@ -147,17 +147,16 @@
     margin = KS // 2
     mask_bf = ocean_mask.astype(jnp.bfloat16)
     masked = state_tile * mask_bf[None]
-    padded = with_halo(masked, ((LON, 2), ("lat", 1)), margin)
     lat_now = lax.axis_index("lat")
     lat_count = lax.axis_size("lat")
     lon_count = lax.axis_size(LON)
-    top_strip = padded[:, tile_rows : tile_rows + margin, :][:, ::-1, ::-1]
+    rows_out = with_halo(masked, (("lat", 1),), margin)
+    top_strip = masked[:, tile_rows - margin :, :][:, ::-1, ::-1]
     mirrored = mirrored_across(top_strip, LON)
-    north_rows = jnp.where(lat_now == lat_count - 1, mirrored, padded[:, tile_rows + margin :, :])
-    south_rows = jnp.where(lat_now == 0, jnp.zeros_like(top_strip), padded[:, :margin, :])
-    padded = jnp.concatenate(
-        [south_rows, padded[:, margin : tile_rows + margin, :], north_rows], axis=1
-    )
+    north_rows = jnp.where(lat_now == lat_count - 1, mirrored, rows_out[:, tile_rows + margin :, :])
+    south_rows = jnp.where(lat_now == 0, jnp.zeros_like(top_strip), rows_out[:, :margin, :])
+    padded = jnp.concatenate([south_rows, masked, north_rows], axis=1)
+    padded = with_halo(padded, ((LON, 2),), margin)
     conv_out = depthwise(padded, dw_weight, tile_rows, tile_cols)
     cell_count = tile_rows * tile_cols
     cot_masked = (cotangent[0] * mask_bf[None]).reshape(channels, cell_count)

time: 171 us -> 186 us (1.088)
  other arithmetic: 25.6 us -> 33 us
  local copies, waits for them, and re-layouts: 14.4 us -> 20.8 us
  starting transfers between devices: 39.3 us -> 35.7 us
  waiting for transfers between devices: 10.7 us -> 13.1 us
  blocking collectives: 68.5 us -> 70.6 us
    ppermute x2, starting transfers between devices: 11 us -> 5.96 us  [with_halo(): lax.ppermute(head, axis, [((i + 1) % count, i) for i in range(count)])]
    another operation x1, local copies, waits for them, and re-layouts: 4.45 us -> 0.17 us  [depthwise_grad(): return jnp.stack(columns, axis=0)]
    reduce_sum x1, other arithmetic: 8.26 us -> 12.1 us  [cell_pass(): chan_mean = jnp.mean(conv_blk, axis=0, keepdims=True)]
    reduce_sum x0 -> x2, local copies, waits for them, and re-layouts: none -> 3 us  [the longest x1 1.5 us: cell_pass(): chan_var = jnp.mean(centred * centred, axis=0, keepdims=True)]
    add x0 -> x1, local copies, waits for them, and re-layouts: none -> 2.57 us  [depthwise(): conv_sum = conv_sum + tap_weight * window]
    unnamed x34 -> x149, local copies, waits for them, and re-layouts: 2.71 us -> 5.09 us
    ppermute x1, starting transfers between devices: 5.6 us -> 7.75 us  [mirrored_across(): return lax.ppermute(array, axis, [(i, count - 1 - i) for i in range(count)])]
    ppermute x1, waiting for transfers between devices: 5.57 us -> 7.61 us  [mirrored_across(): return lax.ppermute(array, axis, [(i, count - 1 - i) for i in range(count)])]
  transfers between devices with their start and end apart: 8 -> 8, of which waited for: 4 -> 4; matrix products, arithmetic and copies ran while one was open for 2% -> 3% of each run, Pallas kernels for 0% -> 0%
where the time goes in v8:
time: 186 us; the launch traced here: 185 us
  blocking collectives  70.6 us (38%)
  starting transfers between devices  35.7 us (19%)
  other arithmetic  33 us (18%)
  local copies, waits for them, and re-layouts  20.8 us (11%)
  waiting for transfers between devices  13.1 us (7%)
  matrix products  9.8 us (5%)
  between operations  1.96 us (1%)
    all_to_all x3, blocking collectives, spread(): return lax.all_to_all(copies, axis, 0, 0, tiled=False)  38.7 us
    all_to_all x2, blocking collectives, tree_psum(): flat = lax.all_to_all(chunks, axis, 0, 0, tiled=False).sum(0)  31.9 us
    ppermute x3, starting transfers between devices, swapped(): lax.ppermute(array, axis, [(i, i ^ 1 << stride) for i in range(lax.axis_s...  16.2 us
    reduce_sum x1, other arithmetic, cell_pass(): chan_mean = jnp.mean(conv_blk, axis=0, keepdims=True)  12.1 us
    reduce_sum x4, other arithmetic, depthwise_grad(): columns.append(jnp.sum(d_conv * window, axis=(1, 2)))  11.8 us
    ppermute x1, starting transfers between devices, mirrored_across(): return lax.ppermute(array, axis, [(i, count - 1 - i) for i in range(count)])  7.75 us
    ppermute x1, waiting for transfers between devices, mirrored_across(): return lax.ppermute(array, axis, [(i, count - 1 - i) for i in range(count)])  7.61 us
    ppermute x2, starting transfers between devices, with_halo(): lax.ppermute(head, axis, [((i + 1) % count, i) for i in range(count)])  5.96 us
  transfers between devices with their start and end apart: 8, of which 4 were waited for; matrix products, arithmetic and copies ran while one was open for 3% of the time, Pallas kernels for 0%

profile of v8, /device:TPU:1, one launch (start us, length us, event | category | flops | bytes accessed | tf_op | source)
XLA Modules:
  0.0 185.0 jit_solution(15820981095210591411)
XLA Ops:
  4.5 3.9 %collective-permute-start = (bf16[200,3,128]{0,1,2:T(4,128)(2,1)S(1)}, bf16[200,3,128]{0,1,2:T(4,128)(2,1)S(1)}, u32[]{:S(2)}, u32[]{:S(2)}) collective-permute-start(bf16[200,3,128]{0,1,2:T(4,128)(2,1)S(1)} %get-tuple-element.76), channel_id=1, source_target_pairs={{0,1},{1,2},{2,3},{3,0},{4,5},{5,6},{6,7},{7,4},{8,9},{9,10},{10,1... | collective-permute-start | bytes 460808 | tf_op jit(solution)/shard_map/ppermute | solution.py:23
  9.1 7.7 %collective-permute-start.1 = (bf16[200,3,128]{0,1,2:T(4,128)(2,1)S(1)}, bf16[200,3,128]{0,1,2:T(4,128)(2,1)S(1)}, u32[]{:S(2)}, u32[]{:S(2)}) collective-permute-start(bf16[200,3,128]{0,1,2:T(4,128)(2,1)S(1)} %rev.3), channel_id=1, source_target_pairs={{0,124},{4,120},{8,116},{12,112},{16,108},{20,104},{24,100},{28,96... | collective-permute-start | bytes 460808 | tf_op jit(solution)/shard_map/ppermute | solution.py:38
  16.8 3.4 %collective-permute-start.2 = (bf16[200,3,128]{0,1,2:T(4,128)(2,1)S(1)}, bf16[200,3,128]{0,1,2:T(4,128)(2,1)S(1)}, u32[]{:S(2)}, u32[]{:S(2)}) collective-permute-start(bf16[200,3,128]{0,1,2:T(4,128)(2,1)S(1)} %get-tuple-element.75), channel_id=1, source_target_pairs={{1,0},{2,1},{3,2},{0,3},{5,4},{6,5},{7,6},{4,7},{9,8},{10,9},{11,1... | collective-permute-start | bytes 460808 | tf_op jit(solution)/shard_map/ppermute | solution.py:25
  21.7 7.6 %collective-permute-done.1 = bf16[200,3,128]{0,1,2:T(4,128)(2,1)S(1)} collective-permute-done((bf16[200,3,128]{0,1,2:T(4,128)(2,1)S(1)}, bf16[200,3,128]{0,1,2:T(4,128)(2,1)S(1)}, u32[]{:S(2)}, u32[]{:S(2)}) %collective-permute-start.1) | collective-permute-done | bytes 153632 | tf_op jit(solution)/shard_map/ppermute | solution.py:38
  29.5 1.9 %collective-permute-start.3 = (bf16[200,14,3]{0,1,2:T(8,128)(2,1)S(1)}, bf16[200,14,3]{0,1,2:T(8,128)(2,1)S(1)}, u32[]{:S(2)}, u32[]{:S(2)}) collective-permute-start(bf16[200,14,3]{0,1,2:T(8,128)(2,1)S(1)} %get-tuple-element.73), channel_id=1, source_target_pairs={{0,4},{4,8},{8,12},{12,16},{16,20},{20,24},{24,28},{28,32},{32,36}... | collective-permute-start | bytes 50408 | tf_op jit(solution)/shard_map/ppermute | solution.py:23
  31.4 2.6 %collective-permute-start.4 = (bf16[200,14,3]{0,1,2:T(8,128)(2,1)S(1)}, bf16[200,14,3]{0,1,2:T(8,128)(2,1)}, u32[]{:S(2)}, u32[]{:S(2)}) collective-permute-start(bf16[200,14,3]{0,1,2:T(8,128)(2,1)S(1)} %get-tuple-element.74), channel_id=1, source_target_pairs={{4,0},{8,4},{12,8},{16,12},{20,16},{24,20},{28,24},{32,28},{36,32}... | collective-permute-start | bytes 50408 | tf_op jit(solution)/shard_map/ppermute | solution.py:25
  38.7 12.1 %fusion.122 = (f32[8,128]{0,1:T(8,128)}, f32[200,8,128]{0,1,2:T(8,128)}) fusion(bf16[200,14,131]{0,1,2:T(8,128)(2,1)S(1)} %get-tuple-element.72, f32[200]{0:T(256)} %bitcast.298, f32[200]{0:T(256)} %bitcast.299, f32[200]{0:T(256)S(1)} %bitcast.252, bf16[200,3,128]{0,1,2:T(4,128)(2,1)S(1)} %broadcast_select_fusion, ...), kind=kLoop, calls=%fused_computation.267 | loop fusion | flops 33790976 | bytes 18782496 | tf_op jit(solution)/shard_map/reduce_sum | solution.py:114
  54.9 2.6 %copy.277 = f32[200,8,128]{2,1,0:T(8,128)} copy(f32[200,8,128]{0,1,2:T(8,128)} %get-tuple-element.67) | data formatting | bytes 1638400 | tf_op jit(solution)/shard_map/add | solution.py:98
  57.5 2.2 %multiply_reduce_fusion = f32[8,128]{0,1:T(8,128)} fusion(f32[200,8,128]{0,1,2:T(8,128)} %get-tuple-element.67, f32[8,128]{0,1:T(8,128)} %copy.279), kind=kLoop, calls=%fused_computation.223 | loop fusion | flops 613376 | bytes 827392 | tf_op jit(solution)/shard_map/reduce_sum | solution.py:116
  61.9 3.3 %fusion.9 = (bf16[800,1024]{1,0:T(8,128)(2,1)}, f32[1024,800]{0,1:T(8,128)S(1)}) fusion(bf16[200,800]{1,0:T(8,128)(2,1)S(1)} %copy-done, f32[200]{0:T(256)} %param.10, f32[1024]{0:T(1024)S(1)} %rsqrt_bitcast_fusion, f32[1024]{0:T(1024)} %get-tuple-element.128, f32[25,8,8,128]{3,2,1,0:T(8,128)} %bitcast.191), kind=kOutput, calls=%fused_computation.12 | convolution fusion | flops 332595200 | bytes 6063392 | tf_op jit(solution)/shard_map/dot_general | solution.py:120
  72.0 2.5 %copy.281 = f32[200,8,128]{0,1,2:T(8,128)} copy(f32[200,8,128]{2,1,0:T(8,128)} %bitcast.195) | data formatting | bytes 1638400 | tf_op jit(solution)/shard_map/reshape | solution.py:173
  74.5 4.4 %fusion.106 = (f32[200]{0:T(256)}, f32[200]{0:T(256)}, f32[200]{0:T(256)}, f32[200]{0:T(256)}, f32[200]{0:T(256)}, /*index=5*/f32[200]{0:T(256)}, f32[200]{0:T(2...) fusion(f32[200,8,128]{0,1,2:T(8,128)} %copy.281, ...), kind=kLoop, calls=%fused_computation.219 | loop fusion | flops 11056800 | bytes 4003200 | tf_op jit(solution)/shard_map/reduce_sum | solution.py:109
  79.0 3.1 %fusion.105 = (f32[200]{0:T(256)S(1)}, f32[200]{0:T(256)S(1)}, f32[200]{0:T(256)S(1)}, f32[200]{0:T(256)S(1)}, f32[200]{0:T(256)S(1)}, /*index=5*/f32[200]{0:T(2...) fusion(f32[200,8,128]{0,1,2:T(8,128)S(1)} %copy-done.1, ...), kind=kLoop, calls=%fused_computation.218 | loop fusion | flops 11055600 | bytes 8206400 | tf_op jit(solution)/shard_map/reduce_sum | solution.py:109
  82.1 3.1 %fusion.109 = (f32[200]{0:T(256)S(1)}, f32[200]{0:T(256)S(1)}, f32[200]{0:T(256)S(1)}, f32[200]{0:T(256)S(1)}, f32[200]{0:T(256)S(1)}, /*index=5*/f32[200]{0:T(2...) fusion(f32[200,8,128]{0,1,2:T(8,128)S(1)} %copy-done.1, ...), kind=kLoop, calls=%fused_computation.222 | loop fusion | flops 11055600 | bytes 8206400 | tf_op jit(solution)/shard_map/reduce_sum | solution.py:109
  86.9 4.5 %collective-permute-start.5 = (f32[208,800]{1,0:T(8,128)S(1)}, f32[208,800]{1,0:T(8,128)S(1)}, u32[]{:S(2)}, u32[]{:S(2)}) collective-permute-start(f32[208,800]{1,0:T(8,128)S(1)} %fusion.112), channel_id=1, source_target_pairs={{0,4},{4,0},{1,5},{5,1},{2,6},{6,2},{3,7},{7,3},{8,12},{12,8},{9,1... | collective-permute-start | bytes 1996808 | tf_op jit(solution)/shard_map/ppermute | solution.py:33
  91.5 1.8 collective-permute-done.5
  93.5 14.4 %all_to_all.25 = f32[4,52,800]{2,1,0:T(8,128)S(1)} all-to-all(f32[4,52,800]{2,1,0:T(8,128)S(1)} %reshape.156), channel_id=1, replica_groups=mesh['ens'=4,'lon_z'=2,'lon_y'=8,'lon_c'=2,'lat'=4] {'lat'}, dimensions={0} | all-to-all | bytes 1331200 | tf_op jit(solution)/shard_map/all_to_all | solution.py:59
  108.0 17.5 %all_to_all.26 = f32[4,13,800]{2,1,0:T(8,128)S(1)} all-to-all(f32[4,13,800]{2,1,0:T(8,128)S(1)} %reshape.157), channel_id=1, replica_groups=mesh['ens'=4,'lon_z'=2,'lon_y'=8,'lon_c'=2,'lat'=4] {'ens'}, dimensions={0} | all-to-all | bytes 332800 | tf_op jit(solution)/shard_map/all_to_all | solution.py:59
  125.6 2.4 %collective-permute-start.6 = (f32[13,800]{1,0:T(8,128)S(1)}, f32[13,800]{1,0:T(8,128)S(1)}, u32[]{:S(2)}, u32[]{:S(2)}) collective-permute-start(f32[13,800]{1,0:T(8,128)S(1)} %reduce_sum.568), channel_id=1, source_target_pairs={{0,64},{64,0},{1,65},{65,1},{2,66},{66,2},{3,67},{67,3},{4,68},{68... | collective-permute-start | bytes 124808 | tf_op jit(solution)/shard_map/ppermute | solution.py:33
  128.0 2.5 %collective-permute-done.6 = f32[13,800]{1,0:T(8,128)S(1)} collective-permute-done((f32[13,800]{1,0:T(8,128)S(1)}, f32[13,800]{1,0:T(8,128)S(1)}, u32[]{:S(2)}, u32[]{:S(2)}) %collective-permute-start.6) | collective-permute-done | bytes 41632 | tf_op jit(solution)/shard_map/ppermute | solution.py:33
  130.6 17.9 %all_to_all.27 = f32[8,13,800]{2,1,0:T(8,128)S(1)} all-to-all(f32[8,13,800]{2,1,0:T(8,128)S(1)} %broadcast_in_dim.11), channel_id=1, replica_groups=mesh['ens'=4,'lon_z'=2,'lon_y'=8,'lon_c'=2,'lat'=4] {'lon_y'}, dimensions={0} | all-to-all | bytes 665600 | tf_op jit(solution)/shard_map/all_to_all | solution.py:48
  148.5 12.1 %all_to_all.28 = bf16[4,13,800]{2,1,0:T(8,128)(2,1)S(1)} all-to-all(bf16[4,13,800]{2,1,0:T(8,128)(2,1)S(1)} %broadcast_in_dim.12), channel_id=1, replica_groups=mesh['ens'=4,'lon_z'=2,'lon_y'=8,'lon_c'=2,'lat'=4] {'ens'}, dimensions={0} | all-to-all | bytes 166400 | tf_op jit(solution)/shard_map/all_to_all | solution.py:48
  160.7 8.7 %all_to_all.29 = bf16[4,52,800]{2,1,0:T(8,128)(2,1)S(1)} all-to-all(bf16[4,52,800]{2,1,0:T(8,128)(2,1)S(1)} %broadcast_in_dim.14), channel_id=1, replica_groups=mesh['ens'=4,'lon_z'=2,'lon_y'=8,'lon_c'=2,'lat'=4] {'lat'}, dimensions={0} | all-to-all | bytes 665600 | tf_op jit(solution)/shard_map/all_to_all | solution.py:48
  169.5 9.2 %collective-permute-start.7 = (bf16[208,800]{1,0:T(8,128)(2,1)S(1)}, bf16[208,800]{1,0:T(8,128)(2,1)S(1)}, u32[]{:S(2)}, u32[]{:S(2)}) collective-permute-start(bf16[208,800]{1,0:T(8,128)(2,1)S(1)} %reshape.158), channel_id=1, source_target_pairs={{0,4},{4,0},{1,5},{5,1},{2,6},{6,2},{3,7},{7,3},{8,12},{12,8},{9,1... | collective-permute-start | bytes 998408 | tf_op jit(solution)/shard_map/ppermute | solution.py:33
  (205 shorter events, 31.4 us)
Async XLA Ops:
  0.6 61.3 %copy-start = (bf16[200,800]{1,0:T(8,128)(2,1)S(1)}, bf16[200,800]{1,0:T(8,128)(2,1)}, u32[]{:S(2)}) copy-start(bf16[200,800]{1,0:T(8,128)(2,1)} %param.11) | copy-start | bytes 960004
  2.6 17.6 %copy-start.10 = (f32[200,49]{0,1:T(8,128)S(1)}, f32[200,49]{0,1:T(8,128)}, u32[]{:S(2)}) copy-start(f32[200,49]{0,1:T(8,128)} %param.9) | copy-start | bytes 117604
  4.5 17.0 %collective-permute-start = (bf16[200,3,128]{0,1,2:T(4,128)(2,1)S(1)}, bf16[200,3,128]{0,1,2:T(4,128)(2,1)S(1)}, u32[]{:S(2)}, u32[]{:S(2)}) collective-permute-start(bf16[200,3,128]{0,1,2:T(4,128)(2,1)S(1)} %get-tuple-element.76), channel_id=1, source_target_pairs={{0,1},{1,2},{2,3},{3,0},{4,5},{5,6},{6,7},{7,4},{8,9},{9,10},{10,1... | collective-permute-start | bytes 460808 | tf_op jit(solution)/shard_map/ppermute | solution.py:23
  9.1 20.2 %collective-permute-start.1 = (bf16[200,3,128]{0,1,2:T(4,128)(2,1)S(1)}, bf16[200,3,128]{0,1,2:T(4,128)(2,1)S(1)}, u32[]{:S(2)}, u32[]{:S(2)}) collective-permute-start(bf16[200,3,128]{0,1,2:T(4,128)(2,1)S(1)} %rev.3), channel_id=1, source_target_pairs={{0,124},{4,120},{8,116},{12,112},{16,108},{20,104},{24,100},{28,96... | collective-permute-start | bytes 460808 | tf_op jit(solution)/shard_map/ppermute | solution.py:38
  16.8 12.5 %collective-permute-start.2 = (bf16[200,3,128]{0,1,2:T(4,128)(2,1)S(1)}, bf16[200,3,128]{0,1,2:T(4,128)(2,1)S(1)}, u32[]{:S(2)}, u32[]{:S(2)}) collective-permute-start(bf16[200,3,128]{0,1,2:T(4,128)(2,1)S(1)} %get-tuple-element.75), channel_id=1, source_target_pairs={{1,0},{2,1},{3,2},{0,3},{5,4},{6,5},{7,6},{4,7},{9,8},{10,9},{11,1... | collective-permute-start | bytes 460808 | tf_op jit(solution)/shard_map/ppermute | solution.py:25
  29.5 5.5 %collective-permute-start.3 = (bf16[200,14,3]{0,1,2:T(8,128)(2,1)S(1)}, bf16[200,14,3]{0,1,2:T(8,128)(2,1)S(1)}, u32[]{:S(2)}, u32[]{:S(2)}) collective-permute-start(bf16[200,14,3]{0,1,2:T(8,128)(2,1)S(1)} %get-tuple-element.73), channel_id=1, source_target_pairs={{0,4},{4,8},{8,12},{12,16},{16,20},{20,24},{24,28},{28,32},{32,36}... | collective-permute-start | bytes 50408 | tf_op jit(solution)/shard_map/ppermute | solution.py:23
  31.4 5.4 %collective-permute-start.4 = (bf16[200,14,3]{0,1,2:T(8,128)(2,1)S(1)}, bf16[200,14,3]{0,1,2:T(8,128)(2,1)}, u32[]{:S(2)}, u32[]{:S(2)}) collective-permute-start(bf16[200,14,3]{0,1,2:T(8,128)(2,1)S(1)} %get-tuple-element.74), channel_id=1, source_target_pairs={{4,0},{8,4},{12,8},{16,12},{20,16},{24,20},{28,24},{32,28},{36,32}... | collective-permute-start | bytes 50408 | tf_op jit(solution)/shard_map/ppermute | solution.py:25
  34.6 3.7 %copy-start.30 = (f32[200,1]{0,1:T(1,128)S(1)}, f32[200,1]{0,1:T(1,128)}, u32[]{:S(2)}) copy-start(f32[200,1]{0,1:T(1,128)} %get-tuple-element.78) | copy-start | bytes 2404
  34.7 3.7 %copy-start.31 = (f32[200,1]{0,1:T(1,128)S(1)}, f32[200,1]{0,1:T(1,128)}, u32[]{:S(2)}) copy-start(f32[200,1]{0,1:T(1,128)} %get-tuple-element.79) | copy-start | bytes 2404
  34.7 3.7 %copy-start.32 = (f32[200,1]{0,1:T(1,128)S(1)}, f32[200,1]{0,1:T(1,128)}, u32[]{:S(2)}) copy-start(f32[200,1]{0,1:T(1,128)} %get-tuple-element.80) | copy-start | bytes 2404
  34.7 3.7 %copy-start.33 = (f32[200,1]{0,1:T(1,128)S(1)}, f32[200,1]{0,1:T(1,128)}, u32[]{:S(2)}) copy-start(f32[200,1]{0,1:T(1,128)} %get-tuple-element.81) | copy-start | bytes 2404
  34.7 3.7 %copy-start.34 = (f32[200,1]{0,1:T(1,128)S(1)}, f32[200,1]{0,1:T(1,128)}, u32[]{:S(2)}) copy-start(f32[200,1]{0,1:T(1,128)} %get-tuple-element.82) | copy-start | bytes 2404
  34.7 3.7 %copy-start.35 = (f32[200,1]{0,1:T(1,128)S(1)}, f32[200,1]{0,1:T(1,128)}, u32[]{:S(2)}) copy-start(f32[200,1]{0,1:T(1,128)} %get-tuple-element.83) | copy-start | bytes 2404
  34.7 3.7 %copy-start.36 = (f32[200,1]{0,1:T(1,128)S(1)}, f32[200,1]{0,1:T(1,128)}, u32[]{:S(2)}) copy-start(f32[200,1]{0,1:T(1,128)} %get-tuple-element.84) | copy-start | bytes 2404
  34.7 3.7 %copy-start.37 = (f32[200,1]{0,1:T(1,128)S(1)}, f32[200,1]{0,1:T(1,128)}, u32[]{:S(2)}) copy-start(f32[200,1]{0,1:T(1,128)} %get-tuple-element.85) | copy-start | bytes 2404
  34.7 3.7 %copy-start.38 = (f32[200,1]{0,1:T(1,128)S(1)}, f32[200,1]{0,1:T(1,128)}, u32[]{:S(2)}) copy-start(f32[200,1]{0,1:T(1,128)} %get-tuple-element.86) | copy-start | bytes 2404
  74.5 4.4 %copy-start.1 = (f32[200,8,128]{0,1,2:T(8,128)S(1)}, f32[200,8,128]{0,1,2:T(8,128)}, u32[]{:S(2)}) copy-start(f32[200,8,128]{0,1,2:T(8,128)} %copy.281) | copy-start | bytes 2457604
  86.9 6.4 %collective-permute-start.5 = (f32[208,800]{1,0:T(8,128)S(1)}, f32[208,800]{1,0:T(8,128)S(1)}, u32[]{:S(2)}, u32[]{:S(2)}) collective-permute-start(f32[208,800]{1,0:T(8,128)S(1)} %fusion.112), channel_id=1, source_target_pairs={{0,4},{4,0},{1,5},{5,1},{2,6},{6,2},{3,7},{7,3},{8,12},{12,8},{9,1... | collective-permute-start | bytes 1996808 | tf_op jit(solution)/shard_map/ppermute | solution.py:33
  125.6 4.9 %collective-permute-start.6 = (f32[13,800]{1,0:T(8,128)S(1)}, f32[13,800]{1,0:T(8,128)S(1)}, u32[]{:S(2)}, u32[]{:S(2)}) collective-permute-start(f32[13,800]{1,0:T(8,128)S(1)} %reduce_sum.568), channel_id=1, source_target_pairs={{0,64},{64,0},{1,65},{65,1},{2,66},{66,2},{3,67},{67,3},{4,68},{68... | collective-permute-start | bytes 124808 | tf_op jit(solution)/shard_map/ppermute | solution.py:33
  148.4 30.2 %copy-start.5 = (bf16[800,1024]{1,0:T(8,128)(2,1)S(1)}, bf16[800,1024]{1,0:T(8,128)(2,1)}, u32[]{:S(2)}) copy-start(bf16[800,1024]{1,0:T(8,128)(2,1)} %get-tuple-element.130) | copy-start | bytes 4915204
  148.5 30.2 %copy-start.7 = (bf16[1,200,8,128]{3,2,1,0:T(8,128)(2,1)S(1)}, bf16[1,200,8,128]{3,2,1,0:T(8,128)(2,1)}, u32[]{:S(2)}) copy-start(bf16[1,200,8,128]{3,2,1,0:T(8,128)(2,1)} %param.7) | copy-start | bytes 1228804
  148.5 30.2 %copy-start.69 = (f32[1024]{0:T(1024)S(1)}, f32[1024]{0:T(1024)}, u32[]{:S(2)}) copy-start(f32[1024]{0:T(1024)} %get-tuple-element.126) | copy-start | bytes 12292
  169.5 11.7 %copy-start.8 = (bf16[208,800]{1,0:T(8,128)(2,1)}, bf16[208,800]{1,0:T(8,128)(2,1)S(1)}, u32[]{:S(2)}) copy-start(bf16[208,800]{1,0:T(8,128)(2,1)S(1)} %reshape.158) | copy-start | bytes 998404
  169.5 11.6 %collective-permute-start.7 = (bf16[208,800]{1,0:T(8,128)(2,1)S(1)}, bf16[208,800]{1,0:T(8,128)(2,1)S(1)}, u32[]{:S(2)}, u32[]{:S(2)}) collective-permute-start(bf16[208,800]{1,0:T(8,128)(2,1)S(1)} %reshape.158), channel_id=1, source_target_pairs={{0,4},{4,0},{1,5},{5,1},{2,6},{6,2},{3,7},{7,3},{8,12},{12,8},{9,1... | collective-permute-start | bytes 998408 | tf_op jit(solution)/shard_map/ppermute | solution.py:33
  (57 other events, 152.2 us)

commit v9 on v7

--- a/solution.py
+++ b/solution.py
@@ -84,7 +84,7 @@
         flat = jnp.where(
             upper == 0, jnp.concatenate([flat, other]), jnp.concatenate([other, flat])
         )
-    return flat.astype(jnp.float32)
+    return flat
 
 
 def depthwise(padded, dw_weight, out_rows, out_cols):
@@ -185,11 +185,11 @@
     small = jnp.pad(small, (0, small_rows * width - small.shape[0])).reshape(small_rows, width)
     packed = jnp.concatenate([grad_expand, grad_reduce.T, small], axis=0)
     packed = tree_psum(packed, REDUCE_ORDER, jnp.bfloat16)
-    grad_expand = packed[:channels]
-    grad_reduce = packed[channels : 2 * channels].T
+    grad_expand = packed[:channels].astype(jnp.float32)
+    grad_reduce = packed[channels : 2 * channels].T.astype(jnp.float32)
     small = packed[2 * channels :].reshape(-1)[: channels * (KS * KS + 1)].reshape(-1, channels)
-    grad_depthwise = small[: KS * KS].T
-    grad_gain = small[KS * KS]
+    grad_depthwise = small[: KS * KS].T.astype(jnp.float32)
+    grad_gain = small[KS * KS].astype(jnp.float32)
     next_state = out_flat.reshape(channels, tile_rows, tile_cols)[None]
     return (next_state, grad_depthwise, grad_gain, grad_expand, grad_reduce)
 

time: 171 us -> 171 us (level)
  other arithmetic: 25.6 us -> 28.1 us
  local copies, waits for them, and re-layouts: 14.4 us -> 12 us
    convert_element_type x1 -> x3, other arithmetic: 0.18 us -> 2.45 us  [the longest x1 1.19 us: body(): grad_reduce = packed[channels:2 * channels].T.astype(jnp.float32)]
    transpose x2 -> x0, local copies, waits for them, and re-layouts: 1.81 us -> none  [the longest x1 1.19 us: body(): grad_reduce = packed[channels:2 * channels].T]
where the time goes in v9:
time: 171 us; the launch traced here: 170 us
  blocking collectives  68.5 us (40%)
  starting transfers between devices  39.3 us (23%)
  other arithmetic  28.1 us (16%)
  local copies, waits for them, and re-layouts  12 us (7%)
  waiting for transfers between devices  10.7 us (6%)
  matrix products  10.1 us (6%)
    all_to_all x3, blocking collectives, spread(): return lax.all_to_all(copies, axis, 0, 0, tiled=False)  36.9 us
    all_to_all x2, blocking collectives, tree_psum(): flat = lax.all_to_all(chunks, axis, 0, 0, tiled=False).sum(0)  31.6 us
    ppermute x3, starting transfers between devices, swapped(): lax.ppermute(array, axis, [(i, i ^ 1 << stride) for i in range(lax.axis_s...  16.2 us
    reduce_sum x4, other arithmetic, depthwise_grad(): columns.append(jnp.sum(d_conv * window, axis=(1, 2)))  11.9 us
    ppermute x2, starting transfers between devices, with_halo(): lax.ppermute(head, axis, [((i + 1) % count, i) for i in range(count)])  11 us
    reduce_sum x1, other arithmetic, cell_pass(): chan_mean = jnp.mean(conv_blk, axis=0, keepdims=True)  8.26 us
    ppermute x2, starting transfers between devices, with_halo(): lax.ppermute(tail, axis, [(i, (i + 1) % count) for i in range(count)])  6.52 us
    ppermute x1, starting transfers between devices, mirrored_across(): return lax.ppermute(array, axis, [(i, count - 1 - i) for i in range(count)])  5.6 us
  transfers between devices with their start and end apart: 8, of which 4 were waited for; matrix products, arithmetic and copies ran while one was open for 2% of the time, Pallas kernels for 0%

profile of v9, /device:TPU:1, one launch (start us, length us, event | category | flops | bytes accessed | tf_op | source)
XLA Modules:
  0.0 169.8 jit_solution(1694632799917909196)
XLA Ops:
  3.5 4.6 %collective-permute-start = (bf16[200,8,3]{0,2,1:T(4,128)(2,1)S(1)}, bf16[200,8,3]{0,2,1:T(4,128)(2,1)S(1)}, u32[]{:S(2)}, u32[]{:S(2)}) collective-permute-start(bf16[200,8,3]{0,2,1:T(4,128)(2,1)S(1)} %get-tuple-element.78), channel_id=1, source_target_pairs={{0,4},{4,8},{8,12},{12,16},{16,20},{20,24},{24,28},{28,32},{32,36}... | collective-permute-start | bytes 28808 | tf_op jit(solution)/shard_map/ppermute | solution.py:23
  8.1 6.1 %collective-permute-start.1 = (bf16[200,8,3]{0,2,1:T(4,128)(2,1)S(1)}, bf16[200,8,3]{0,2,1:T(4,128)(2,1)S(1)}, u32[]{:S(2)}, u32[]{:S(2)}) collective-permute-start(bf16[200,8,3]{0,2,1:T(4,128)(2,1)S(1)} %get-tuple-element.79), channel_id=1, source_target_pairs={{4,0},{8,4},{12,8},{16,12},{20,16},{24,20},{28,24},{32,28},{36,32}... | collective-permute-start | bytes 28808 | tf_op jit(solution)/shard_map/ppermute | solution.py:25
  15.2 1.9 %collective-permute-start.2 = (bf16[200,3,134]{0,2,1:T(8,128)(2,1)S(1)}, bf16[200,3,134]{0,2,1:T(8,128)(2,1)S(1)}, u32[]{:S(2)}, u32[]{:S(2)}) collective-permute-start(bf16[200,3,134]{0,2,1:T(8,128)(2,1)S(1)} %get-tuple-element.77), channel_id=1, source_target_pairs={{0,1},{1,2},{2,3},{3,0},{4,5},{5,6},{6,7},{7,4},{8,9},{9,10},{10,1... | collective-permute-start | bytes 482408 | tf_op jit(solution)/shard_map/ppermute | solution.py:23
  18.1 5.6 %collective-permute-start.3 = (bf16[200,3,134]{0,2,1:T(8,128)(2,1)S(1)}, bf16[200,3,134]{0,2,1:T(8,128)(2,1)S(1)}, u32[]{:S(2)}, u32[]{:S(2)}) collective-permute-start(bf16[200,3,134]{0,2,1:T(8,128)(2,1)S(1)} %rev.3), channel_id=1, source_target_pairs={{0,124},{4,120},{8,116},{12,112},{16,108},{20,104},{24,100},{28,96... | collective-permute-start | bytes 482408 | tf_op jit(solution)/shard_map/ppermute | solution.py:38
  23.7 4.9 %collective-permute-start.4 = (bf16[200,3,134]{0,2,1:T(8,128)(2,1)S(1)}, bf16[200,3,134]{0,2,1:T(8,128)(2,1)S(1)}, u32[]{:S(2)}, u32[]{:S(2)}) collective-permute-start(bf16[200,3,134]{0,2,1:T(8,128)(2,1)S(1)} %get-tuple-element.76), channel_id=1, source_target_pairs={{1,0},{2,1},{3,2},{0,3},{5,4},{6,5},{7,6},{4,7},{9,8},{10,9},{11,1... | collective-permute-start | bytes 482408 | tf_op jit(solution)/shard_map/ppermute | solution.py:25
  28.6 5.6 %collective-permute-done.3 = bf16[200,3,134]{0,2,1:T(8,128)(2,1)S(1)} collective-permute-done((bf16[200,3,134]{0,2,1:T(8,128)(2,1)S(1)}, bf16[200,3,134]{0,2,1:T(8,128)(2,1)S(1)}, u32[]{:S(2)}, u32[]{:S(2)}) %collective-permute-start.3) | collective-permute-done | bytes 160832 | tf_op jit(solution)/shard_map/ppermute | solution.py:38
  34.5 8.3 %fusion.119 = (f32[8,128]{1,0:T(8,128)S(1)}, f32[200,8,128]{0,2,1:T(8,128)S(1)}) fusion(bf16[200,11,134]{0,2,1:T(8,128)(2,1)S(1)} %get-tuple-element.75, f32[200]{0:T(256)S(1)} %bitcast.308, f32[200]{0:T(256)S(1)} %bitcast.309, f32[200]{0:T(256)S(1)} %bitcast.262, f32[200]{0:T(256)S(1)} %bitcast.263, f32[200]{0:T(256)S(1)} %bitcast.264, ...), kind=kLoop, calls=%fused_computation.262 | loop fusion | flops 33790976 | bytes 18494496 | tf_op jit(solution)/shard_map/reduce_sum | solution.py:114
  45.3 2.2 %fusion.9 = (bf16[800,1024]{1,0:T(8,128)(2,1)}, f32[1024,800]{0,1:T(8,128)S(1)}) fusion(bf16[200,800]{1,0:T(8,128)(2,1)S(1)} %copy-done, f32[200,1024]{1,0:T(8,128)S(1)} %copy.163, f32[200]{0:T(256)S(1)} %copy-done.9, f32[1024]{0:T(1024)S(1)} %rsqrt_bitcast_fusion, f32[1024]{0:T(1024)S(1)} %get-tuple-element.131), kind=kOutput, calls=%fused_computation.12 | convolution fusion | flops 332595200 | bytes 6063392 | tf_op jit(solution)/shard_map/dot_general | solution.py:120
  47.5 1.7 fusion.5
  49.2 1.7 %convolution_multiply_fusion.1 = f32[200,800]{1,0:T(8,128)} fusion(bf16[800,1024]{1,0:T(8,128)(2,1)S(1)} %fusion.5, f32[200,1024]{1,0:T(8,128)S(1)} %copy.163, f32[200]{0:T(256)S(1)} %copy-done.9, f32[1024]{0:T(1024)S(1)} %rsqrt_bitcast_fusion, f32[1024]{0:T(1024)S(1)} %get-tuple-element.131), kind=kOutput, calls=%fused_computation.114 | convolution fusion | flops 328659200 | bytes 3106592 | tf_op jit(solution)/shard_map/dot_general | solution.py:130
  55.0 3.8 %fusion.59 = (f32[200]{0:T(256)S(1)}, f32[200]{0:T(256)S(1)}, f32[200]{0:T(256)S(1)}, f32[200]{0:T(256)S(1)}, f32[200]{0:T(256)S(1)}, /*index=5*/f32[200]{0:T(25...) fusion(bf16[200,11,134]{0,2,1:T(8,128)(2,1)S(1)} %get-tuple-ele, ...), kind=kLoop, calls=%fused_computation.162 | loop fusion | flops 11055600 | bytes 8206400 | tf_op jit(solution)/shard_map/reduce_sum | solution.py:109
  58.8 3.8 %fusion.109 = (f32[200]{0:T(256)}, f32[200]{0:T(256)}, f32[200]{0:T(256)}, f32[200]{0:T(256)}, f32[200]{0:T(256)}, /*index=5*/f32[200]{0:T(256)}, f32[200]{0:T(2...) fusion(bf16[200,11,134]{0,2,1:T(8,128)(2,1)S(1)} %get-tuple-ele, ...), kind=kLoop, calls=%fused_computation.212 | loop fusion | flops 11055600 | bytes 8206400 | tf_op jit(solution)/shard_map/reduce_sum | solution.py:109
  64.8 3.0 %fusion.91 = (f32[200]{0:T(256)}, f32[200]{0:T(256)}, f32[200]{0:T(256)}, f32[200]{0:T(256)}, f32[200]{0:T(256)}, /*index=5*/f32[200]{0:T(256)}, f32[200]{0:T(25...) fusion(bf16[200,11,134]{0,2,1:T(8,128)(2,1)S(1)} %get-tuple-element.75, ...), kind=kLoop, calls=%fused_computation.194 | loop fusion | flops 11056800 | bytes 3715200 | tf_op jit(solution)/shard_map/reduce_sum | solution.py:109
  67.9 4.4 %stack.199 = f32[49,200]{1,0:T(8,128)S(1)} concatenate(f32[1,200]{1,0:T(1,128)} %bitcast.314, f32[1,200]{1,0:T(1,128)} %bitcast.315, f32[1,200]{1,0:T(1,128)} %bitcast.316, f32[1,200]{1,0:T(1,128)} %bitcast.242, f32[1,200]{1,0:T(1,128)} %bitcast.241, f32[1,200]{1,0:T(1,128)} %bitcast.240, f32[1,200]{1,0:T(1,128)} %bitcast.239, f32[1,200]{1,0:T(1,128)} %bitcast.238, ...), dimensions={0} | concatenate | bytes 78400 | tf_op jit(solution)/shard_map/stack | solution.py:110
  74.6 4.4 %collective-permute-start.5 = (f32[208,800]{1,0:T(8,128)S(1)}, f32[208,800]{1,0:T(8,128)S(1)}, u32[]{:S(2)}, u32[]{:S(2)}) collective-permute-start(f32[208,800]{1,0:T(8,128)S(1)} %fusion.110), channel_id=1, source_target_pairs={{0,4},{4,0},{1,5},{5,1},{2,6},{6,2},{3,7},{7,3},{8,12},{12,8},{9,1... | collective-permute-start | bytes 1996808 | tf_op jit(solution)/shard_map/ppermute | solution.py:33
  79.0 1.7 collective-permute-done.5
  80.9 16.4 %all_to_all.25 = f32[4,52,800]{2,1,0:T(8,128)S(1)} all-to-all(f32[4,52,800]{2,1,0:T(8,128)S(1)} %reshape.156), channel_id=1, replica_groups=mesh['ens'=4,'lon_z'=2,'lon_y'=8,'lon_c'=2,'lat'=4] {'lat'}, dimensions={0} | all-to-all | bytes 1331200 | tf_op jit(solution)/shard_map/all_to_all | solution.py:59
  97.4 15.2 %all_to_all.26 = f32[4,13,800]{2,1,0:T(8,128)S(1)} all-to-all(f32[4,13,800]{2,1,0:T(8,128)S(1)} %reshape.157), channel_id=1, replica_groups=mesh['ens'=4,'lon_z'=2,'lon_y'=8,'lon_c'=2,'lat'=4] {'ens'}, dimensions={0} | all-to-all | bytes 332800 | tf_op jit(solution)/shard_map/all_to_all | solution.py:59
  112.6 2.1 %collective-permute-start.6 = (f32[13,800]{1,0:T(8,128)S(1)}, f32[13,800]{1,0:T(8,128)S(1)}, u32[]{:S(2)}, u32[]{:S(2)}) collective-permute-start(f32[13,800]{1,0:T(8,128)S(1)} %reduce_sum.568), channel_id=1, source_target_pairs={{0,64},{64,0},{1,65},{65,1},{2,66},{66,2},{3,67},{67,3},{4,68},{68... | collective-permute-start | bytes 124808 | tf_op jit(solution)/shard_map/ppermute | solution.py:33
  114.7 2.8 %collective-permute-done.6 = f32[13,800]{1,0:T(8,128)S(1)} collective-permute-done((f32[13,800]{1,0:T(8,128)S(1)}, f32[13,800]{1,0:T(8,128)S(1)}, u32[]{:S(2)}, u32[]{:S(2)}) %collective-permute-start.6) | collective-permute-done | bytes 41632 | tf_op jit(solution)/shard_map/ppermute | solution.py:33
  117.6 17.2 %all_to_all.27 = f32[8,13,800]{2,1,0:T(8,128)S(1)} all-to-all(f32[8,13,800]{2,1,0:T(8,128)S(1)} %broadcast_in_dim.11), channel_id=1, replica_groups=mesh['ens'=4,'lon_z'=2,'lon_y'=8,'lon_c'=2,'lat'=4] {'lon_y'}, dimensions={0} | all-to-all | bytes 665600 | tf_op jit(solution)/shard_map/all_to_all | solution.py:48
  134.8 11.0 %all_to_all.28 = bf16[4,13,800]{2,1,0:T(8,128)(2,1)S(1)} all-to-all(bf16[4,13,800]{2,1,0:T(8,128)(2,1)S(1)} %broadcast_in_dim.12), channel_id=1, replica_groups=mesh['ens'=4,'lon_z'=2,'lon_y'=8,'lon_c'=2,'lat'=4] {'ens'}, dimensions={0} | all-to-all | bytes 166400 | tf_op jit(solution)/shard_map/all_to_all | solution.py:48
  145.9 8.7 %all_to_all.29 = bf16[4,52,800]{2,1,0:T(8,128)(2,1)S(1)} all-to-all(bf16[4,52,800]{2,1,0:T(8,128)(2,1)S(1)} %broadcast_in_dim.14), channel_id=1, replica_groups=mesh['ens'=4,'lon_z'=2,'lon_y'=8,'lon_c'=2,'lat'=4] {'lat'}, dimensions={0} | all-to-all | bytes 665600 | tf_op jit(solution)/shard_map/all_to_all | solution.py:48
  154.7 9.7 %collective-permute-start.7 = (bf16[208,800]{1,0:T(8,128)(2,1)S(1)}, bf16[208,800]{1,0:T(8,128)(2,1)S(1)}, u32[]{:S(2)}, u32[]{:S(2)}) collective-permute-start(bf16[208,800]{1,0:T(8,128)(2,1)S(1)} %reshape.158), channel_id=1, source_target_pairs={{0,4},{4,0},{1,5},{5,1},{2,6},{6,2},{3,7},{7,3},{8,12},{12,8},{9,1... | collective-permute-start | bytes 998408 | tf_op jit(solution)/shard_map/ppermute | solution.py:33
  (86 shorter events, 22.1 us)
Async XLA Ops:
  0.6 44.7 %copy-start = (bf16[200,800]{1,0:T(8,128)(2,1)S(1)}, bf16[200,800]{1,0:T(8,128)(2,1)}, u32[]{:S(2)}) copy-start(bf16[200,800]{1,0:T(8,128)(2,1)} %param.11) | copy-start | bytes 960004
  0.6 13.6 %copy-start.8 = (f32[200,49]{0,1:T(8,128)S(1)}, f32[200,49]{0,1:T(8,128)}, u32[]{:S(2)}) copy-start(f32[200,49]{0,1:T(8,128)} %param.9) | copy-start | bytes 117604
  3.5 10.8 %collective-permute-start = (bf16[200,8,3]{0,2,1:T(4,128)(2,1)S(1)}, bf16[200,8,3]{0,2,1:T(4,128)(2,1)S(1)}, u32[]{:S(2)}, u32[]{:S(2)}) collective-permute-start(bf16[200,8,3]{0,2,1:T(4,128)(2,1)S(1)} %get-tuple-element.78), channel_id=1, source_target_pairs={{0,4},{4,8},{8,12},{12,16},{16,20},{20,24},{24,28},{28,32},{32,36}... | collective-permute-start | bytes 28808 | tf_op jit(solution)/shard_map/ppermute | solution.py:23
  8.1 6.9 %collective-permute-start.1 = (bf16[200,8,3]{0,2,1:T(4,128)(2,1)S(1)}, bf16[200,8,3]{0,2,1:T(4,128)(2,1)S(1)}, u32[]{:S(2)}, u32[]{:S(2)}) collective-permute-start(bf16[200,8,3]{0,2,1:T(4,128)(2,1)S(1)} %get-tuple-element.79), channel_id=1, source_target_pairs={{4,0},{8,4},{12,8},{16,12},{20,16},{24,20},{28,24},{32,28},{36,32}... | collective-permute-start | bytes 28808 | tf_op jit(solution)/shard_map/ppermute | solution.py:25
  15.2 13.4 %collective-permute-start.2 = (bf16[200,3,134]{0,2,1:T(8,128)(2,1)S(1)}, bf16[200,3,134]{0,2,1:T(8,128)(2,1)S(1)}, u32[]{:S(2)}, u32[]{:S(2)}) collective-permute-start(bf16[200,3,134]{0,2,1:T(8,128)(2,1)S(1)} %get-tuple-element.77), channel_id=1, source_target_pairs={{0,1},{1,2},{2,3},{3,0},{4,5},{5,6},{6,7},{7,4},{8,9},{9,10},{10,1... | collective-permute-start | bytes 482408 | tf_op jit(solution)/shard_map/ppermute | solution.py:23
  18.1 16.1 %collective-permute-start.3 = (bf16[200,3,134]{0,2,1:T(8,128)(2,1)S(1)}, bf16[200,3,134]{0,2,1:T(8,128)(2,1)S(1)}, u32[]{:S(2)}, u32[]{:S(2)}) collective-permute-start(bf16[200,3,134]{0,2,1:T(8,128)(2,1)S(1)} %rev.3), channel_id=1, source_target_pairs={{0,124},{4,120},{8,116},{12,112},{16,108},{20,104},{24,100},{28,96... | collective-permute-start | bytes 482408 | tf_op jit(solution)/shard_map/ppermute | solution.py:38
  23.7 10.5 %collective-permute-start.4 = (bf16[200,3,134]{0,2,1:T(8,128)(2,1)S(1)}, bf16[200,3,134]{0,2,1:T(8,128)(2,1)S(1)}, u32[]{:S(2)}, u32[]{:S(2)}) collective-permute-start(bf16[200,3,134]{0,2,1:T(8,128)(2,1)S(1)} %get-tuple-element.76), channel_id=1, source_target_pairs={{1,0},{2,1},{3,2},{0,3},{5,4},{6,5},{7,6},{4,7},{9,8},{10,9},{11,1... | collective-permute-start | bytes 482408 | tf_op jit(solution)/shard_map/ppermute | solution.py:25
  42.8 1.0 copy-start.1
  42.8 2.5 %copy-start.9 = (f32[200]{0:T(256)S(1)}, f32[200]{0:T(256)}, u32[]{:S(2)}) copy-start(f32[200]{0:T(256)} %param.10) | copy-start | bytes 2404
  45.3 2.2 %copy-start.13 = (bf16[1,200,8,128]{3,2,1,0:T(8,128)(2,1)S(1)}, bf16[1,200,8,128]{3,2,1,0:T(8,128)(2,1)}, u32[]{:S(2)}) copy-start(bf16[1,200,8,128]{3,2,1,0:T(8,128)(2,1)} %param.13) | copy-start | bytes 1228804
  45.3 2.2 %copy-start.15 = (bf16[800,200]{0,1:T(8,128)(2,1)S(1)}, bf16[800,200]{0,1:T(8,128)(2,1)}, u32[]{:S(2)}) copy-start(bf16[800,200]{0,1:T(8,128)(2,1)} %param.12) | copy-start | bytes 960004
  50.9 1.4 copy-start.6
  58.8 3.8 %copy-start.4 = (bf16[800,1024]{1,0:T(8,128)(2,1)S(1)}, bf16[800,1024]{1,0:T(8,128)(2,1)}, u32[]{:S(2)}) copy-start(bf16[800,1024]{1,0:T(8,128)(2,1)} %get-tuple-element.133) | copy-start | bytes 4915204
  58.8 3.8 %copy-start.14 = (bf16[1,200,8,128]{3,2,1,0:T(8,128)(2,1)S(1)}, bf16[1,200,8,128]{3,2,1,0:T(8,128)(2,1)}, u32[]{:S(2)}) copy-start(bf16[1,200,8,128]{3,2,1,0:T(8,128)(2,1)} %param.13) | copy-start | bytes 1228804
  62.6 1.6 copy-start.12
  64.8 3.0 %copy-start.10 = (f32[200]{0:T(256)S(1)}, f32[200]{0:T(256)}, u32[]{:S(2)}) copy-start(f32[200]{0:T(256)} %get-tuple-element.38) | copy-start | bytes 2404
  67.8 12.8 %copy-start.2 = (f32[200,800]{1,0:T(8,128)S(1)}, f32[200,800]{1,0:T(8,128)}, u32[]{:S(2)}) copy-start(f32[200,800]{1,0:T(8,128)} %convolution_multiply_fusion.1) | copy-start | bytes 1920004
  67.8 12.8 %copy-start.3 = (f32[200,800]{1,0:T(8,128)S(1)}, f32[200,800]{1,0:T(8,128)}, u32[]{:S(2)}) copy-start(f32[200,800]{1,0:T(8,128)} %convolution_multiply_fusion) | copy-start | bytes 1920004
  74.6 6.0 %collective-permute-start.5 = (f32[208,800]{1,0:T(8,128)S(1)}, f32[208,800]{1,0:T(8,128)S(1)}, u32[]{:S(2)}, u32[]{:S(2)}) collective-permute-start(f32[208,800]{1,0:T(8,128)S(1)} %fusion.110), channel_id=1, source_target_pairs={{0,4},{4,0},{1,5},{5,1},{2,6},{6,2},{3,7},{7,3},{8,12},{12,8},{9,1... | collective-permute-start | bytes 1996808 | tf_op jit(solution)/shard_map/ppermute | solution.py:33
  112.6 4.9 %collective-permute-start.6 = (f32[13,800]{1,0:T(8,128)S(1)}, f32[13,800]{1,0:T(8,128)S(1)}, u32[]{:S(2)}, u32[]{:S(2)}) collective-permute-start(f32[13,800]{1,0:T(8,128)S(1)} %reduce_sum.568), channel_id=1, source_target_pairs={{0,64},{64,0},{1,65},{65,1},{2,66},{66,2},{3,67},{67,3},{4,68},{68... | collective-permute-start | bytes 124808 | tf_op jit(solution)/shard_map/ppermute | solution.py:33
  134.8 29.7 %copy-start.5 = (bf16[800,1024]{1,0:T(8,128)(2,1)S(1)}, bf16[800,1024]{1,0:T(8,128)(2,1)}, u32[]{:S(2)}) copy-start(bf16[800,1024]{1,0:T(8,128)(2,1)} %get-tuple-element.133) | copy-start | bytes 4915204
  134.8 29.7 %copy-start.7 = (bf16[1,200,8,128]{3,2,1,0:T(8,128)(2,1)S(1)}, bf16[1,200,8,128]{3,2,1,0:T(8,128)(2,1)}, u32[]{:S(2)}) copy-start(bf16[1,200,8,128]{3,2,1,0:T(8,128)(2,1)} %param.7) | copy-start | bytes 1228804
  134.8 29.7 %copy-start.11 = (f32[1024]{0:T(1024)S(1)}, f32[1024]{0:T(1024)}, u32[]{:S(2)}) copy-start(f32[1024]{0:T(1024)} %get-tuple-element.129) | copy-start | bytes 12292
  154.7 12.2 %collective-permute-start.7 = (bf16[208,800]{1,0:T(8,128)(2,1)S(1)}, bf16[208,800]{1,0:T(8,128)(2,1)S(1)}, u32[]{:S(2)}, u32[]{:S(2)}) collective-permute-start(bf16[208,800]{1,0:T(8,128)(2,1)S(1)} %reshape.158), channel_id=1, source_target_pairs={{0,4},{4,0},{1,5},{5,1},{2,6},{6,2},{3,7},{7,3},{8,12},{12,8},{9,1... | collective-permute-start | bytes 998408 | tf_op jit(solution)/shard_map/ppermute | solution.py:33

commit v10 on v9

--- a/solution.py
+++ b/solution.py
@@ -66,9 +66,8 @@
         upper = (lax.axis_index(axis) >> bit) & 1
         if rows % 2 == 0 and rows >= 8:
             half = rows // 2
-            low, high = flat[:half], flat[half:]
-            keep = jnp.where(upper == 0, low, high)
-            send = jnp.where(upper == 0, high, low)
+            keep = lax.dynamic_slice_in_dim(flat, upper * half, half, 0)
+            send = lax.dynamic_slice_in_dim(flat, (1 - upper) * half, half, 0)
             flat = keep + swapped(send, axis, bit)
             scattered.append((axis, bit))
         else:
@@ -81,9 +80,10 @@
             continue
         upper = (lax.axis_index(axis) >> bit) & 1
         other = swapped(flat, axis, bit)
-        flat = jnp.where(
-            upper == 0, jnp.concatenate([flat, other]), jnp.concatenate([other, flat])
-        )
+        rows = flat.shape[0]
+        both = jnp.zeros((2 * rows,) + flat.shape[1:], flat.dtype)
+        both = lax.dynamic_update_slice_in_dim(both, flat, upper * rows, 0)
+        flat = lax.dynamic_update_slice_in_dim(both, other, (1 - upper) * rows, 0)
     return flat
 
 

time: 171 us -> 169 us (0.988)
  no operation moved by 1% of the time
where the time goes in v10:
time: 169 us; the launch traced here: 168 us
  blocking collectives  68.5 us (41%)
  starting transfers between devices  39.3 us (23%)
  other arithmetic  27.1 us (16%)
  local copies, waits for them, and re-layouts  11.4 us (7%)
  waiting for transfers between devices  10.9 us (6%)
  matrix products  9.89 us (6%)
    all_to_all x3, blocking collectives, spread(): return lax.all_to_all(copies, axis, 0, 0, tiled=False)  36.9 us
    all_to_all x2, blocking collectives, tree_psum(): flat = lax.all_to_all(chunks, axis, 0, 0, tiled=False).sum(0)  31.6 us
    ppermute x3, starting transfers between devices, swapped(): lax.ppermute(array, axis, [(i, i ^ 1 << stride) for i in range(lax.axis_s...  16.2 us
    reduce_sum x4, other arithmetic, depthwise_grad(): columns.append(jnp.sum(d_conv * window, axis=(1, 2)))  11.8 us
    ppermute x2, starting transfers between devices, with_halo(): lax.ppermute(head, axis, [((i + 1) % count, i) for i in range(count)])  11 us
    reduce_sum x1, other arithmetic, cell_pass(): chan_mean = jnp.mean(conv_blk, axis=0, keepdims=True)  8.32 us
    ppermute x2, starting transfers between devices, with_halo(): lax.ppermute(tail, axis, [(i, (i + 1) % count) for i in range(count)])  6.52 us
    ppermute x1, starting transfers between devices, mirrored_across(): return lax.ppermute(array, axis, [(i, count - 1 - i) for i in range(count)])  5.6 us
  transfers between devices with their start and end apart: 8, of which 4 were waited for; matrix products, arithmetic and copies ran while one was open for 2% of the time, Pallas kernels for 0%

profile of v10, /device:TPU:1, one launch (start us, length us, event | category | flops | bytes accessed | tf_op | source)
XLA Modules:
  0.0 168.3 jit_solution(15543629245213136703)
XLA Ops:
  3.5 4.6 %collective-permute-start = (bf16[200,8,3]{0,2,1:T(4,128)(2,1)S(1)}, bf16[200,8,3]{0,2,1:T(4,128)(2,1)S(1)}, u32[]{:S(2)}, u32[]{:S(2)}) collective-permute-start(bf16[200,8,3]{0,2,1:T(4,128)(2,1)S(1)} %get-tuple-element.78), channel_id=1, source_target_pairs={{0,4},{4,8},{8,12},{12,16},{16,20},{20,24},{24,28},{28,32},{32,36}... | collective-permute-start | bytes 28808 | tf_op jit(solution)/shard_map/ppermute | solution.py:23
  8.1 6.1 %collective-permute-start.1 = (bf16[200,8,3]{0,2,1:T(4,128)(2,1)S(1)}, bf16[200,8,3]{0,2,1:T(4,128)(2,1)S(1)}, u32[]{:S(2)}, u32[]{:S(2)}) collective-permute-start(bf16[200,8,3]{0,2,1:T(4,128)(2,1)S(1)} %get-tuple-element.79), channel_id=1, source_target_pairs={{4,0},{8,4},{12,8},{16,12},{20,16},{24,20},{28,24},{32,28},{36,32}... | collective-permute-start | bytes 28808 | tf_op jit(solution)/shard_map/ppermute | solution.py:25
  15.2 1.9 %collective-permute-start.2 = (bf16[200,3,134]{0,2,1:T(8,128)(2,1)S(1)}, bf16[200,3,134]{0,2,1:T(8,128)(2,1)S(1)}, u32[]{:S(2)}, u32[]{:S(2)}) collective-permute-start(bf16[200,3,134]{0,2,1:T(8,128)(2,1)S(1)} %get-tuple-element.77), channel_id=1, source_target_pairs={{0,1},{1,2},{2,3},{3,0},{4,5},{5,6},{6,7},{7,4},{8,9},{9,10},{10,1... | collective-permute-start | bytes 482408 | tf_op jit(solution)/shard_map/ppermute | solution.py:23
  18.1 5.6 %collective-permute-start.3 = (bf16[200,3,134]{0,2,1:T(8,128)(2,1)S(1)}, bf16[200,3,134]{0,2,1:T(8,128)(2,1)S(1)}, u32[]{:S(2)}, u32[]{:S(2)}) collective-permute-start(bf16[200,3,134]{0,2,1:T(8,128)(2,1)S(1)} %rev.3), channel_id=1, source_target_pairs={{0,124},{4,120},{8,116},{12,112},{16,108},{20,104},{24,100},{28,96... | collective-permute-start | bytes 482408 | tf_op jit(solution)/shard_map/ppermute | solution.py:38
  23.7 4.9 %collective-permute-start.4 = (bf16[200,3,134]{0,2,1:T(8,128)(2,1)S(1)}, bf16[200,3,134]{0,2,1:T(8,128)(2,1)S(1)}, u32[]{:S(2)}, u32[]{:S(2)}) collective-permute-start(bf16[200,3,134]{0,2,1:T(8,128)(2,1)S(1)} %get-tuple-element.76), channel_id=1, source_target_pairs={{1,0},{2,1},{3,2},{0,3},{5,4},{6,5},{7,6},{4,7},{9,8},{10,9},{11,1... | collective-permute-start | bytes 482408 | tf_op jit(solution)/shard_map/ppermute | solution.py:25
  28.6 5.6 %collective-permute-done.3 = bf16[200,3,134]{0,2,1:T(8,128)(2,1)S(1)} collective-permute-done((bf16[200,3,134]{0,2,1:T(8,128)(2,1)S(1)}, bf16[200,3,134]{0,2,1:T(8,128)(2,1)S(1)}, u32[]{:S(2)}, u32[]{:S(2)}) %collective-permute-start.3) | collective-permute-done | bytes 160832 | tf_op jit(solution)/shard_map/ppermute | solution.py:38
  34.5 8.3 %fusion.118 = (f32[8,128]{1,0:T(8,128)S(1)}, f32[200,8,128]{0,2,1:T(8,128)S(1)}) fusion(bf16[200,11,134]{0,2,1:T(8,128)(2,1)S(1)} %get-tuple-element.75, f32[200]{0:T(256)S(1)} %bitcast.308, f32[200]{0:T(256)S(1)} %bitcast.309, f32[200]{0:T(256)S(1)} %bitcast.262, f32[200]{0:T(256)S(1)} %bitcast.263, f32[200]{0:T(256)S(1)} %bitcast.264, ...), kind=kLoop, calls=%fused_computation.262 | loop fusion | flops 33790976 | bytes 18494496 | tf_op jit(solution)/shard_map/reduce_sum | solution.py:114
  45.4 2.2 %fusion.9 = (bf16[800,1024]{1,0:T(8,128)(2,1)}, f32[1024,800]{0,1:T(8,128)S(1)}) fusion(bf16[200,800]{1,0:T(8,128)(2,1)S(1)} %copy-done, f32[200,1024]{1,0:T(8,128)S(1)} %copy.163, f32[200]{0:T(256)S(1)} %copy-done.7, f32[1024]{0:T(1024)S(1)} %rsqrt_bitcast_fusion, f32[1024]{0:T(1024)S(1)} %get-tuple-element.131), kind=kOutput, calls=%fused_computation.12 | convolution fusion | flops 332595200 | bytes 6063392 | tf_op jit(solution)/shard_map/dot_general | solution.py:120
  49.3 1.7 %convolution_multiply_fusion.1 = f32[200,800]{1,0:T(8,128)} fusion(bf16[800,1024]{1,0:T(8,128)(2,1)S(1)} %fusion.5, f32[200,1024]{1,0:T(8,128)S(1)} %copy.163, f32[200]{0:T(256)S(1)} %copy-done.7, f32[1024]{0:T(1024)S(1)} %rsqrt_bitcast_fusion, f32[1024]{0:T(1024)S(1)} %get-tuple-element.131), kind=kOutput, calls=%fused_computation.115 | convolution fusion | flops 328659200 | bytes 3106592 | tf_op jit(solution)/shard_map/dot_general | solution.py:130
  55.1 3.8 %fusion.109 = (f32[200]{0:T(256)S(1)}, f32[200]{0:T(256)S(1)}, f32[200]{0:T(256)S(1)}, f32[200]{0:T(256)S(1)}, f32[200]{0:T(256)S(1)}, /*index=5*/f32[200]{0:T(2...) fusion(bf16[200,11,134]{0,2,1:T(8,128)(2,1)S(1)} %get-tuple-ele, ...), kind=kLoop, calls=%fused_computation.213 | loop fusion | flops 11055600 | bytes 8206400 | tf_op jit(solution)/shard_map/reduce_sum | solution.py:109
  58.9 3.8 %fusion.59 = (f32[200]{0:T(256)}, f32[200]{0:T(256)}, f32[200]{0:T(256)}, f32[200]{0:T(256)}, f32[200]{0:T(256)}, /*index=5*/f32[200]{0:T(256)}, f32[200]{0:T(25...) fusion(bf16[200,11,134]{0,2,1:T(8,128)(2,1)S(1)} %get-tuple-ele, ...), kind=kLoop, calls=%fused_computation.163 | loop fusion | flops 11055600 | bytes 8206400 | tf_op jit(solution)/shard_map/reduce_sum | solution.py:109
  62.7 3.0 %fusion.91 = (f32[200]{0:T(256)}, f32[200]{0:T(256)}, f32[200]{0:T(256)}, f32[200]{0:T(256)}, f32[200]{0:T(256)}, /*index=5*/f32[200]{0:T(256)}, f32[200]{0:T(25...) fusion(bf16[200,11,134]{0,2,1:T(8,128)(2,1)S(1)} %get-tuple-element.75, ...), kind=kLoop, calls=%fused_computation.195 | loop fusion | flops 11056800 | bytes 3715200 | tf_op jit(solution)/shard_map/reduce_sum | solution.py:109
  65.7 3.7 %stack.199 = f32[49,200]{1,0:T(8,128)S(1)} concatenate(f32[1,200]{1,0:T(1,128)} %bitcast.314, f32[1,200]{1,0:T(1,128)} %bitcast.315, f32[1,200]{1,0:T(1,128)} %bitcast.316, f32[1,200]{1,0:T(1,128)} %bitcast.260, f32[1,200]{1,0:T(1,128)} %bitcast.259, f32[1,200]{1,0:T(1,128)} %bitcast.258, f32[1,200]{1,0:T(1,128)} %bitcast.257, f32[1,200]{1,0:T(1,128)} %bitcast.256, ...), dimensions={0} | concatenate | bytes 78400 | tf_op jit(solution)/shard_map/stack | solution.py:110
  70.4 2.3 %convolution_multiply_fusion = f32[200,800]{1,0:T(8,128)S(1)} fusion(bf16[800,1024]{1,0:T(8,128)(2,1)} %get-tuple-element.133, bf16[25,8,8,128]{3,2,1,0:T(8,128)(2,1)} %bitcast.323, bf16[1024]{0:T(1024)(128)(2,1)S(1)} %bitcast.223), kind=kOutput, calls=%fused_computation.114 | convolution fusion | flops 328044800 | bytes 2690048 | tf_op jit(solution)/shard_map/dot_general | solution.py:127
  72.9 4.4 %collective-permute-start.5 = (f32[208,800]{1,0:T(8,128)S(1)}, f32[208,800]{1,0:T(8,128)}, u32[]{:S(2)}, u32[]{:S(2)}) collective-permute-start(f32[208,800]{1,0:T(8,128)S(1)} %constant_dynamic-slice_fusion), channel_id=1, source_target_pairs={{0,4},{4,0},{1,5},{5,1},{2,6},{6,2},{3,7},{7,3},{8,12},{12,8},{9,1... | collective-permute-start | bytes 1996808 | tf_op jit(solution)/shard_map/ppermute | solution.py:33
  77.3 1.8 %collective-permute-done.5 = f32[208,800]{1,0:T(8,128)} collective-permute-done((f32[208,800]{1,0:T(8,128)S(1)}, f32[208,800]{1,0:T(8,128)}, u32[]{:S(2)}, u32[]{:S(2)}) %collective-permute-start.5) | collective-permute-done | bytes 665632 | tf_op jit(solution)/shard_map/ppermute | solution.py:33
  80.3 16.4 %all_to_all.25 = f32[4,52,800]{2,1,0:T(8,128)S(1)} all-to-all(f32[4,52,800]{2,1,0:T(8,128)S(1)} %reshape.156), channel_id=1, replica_groups=mesh['ens'=4,'lon_z'=2,'lon_y'=8,'lon_c'=2,'lat'=4] {'lat'}, dimensions={0} | all-to-all | bytes 1331200 | tf_op jit(solution)/shard_map/all_to_all | solution.py:59
  96.8 15.2 %all_to_all.26 = f32[4,13,800]{2,1,0:T(8,128)S(1)} all-to-all(f32[4,13,800]{2,1,0:T(8,128)S(1)} %reshape.157), channel_id=1, replica_groups=mesh['ens'=4,'lon_z'=2,'lon_y'=8,'lon_c'=2,'lat'=4] {'ens'}, dimensions={0} | all-to-all | bytes 332800 | tf_op jit(solution)/shard_map/all_to_all | solution.py:59
  112.0 2.1 %collective-permute-start.6 = (f32[13,800]{1,0:T(8,128)S(1)}, f32[13,800]{1,0:T(8,128)S(1)}, u32[]{:S(2)}, u32[]{:S(2)}) collective-permute-start(f32[13,800]{1,0:T(8,128)S(1)} %reduce_sum.568), channel_id=1, source_target_pairs={{0,64},{64,0},{1,65},{65,1},{2,66},{66,2},{3,67},{67,3},{4,68},{68... | collective-permute-start | bytes 124808 | tf_op jit(solution)/shard_map/ppermute | solution.py:33
  114.2 2.8 %collective-permute-done.6 = f32[13,800]{1,0:T(8,128)S(1)} collective-permute-done((f32[13,800]{1,0:T(8,128)S(1)}, f32[13,800]{1,0:T(8,128)S(1)}, u32[]{:S(2)}, u32[]{:S(2)}) %collective-permute-start.6) | collective-permute-done | bytes 41632 | tf_op jit(solution)/shard_map/ppermute | solution.py:33
  117.0 17.2 %all_to_all.27 = f32[8,13,800]{2,1,0:T(8,128)S(1)} all-to-all(f32[8,13,800]{2,1,0:T(8,128)S(1)} %broadcast_in_dim.14), channel_id=1, replica_groups=mesh['ens'=4,'lon_z'=2,'lon_y'=8,'lon_c'=2,'lat'=4] {'lon_y'}, dimensions={0} | all-to-all | bytes 665600 | tf_op jit(solution)/shard_map/all_to_all | solution.py:48
  134.3 11.0 %all_to_all.28 = bf16[4,13,800]{2,1,0:T(8,128)(2,1)S(1)} all-to-all(bf16[4,13,800]{2,1,0:T(8,128)(2,1)S(1)} %broadcast_in_dim.15), channel_id=1, replica_groups=mesh['ens'=4,'lon_z'=2,'lon_y'=8,'lon_c'=2,'lat'=4] {'ens'}, dimensions={0} | all-to-all | bytes 166400 | tf_op jit(solution)/shard_map/all_to_all | solution.py:48
  145.4 8.7 %all_to_all.29 = bf16[4,52,800]{2,1,0:T(8,128)(2,1)S(1)} all-to-all(bf16[4,52,800]{2,1,0:T(8,128)(2,1)S(1)} %broadcast_in_dim.17), channel_id=1, replica_groups=mesh['ens'=4,'lon_z'=2,'lon_y'=8,'lon_c'=2,'lat'=4] {'lat'}, dimensions={0} | all-to-all | bytes 665600 | tf_op jit(solution)/shard_map/all_to_all | solution.py:48
  154.2 9.7 %collective-permute-start.7 = (bf16[208,800]{1,0:T(8,128)(2,1)S(1)}, bf16[208,800]{1,0:T(8,128)(2,1)S(1)}, u32[]{:S(2)}, u32[]{:S(2)}) collective-permute-start(bf16[208,800]{1,0:T(8,128)(2,1)S(1)} %reshape.158), channel_id=1, source_target_pairs={{0,4},{4,0},{1,5},{5,1},{2,6},{6,2},{3,7},{7,3},{8,12},{12,8},{9,1... | collective-permute-start | bytes 998408 | tf_op jit(solution)/shard_map/ppermute | solution.py:33
  (81 shorter events, 20.4 us)
Async XLA Ops:
  0.6 44.7 %copy-start = (bf16[200,800]{1,0:T(8,128)(2,1)S(1)}, bf16[200,800]{1,0:T(8,128)(2,1)}, u32[]{:S(2)}) copy-start(bf16[200,800]{1,0:T(8,128)(2,1)} %param.11) | copy-start | bytes 960004
  0.6 13.6 %copy-start.6 = (f32[200,49]{0,1:T(8,128)S(1)}, f32[200,49]{0,1:T(8,128)}, u32[]{:S(2)}) copy-start(f32[200,49]{0,1:T(8,128)} %param.9) | copy-start | bytes 117604
  3.5 10.8 %collective-permute-start = (bf16[200,8,3]{0,2,1:T(4,128)(2,1)S(1)}, bf16[200,8,3]{0,2,1:T(4,128)(2,1)S(1)}, u32[]{:S(2)}, u32[]{:S(2)}) collective-permute-start(bf16[200,8,3]{0,2,1:T(4,128)(2,1)S(1)} %get-tuple-element.78), channel_id=1, source_target_pairs={{0,4},{4,8},{8,12},{12,16},{16,20},{20,24},{24,28},{28,32},{32,36}... | collective-permute-start | bytes 28808 | tf_op jit(solution)/shard_map/ppermute | solution.py:23
  8.1 6.9 %collective-permute-start.1 = (bf16[200,8,3]{0,2,1:T(4,128)(2,1)S(1)}, bf16[200,8,3]{0,2,1:T(4,128)(2,1)S(1)}, u32[]{:S(2)}, u32[]{:S(2)}) collective-permute-start(bf16[200,8,3]{0,2,1:T(4,128)(2,1)S(1)} %get-tuple-element.79), channel_id=1, source_target_pairs={{4,0},{8,4},{12,8},{16,12},{20,16},{24,20},{28,24},{32,28},{36,32}... | collective-permute-start | bytes 28808 | tf_op jit(solution)/shard_map/ppermute | solution.py:25
  15.2 13.4 %collective-permute-start.2 = (bf16[200,3,134]{0,2,1:T(8,128)(2,1)S(1)}, bf16[200,3,134]{0,2,1:T(8,128)(2,1)S(1)}, u32[]{:S(2)}, u32[]{:S(2)}) collective-permute-start(bf16[200,3,134]{0,2,1:T(8,128)(2,1)S(1)} %get-tuple-element.77), channel_id=1, source_target_pairs={{0,1},{1,2},{2,3},{3,0},{4,5},{5,6},{6,7},{7,4},{8,9},{9,10},{10,1... | collective-permute-start | bytes 482408 | tf_op jit(solution)/shard_map/ppermute | solution.py:23
  18.1 16.1 %collective-permute-start.3 = (bf16[200,3,134]{0,2,1:T(8,128)(2,1)S(1)}, bf16[200,3,134]{0,2,1:T(8,128)(2,1)S(1)}, u32[]{:S(2)}, u32[]{:S(2)}) collective-permute-start(bf16[200,3,134]{0,2,1:T(8,128)(2,1)S(1)} %rev.3), channel_id=1, source_target_pairs={{0,124},{4,120},{8,116},{12,112},{16,108},{20,104},{24,100},{28,96... | collective-permute-start | bytes 482408 | tf_op jit(solution)/shard_map/ppermute | solution.py:38
  23.7 10.5 %collective-permute-start.4 = (bf16[200,3,134]{0,2,1:T(8,128)(2,1)S(1)}, bf16[200,3,134]{0,2,1:T(8,128)(2,1)S(1)}, u32[]{:S(2)}, u32[]{:S(2)}) collective-permute-start(bf16[200,3,134]{0,2,1:T(8,128)(2,1)S(1)} %get-tuple-element.76), channel_id=1, source_target_pairs={{1,0},{2,1},{3,2},{0,3},{5,4},{6,5},{7,6},{4,7},{9,8},{10,9},{11,1... | collective-permute-start | bytes 482408 | tf_op jit(solution)/shard_map/ppermute | solution.py:25
  42.8 1.0 copy-start.1
  42.8 2.5 %copy-start.7 = (f32[200]{0:T(256)S(1)}, f32[200]{0:T(256)}, u32[]{:S(2)}) copy-start(f32[200]{0:T(256)} %param.10) | copy-start | bytes 2404
  45.4 2.2 %copy-start.9 = (bf16[1,200,8,128]{3,2,1,0:T(8,128)(2,1)S(1)}, bf16[1,200,8,128]{3,2,1,0:T(8,128)(2,1)}, u32[]{:S(2)}) copy-start(bf16[1,200,8,128]{3,2,1,0:T(8,128)(2,1)} %param.13) | copy-start | bytes 1228804
  45.4 2.2 %copy-start.10 = (bf16[800,200]{0,1:T(8,128)(2,1)S(1)}, bf16[800,200]{0,1:T(8,128)(2,1)}, u32[]{:S(2)}) copy-start(bf16[800,200]{0,1:T(8,128)(2,1)} %param.12) | copy-start | bytes 960004
  51.0 1.4 copy-start.4
  69.4 3.3 %copy-start.2 = (f32[200,800]{1,0:T(8,128)S(1)}, f32[200,800]{1,0:T(8,128)}, u32[]{:S(2)}) copy-start(f32[200,800]{1,0:T(8,128)} %convolution_multiply_fusion.1) | copy-start | bytes 1920004
  72.9 6.1 %collective-permute-start.5 = (f32[208,800]{1,0:T(8,128)S(1)}, f32[208,800]{1,0:T(8,128)}, u32[]{:S(2)}, u32[]{:S(2)}) collective-permute-start(f32[208,800]{1,0:T(8,128)S(1)} %constant_dynamic-slice_fusion), channel_id=1, source_target_pairs={{0,4},{4,0},{1,5},{5,1},{2,6},{6,2},{3,7},{7,3},{8,12},{12,8},{9,1... | collective-permute-start | bytes 1996808 | tf_op jit(solution)/shard_map/ppermute | solution.py:33
  112.0 4.9 %collective-permute-start.6 = (f32[13,800]{1,0:T(8,128)S(1)}, f32[13,800]{1,0:T(8,128)S(1)}, u32[]{:S(2)}, u32[]{:S(2)}) collective-permute-start(f32[13,800]{1,0:T(8,128)S(1)} %reduce_sum.568), channel_id=1, source_target_pairs={{0,64},{64,0},{1,65},{65,1},{2,66},{66,2},{3,67},{67,3},{4,68},{68... | collective-permute-start | bytes 124808 | tf_op jit(solution)/shard_map/ppermute | solution.py:33
  134.2 29.7 %copy-start.3 = (bf16[800,1024]{1,0:T(8,128)(2,1)S(1)}, bf16[800,1024]{1,0:T(8,128)(2,1)}, u32[]{:S(2)}) copy-start(bf16[800,1024]{1,0:T(8,128)(2,1)} %get-tuple-element.133) | copy-start | bytes 4915204
  134.2 29.7 %copy-start.5 = (bf16[1,200,8,128]{3,2,1,0:T(8,128)(2,1)S(1)}, bf16[1,200,8,128]{3,2,1,0:T(8,128)(2,1)}, u32[]{:S(2)}) copy-start(bf16[1,200,8,128]{3,2,1,0:T(8,128)(2,1)} %param.7) | copy-start | bytes 1228804
  134.2 29.7 %copy-start.8 = (f32[1024]{0:T(1024)S(1)}, f32[1024]{0:T(1024)}, u32[]{:S(2)}) copy-start(f32[1024]{0:T(1024)} %get-tuple-element.129) | copy-start | bytes 12292
  134.2 29.8 %copy-start.11 = (bf16[800,200]{0,1:T(8,128)(2,1)S(1)}, bf16[800,200]{0,1:T(8,128)(2,1)}, u32[]{:S(2)}) copy-start(bf16[800,200]{0,1:T(8,128)(2,1)} %param.12) | copy-start | bytes 960004
  154.2 11.4 %collective-permute-start.7 = (bf16[208,800]{1,0:T(8,128)(2,1)S(1)}, bf16[208,800]{1,0:T(8,128)(2,1)S(1)}, u32[]{:S(2)}, u32[]{:S(2)}) collective-permute-start(bf16[208,800]{1,0:T(8,128)(2,1)S(1)} %reshape.158), channel_id=1, source_target_pairs={{0,4},{4,0},{1,5},{5,1},{2,6},{6,2},{3,7},{7,3},{8,12},{12,8},{9,1... | collective-permute-start | bytes 998408 | tf_op jit(solution)/shard_map/ppermute | solution.py:33

commit v11 on v10

--- a/solution.py
+++ b/solution.py
@@ -80,10 +80,9 @@
             continue
         upper = (lax.axis_index(axis) >> bit) & 1
         other = swapped(flat, axis, bit)
-        rows = flat.shape[0]
-        both = jnp.zeros((2 * rows,) + flat.shape[1:], flat.dtype)
-        both = lax.dynamic_update_slice_in_dim(both, flat, upper * rows, 0)
-        flat = lax.dynamic_update_slice_in_dim(both, other, (1 - upper) * rows, 0)
+        first = jnp.where(upper == 0, flat, other)
+        second = jnp.where(upper == 0, other, flat)
+        flat = jnp.concatenate([first, second])
     return flat
 
 

time: 169 us -> 170 us (level)
  transfers between devices with their start and end apart: 8 -> 8, of which waited for: 4 -> 4; matrix products, arithmetic and copies ran while one was open for 2% -> 1% of each run, Pallas kernels for 0% -> 0%
where the time goes in v11:
time: 170 us; the launch traced here: 169 us
  blocking collectives  68.5 us (40%)
  starting transfers between devices  39.2 us (23%)
  other arithmetic  28.2 us (17%)
  local copies, waits for them, and re-layouts  11.3 us (7%)
  waiting for transfers between devices  11 us (6%)
  matrix products  9.86 us (6%)
    all_to_all x3, blocking collectives, spread(): return lax.all_to_all(copies, axis, 0, 0, tiled=False)  36.9 us
    all_to_all x2, blocking collectives, tree_psum(): flat = lax.all_to_all(chunks, axis, 0, 0, tiled=False).sum(0)  31.6 us
    ppermute x3, starting transfers between devices, swapped(): lax.ppermute(array, axis, [(i, i ^ 1 << stride) for i in range(lax.axis_s...  16.1 us
    reduce_sum x4, other arithmetic, depthwise_grad(): columns.append(jnp.sum(d_conv * window, axis=(1, 2)))  11.8 us
    ppermute x2, starting transfers between devices, with_halo(): lax.ppermute(head, axis, [((i + 1) % count, i) for i in range(count)])  11 us
    reduce_sum x1, other arithmetic, cell_pass(): chan_mean = jnp.mean(conv_blk, axis=0, keepdims=True)  8.32 us
    ppermute x2, starting transfers between devices, with_halo(): lax.ppermute(tail, axis, [(i, (i + 1) % count) for i in range(count)])  6.52 us
    ppermute x1, starting transfers between devices, mirrored_across(): return lax.ppermute(array, axis, [(i, count - 1 - i) for i in range(count)])  5.6 us
  transfers between devices with their start and end apart: 8, of which 4 were waited for; matrix products, arithmetic and copies ran while one was open for 1% of the time, Pallas kernels for 0%

profile of v11, /device:TPU:1, one launch (start us, length us, event | category | flops | bytes accessed | tf_op | source)
XLA Modules:
  0.0 169.2 jit_solution(2920510570919079876)
XLA Ops:
  3.5 4.6 %collective-permute-start = (bf16[200,8,3]{0,2,1:T(4,128)(2,1)S(1)}, bf16[200,8,3]{0,2,1:T(4,128)(2,1)S(1)}, u32[]{:S(2)}, u32[]{:S(2)}) collective-permute-start(bf16[200,8,3]{0,2,1:T(4,128)(2,1)S(1)} %get-tuple-element.78), channel_id=1, source_target_pairs={{0,4},{4,8},{8,12},{12,16},{16,20},{20,24},{24,28},{28,32},{32,36}... | collective-permute-start | bytes 28808 | tf_op jit(solution)/shard_map/ppermute | solution.py:23
  8.1 6.1 %collective-permute-start.1 = (bf16[200,8,3]{0,2,1:T(4,128)(2,1)S(1)}, bf16[200,8,3]{0,2,1:T(4,128)(2,1)S(1)}, u32[]{:S(2)}, u32[]{:S(2)}) collective-permute-start(bf16[200,8,3]{0,2,1:T(4,128)(2,1)S(1)} %get-tuple-element.79), channel_id=1, source_target_pairs={{4,0},{8,4},{12,8},{16,12},{20,16},{24,20},{28,24},{32,28},{36,32}... | collective-permute-start | bytes 28808 | tf_op jit(solution)/shard_map/ppermute | solution.py:25
  15.2 1.9 %collective-permute-start.2 = (bf16[200,3,134]{0,2,1:T(8,128)(2,1)S(1)}, bf16[200,3,134]{0,2,1:T(8,128)(2,1)S(1)}, u32[]{:S(2)}, u32[]{:S(2)}) collective-permute-start(bf16[200,3,134]{0,2,1:T(8,128)(2,1)S(1)} %get-tuple-element.77), channel_id=1, source_target_pairs={{0,1},{1,2},{2,3},{3,0},{4,5},{5,6},{6,7},{7,4},{8,9},{9,10},{10,1... | collective-permute-start | bytes 482408 | tf_op jit(solution)/shard_map/ppermute | solution.py:23
  18.1 5.6 %collective-permute-start.3 = (bf16[200,3,134]{0,2,1:T(8,128)(2,1)S(1)}, bf16[200,3,134]{0,2,1:T(8,128)(2,1)S(1)}, u32[]{:S(2)}, u32[]{:S(2)}) collective-permute-start(bf16[200,3,134]{0,2,1:T(8,128)(2,1)S(1)} %rev.3), channel_id=1, source_target_pairs={{0,124},{4,120},{8,116},{12,112},{16,108},{20,104},{24,100},{28,96... | collective-permute-start | bytes 482408 | tf_op jit(solution)/shard_map/ppermute | solution.py:38
  23.7 4.9 %collective-permute-start.4 = (bf16[200,3,134]{0,2,1:T(8,128)(2,1)S(1)}, bf16[200,3,134]{0,2,1:T(8,128)(2,1)S(1)}, u32[]{:S(2)}, u32[]{:S(2)}) collective-permute-start(bf16[200,3,134]{0,2,1:T(8,128)(2,1)S(1)} %get-tuple-element.76), channel_id=1, source_target_pairs={{1,0},{2,1},{3,2},{0,3},{5,4},{6,5},{7,6},{4,7},{9,8},{10,9},{11,1... | collective-permute-start | bytes 482408 | tf_op jit(solution)/shard_map/ppermute | solution.py:25
  28.6 5.6 %collective-permute-done.3 = bf16[200,3,134]{0,2,1:T(8,128)(2,1)S(1)} collective-permute-done((bf16[200,3,134]{0,2,1:T(8,128)(2,1)S(1)}, bf16[200,3,134]{0,2,1:T(8,128)(2,1)S(1)}, u32[]{:S(2)}, u32[]{:S(2)}) %collective-permute-start.3) | collective-permute-done | bytes 160832 | tf_op jit(solution)/shard_map/ppermute | solution.py:38
  34.5 8.3 %fusion.118 = (f32[8,128]{1,0:T(8,128)S(1)}, f32[200,8,128]{0,2,1:T(8,128)S(1)}) fusion(bf16[200,11,134]{0,2,1:T(8,128)(2,1)S(1)} %get-tuple-element.75, f32[200]{0:T(256)S(1)} %bitcast.308, f32[200]{0:T(256)S(1)} %bitcast.309, f32[200]{0:T(256)S(1)} %bitcast.262, f32[200]{0:T(256)S(1)} %bitcast.263, f32[200]{0:T(256)S(1)} %bitcast.264, ...), kind=kLoop, calls=%fused_computation.263 | loop fusion | flops 33790976 | bytes 18494496 | tf_op jit(solution)/shard_map/reduce_sum | solution.py:113
  45.4 2.2 %fusion.9 = (bf16[800,1024]{1,0:T(8,128)(2,1)}, f32[1024,800]{0,1:T(8,128)S(1)}) fusion(bf16[200,800]{1,0:T(8,128)(2,1)S(1)} %copy-done, f32[200,1024]{1,0:T(8,128)S(1)} %copy.163, f32[200]{0:T(256)S(1)} %copy-done.7, f32[1024]{0:T(1024)S(1)} %rsqrt_bitcast_fusion, f32[1024]{0:T(1024)S(1)} %get-tuple-element.133), kind=kOutput, calls=%fused_computation.12 | convolution fusion | flops 332595200 | bytes 6063392 | tf_op jit(solution)/shard_map/dot_general | solution.py:119
  49.3 1.7 %convolution_multiply_fusion.1 = f32[200,800]{1,0:T(8,128)} fusion(bf16[800,1024]{1,0:T(8,128)(2,1)S(1)} %fusion.5, f32[200,1024]{1,0:T(8,128)S(1)} %copy.163, f32[200]{0:T(256)S(1)} %copy-done.7, f32[1024]{0:T(1024)S(1)} %rsqrt_bitcast_fusion, f32[1024]{0:T(1024)S(1)} %get-tuple-element.133), kind=kOutput, calls=%fused_computation.115 | convolution fusion | flops 328659200 | bytes 3106592 | tf_op jit(solution)/shard_map/dot_general | solution.py:129
  55.1 3.8 %fusion.109 = (f32[200]{0:T(256)S(1)}, f32[200]{0:T(256)S(1)}, f32[200]{0:T(256)S(1)}, f32[200]{0:T(256)S(1)}, f32[200]{0:T(256)S(1)}, /*index=5*/f32[200]{0:T(2...) fusion(bf16[200,11,134]{0,2,1:T(8,128)(2,1)S(1)} %get-tuple-ele, ...), kind=kLoop, calls=%fused_computation.213 | loop fusion | flops 11055600 | bytes 8206400 | tf_op jit(solution)/shard_map/reduce_sum | solution.py:108
  58.9 3.8 %fusion.59 = (f32[200]{0:T(256)}, f32[200]{0:T(256)}, f32[200]{0:T(256)}, f32[200]{0:T(256)}, f32[200]{0:T(256)}, /*index=5*/f32[200]{0:T(256)}, f32[200]{0:T(25...) fusion(bf16[200,11,134]{0,2,1:T(8,128)(2,1)S(1)} %get-tuple-ele, ...), kind=kLoop, calls=%fused_computation.163 | loop fusion | flops 11055600 | bytes 8206400 | tf_op jit(solution)/shard_map/reduce_sum | solution.py:108
  62.6 3.0 %fusion.91 = (f32[200]{0:T(256)}, f32[200]{0:T(256)}, f32[200]{0:T(256)}, f32[200]{0:T(256)}, f32[200]{0:T(256)}, /*index=5*/f32[200]{0:T(256)}, f32[200]{0:T(25...) fusion(bf16[200,11,134]{0,2,1:T(8,128)(2,1)S(1)} %get-tuple-element.75, ...), kind=kLoop, calls=%fused_computation.195 | loop fusion | flops 11056800 | bytes 3715200 | tf_op jit(solution)/shard_map/reduce_sum | solution.py:108
  65.6 3.7 %stack.199 = f32[49,200]{1,0:T(8,128)S(1)} concatenate(f32[1,200]{1,0:T(1,128)} %bitcast.314, f32[1,200]{1,0:T(1,128)} %bitcast.315, f32[1,200]{1,0:T(1,128)} %bitcast.316, f32[1,200]{1,0:T(1,128)} %bitcast.260, f32[1,200]{1,0:T(1,128)} %bitcast.259, f32[1,200]{1,0:T(1,128)} %bitcast.258, f32[1,200]{1,0:T(1,128)} %bitcast.257, f32[1,200]{1,0:T(1,128)} %bitcast.256, ...), dimensions={0} | concatenate | bytes 78400 | tf_op jit(solution)/shard_map/stack | solution.py:109
  70.3 2.3 %convolution_multiply_fusion = f32[200,800]{1,0:T(8,128)S(1)} fusion(bf16[800,1024]{1,0:T(8,128)(2,1)} %get-tuple-element.135, bf16[25,8,8,128]{3,2,1,0:T(8,128)(2,1)} %bitcast.323, bf16[1024]{0:T(1024)(128)(2,1)S(1)} %bitcast.223), kind=kOutput, calls=%fused_computation.114 | convolution fusion | flops 328044800 | bytes 2690048 | tf_op jit(solution)/shard_map/dot_general | solution.py:126
  72.9 4.2 %collective-permute-start.5 = (f32[208,800]{1,0:T(8,128)S(1)}, f32[208,800]{1,0:T(8,128)}, u32[]{:S(2)}, u32[]{:S(2)}) collective-permute-start(f32[208,800]{1,0:T(8,128)S(1)} %constant_dynamic-slice_fusion), channel_id=1, source_target_pairs={{0,4},{4,0},{1,5},{5,1},{2,6},{6,2},{3,7},{7,3},{8,12},{12,8},{9,1... | collective-permute-start | bytes 1996808 | tf_op jit(solution)/shard_map/ppermute | solution.py:33
  77.1 2.0 %collective-permute-done.5 = f32[208,800]{1,0:T(8,128)} collective-permute-done((f32[208,800]{1,0:T(8,128)S(1)}, f32[208,800]{1,0:T(8,128)}, u32[]{:S(2)}, u32[]{:S(2)}) %collective-permute-start.5) | collective-permute-done | bytes 665632 | tf_op jit(solution)/shard_map/ppermute | solution.py:33
  80.3 16.4 %all_to_all.25 = f32[4,52,800]{2,1,0:T(8,128)S(1)} all-to-all(f32[4,52,800]{2,1,0:T(8,128)S(1)} %reshape.156), channel_id=1, replica_groups=mesh['ens'=4,'lon_z'=2,'lon_y'=8,'lon_c'=2,'lat'=4] {'lat'}, dimensions={0} | all-to-all | bytes 1331200 | tf_op jit(solution)/shard_map/all_to_all | solution.py:59
  96.8 15.2 %all_to_all.26 = f32[4,13,800]{2,1,0:T(8,128)S(1)} all-to-all(f32[4,13,800]{2,1,0:T(8,128)S(1)} %reshape.157), channel_id=1, replica_groups=mesh['ens'=4,'lon_z'=2,'lon_y'=8,'lon_c'=2,'lat'=4] {'ens'}, dimensions={0} | all-to-all | bytes 332800 | tf_op jit(solution)/shard_map/all_to_all | solution.py:59
  112.0 2.1 %collective-permute-start.6 = (f32[13,800]{1,0:T(8,128)S(1)}, f32[13,800]{1,0:T(8,128)S(1)}, u32[]{:S(2)}, u32[]{:S(2)}) collective-permute-start(f32[13,800]{1,0:T(8,128)S(1)} %reduce_sum.568), channel_id=1, source_target_pairs={{0,64},{64,0},{1,65},{65,1},{2,66},{66,2},{3,67},{67,3},{4,68},{68... | collective-permute-start | bytes 124808 | tf_op jit(solution)/shard_map/ppermute | solution.py:33
  114.2 2.8 %collective-permute-done.6 = f32[13,800]{1,0:T(8,128)S(1)} collective-permute-done((f32[13,800]{1,0:T(8,128)S(1)}, f32[13,800]{1,0:T(8,128)S(1)}, u32[]{:S(2)}, u32[]{:S(2)}) %collective-permute-start.6) | collective-permute-done | bytes 41632 | tf_op jit(solution)/shard_map/ppermute | solution.py:33
  117.0 17.2 %all_to_all.27 = f32[8,13,800]{2,1,0:T(8,128)S(1)} all-to-all(f32[8,13,800]{2,1,0:T(8,128)S(1)} %broadcast_in_dim.11), channel_id=1, replica_groups=mesh['ens'=4,'lon_z'=2,'lon_y'=8,'lon_c'=2,'lat'=4] {'lon_y'}, dimensions={0} | all-to-all | bytes 665600 | tf_op jit(solution)/shard_map/all_to_all | solution.py:48
  134.3 11.0 %all_to_all.28 = bf16[4,13,800]{2,1,0:T(8,128)(2,1)S(1)} all-to-all(bf16[4,13,800]{2,1,0:T(8,128)(2,1)S(1)} %broadcast_in_dim.12), channel_id=1, replica_groups=mesh['ens'=4,'lon_z'=2,'lon_y'=8,'lon_c'=2,'lat'=4] {'ens'}, dimensions={0} | all-to-all | bytes 166400 | tf_op jit(solution)/shard_map/all_to_all | solution.py:48
  145.4 8.7 %all_to_all.29 = bf16[4,52,800]{2,1,0:T(8,128)(2,1)S(1)} all-to-all(bf16[4,52,800]{2,1,0:T(8,128)(2,1)S(1)} %broadcast_in_dim.14), channel_id=1, replica_groups=mesh['ens'=4,'lon_z'=2,'lon_y'=8,'lon_c'=2,'lat'=4] {'lat'}, dimensions={0} | all-to-all | bytes 665600 | tf_op jit(solution)/shard_map/all_to_all | solution.py:48
  154.2 9.8 %collective-permute-start.7 = (bf16[208,800]{1,0:T(8,128)(2,1)S(1)}, bf16[208,800]{1,0:T(8,128)(2,1)}, u32[]{:S(2)}, u32[]{:S(2)}) collective-permute-start(bf16[208,800]{1,0:T(8,128)(2,1)S(1)} %reshape.158), channel_id=1, source_target_pairs={{0,4},{4,0},{1,5},{5,1},{2,6},{6,2},{3,7},{7,3},{8,12},{12,8},{9,1... | collective-permute-start | bytes 998408 | tf_op jit(solution)/shard_map/ppermute | solution.py:33
  (79 shorter events, 21.3 us)
Async XLA Ops:
  0.6 44.7 %copy-start = (bf16[200,800]{1,0:T(8,128)(2,1)S(1)}, bf16[200,800]{1,0:T(8,128)(2,1)}, u32[]{:S(2)}) copy-start(bf16[200,800]{1,0:T(8,128)(2,1)} %param.11) | copy-start | bytes 960004
  0.6 13.6 %copy-start.6 = (f32[200,49]{0,1:T(8,128)S(1)}, f32[200,49]{0,1:T(8,128)}, u32[]{:S(2)}) copy-start(f32[200,49]{0,1:T(8,128)} %param.9) | copy-start | bytes 117604
  3.5 10.8 %collective-permute-start = (bf16[200,8,3]{0,2,1:T(4,128)(2,1)S(1)}, bf16[200,8,3]{0,2,1:T(4,128)(2,1)S(1)}, u32[]{:S(2)}, u32[]{:S(2)}) collective-permute-start(bf16[200,8,3]{0,2,1:T(4,128)(2,1)S(1)} %get-tuple-element.78), channel_id=1, source_target_pairs={{0,4},{4,8},{8,12},{12,16},{16,20},{20,24},{24,28},{28,32},{32,36}... | collective-permute-start | bytes 28808 | tf_op jit(solution)/shard_map/ppermute | solution.py:23
  8.1 6.9 %collective-permute-start.1 = (bf16[200,8,3]{0,2,1:T(4,128)(2,1)S(1)}, bf16[200,8,3]{0,2,1:T(4,128)(2,1)S(1)}, u32[]{:S(2)}, u32[]{:S(2)}) collective-permute-start(bf16[200,8,3]{0,2,1:T(4,128)(2,1)S(1)} %get-tuple-element.79), channel_id=1, source_target_pairs={{4,0},{8,4},{12,8},{16,12},{20,16},{24,20},{28,24},{32,28},{36,32}... | collective-permute-start | bytes 28808 | tf_op jit(solution)/shard_map/ppermute | solution.py:25
  15.2 13.4 %collective-permute-start.2 = (bf16[200,3,134]{0,2,1:T(8,128)(2,1)S(1)}, bf16[200,3,134]{0,2,1:T(8,128)(2,1)S(1)}, u32[]{:S(2)}, u32[]{:S(2)}) collective-permute-start(bf16[200,3,134]{0,2,1:T(8,128)(2,1)S(1)} %get-tuple-element.77), channel_id=1, source_target_pairs={{0,1},{1,2},{2,3},{3,0},{4,5},{5,6},{6,7},{7,4},{8,9},{9,10},{10,1... | collective-permute-start | bytes 482408 | tf_op jit(solution)/shard_map/ppermute | solution.py:23
  18.1 16.1 %collective-permute-start.3 = (bf16[200,3,134]{0,2,1:T(8,128)(2,1)S(1)}, bf16[200,3,134]{0,2,1:T(8,128)(2,1)S(1)}, u32[]{:S(2)}, u32[]{:S(2)}) collective-permute-start(bf16[200,3,134]{0,2,1:T(8,128)(2,1)S(1)} %rev.3), channel_id=1, source_target_pairs={{0,124},{4,120},{8,116},{12,112},{16,108},{20,104},{24,100},{28,96... | collective-permute-start | bytes 482408 | tf_op jit(solution)/shard_map/ppermute | solution.py:38
  23.7 10.5 %collective-permute-start.4 = (bf16[200,3,134]{0,2,1:T(8,128)(2,1)S(1)}, bf16[200,3,134]{0,2,1:T(8,128)(2,1)S(1)}, u32[]{:S(2)}, u32[]{:S(2)}) collective-permute-start(bf16[200,3,134]{0,2,1:T(8,128)(2,1)S(1)} %get-tuple-element.76), channel_id=1, source_target_pairs={{1,0},{2,1},{3,2},{0,3},{5,4},{6,5},{7,6},{4,7},{9,8},{10,9},{11,1... | collective-permute-start | bytes 482408 | tf_op jit(solution)/shard_map/ppermute | solution.py:25
  42.8 1.0 copy-start.1
  42.8 2.5 %copy-start.7 = (f32[200]{0:T(256)S(1)}, f32[200]{0:T(256)}, u32[]{:S(2)}) copy-start(f32[200]{0:T(256)} %param.10) | copy-start | bytes 2404
  45.4 2.2 %copy-start.9 = (bf16[1,200,8,128]{3,2,1,0:T(8,128)(2,1)S(1)}, bf16[1,200,8,128]{3,2,1,0:T(8,128)(2,1)}, u32[]{:S(2)}) copy-start(bf16[1,200,8,128]{3,2,1,0:T(8,128)(2,1)} %param.13) | copy-start | bytes 1228804
  45.4 2.2 %copy-start.10 = (bf16[800,200]{0,1:T(8,128)(2,1)S(1)}, bf16[800,200]{0,1:T(8,128)(2,1)}, u32[]{:S(2)}) copy-start(bf16[800,200]{0,1:T(8,128)(2,1)} %param.12) | copy-start | bytes 960004
  51.0 1.4 copy-start.4
  69.4 3.3 %copy-start.2 = (f32[200,800]{1,0:T(8,128)S(1)}, f32[200,800]{1,0:T(8,128)}, u32[]{:S(2)}) copy-start(f32[200,800]{1,0:T(8,128)} %convolution_multiply_fusion.1) | copy-start | bytes 1920004
  72.9 6.2 %collective-permute-start.5 = (f32[208,800]{1,0:T(8,128)S(1)}, f32[208,800]{1,0:T(8,128)}, u32[]{:S(2)}, u32[]{:S(2)}) collective-permute-start(f32[208,800]{1,0:T(8,128)S(1)} %constant_dynamic-slice_fusion), channel_id=1, source_target_pairs={{0,4},{4,0},{1,5},{5,1},{2,6},{6,2},{3,7},{7,3},{8,12},{12,8},{9,1... | collective-permute-start | bytes 1996808 | tf_op jit(solution)/shard_map/ppermute | solution.py:33
  112.0 4.9 %collective-permute-start.6 = (f32[13,800]{1,0:T(8,128)S(1)}, f32[13,800]{1,0:T(8,128)S(1)}, u32[]{:S(2)}, u32[]{:S(2)}) collective-permute-start(f32[13,800]{1,0:T(8,128)S(1)} %reduce_sum.568), channel_id=1, source_target_pairs={{0,64},{64,0},{1,65},{65,1},{2,66},{66,2},{3,67},{67,3},{4,68},{68... | collective-permute-start | bytes 124808 | tf_op jit(solution)/shard_map/ppermute | solution.py:33
  134.2 29.7 %copy-start.3 = (bf16[800,1024]{1,0:T(8,128)(2,1)S(1)}, bf16[800,1024]{1,0:T(8,128)(2,1)}, u32[]{:S(2)}) copy-start(bf16[800,1024]{1,0:T(8,128)(2,1)} %get-tuple-element.135) | copy-start | bytes 4915204
  134.2 29.7 %copy-start.5 = (bf16[1,200,8,128]{3,2,1,0:T(8,128)(2,1)S(1)}, bf16[1,200,8,128]{3,2,1,0:T(8,128)(2,1)}, u32[]{:S(2)}) copy-start(bf16[1,200,8,128]{3,2,1,0:T(8,128)(2,1)} %param.7) | copy-start | bytes 1228804
  134.2 29.7 %copy-start.8 = (f32[1024]{0:T(1024)S(1)}, f32[1024]{0:T(1024)}, u32[]{:S(2)}) copy-start(f32[1024]{0:T(1024)} %get-tuple-element.131) | copy-start | bytes 12292
  134.2 29.8 %copy-start.11 = (bf16[800,200]{0,1:T(8,128)(2,1)S(1)}, bf16[800,200]{0,1:T(8,128)(2,1)}, u32[]{:S(2)}) copy-start(bf16[800,200]{0,1:T(8,128)(2,1)} %param.12) | copy-start | bytes 960004
  154.2 11.2 %collective-permute-start.7 = (bf16[208,800]{1,0:T(8,128)(2,1)S(1)}, bf16[208,800]{1,0:T(8,128)(2,1)}, u32[]{:S(2)}, u32[]{:S(2)}) collective-permute-start(bf16[208,800]{1,0:T(8,128)(2,1)S(1)} %reshape.158), channel_id=1, source_target_pairs={{0,4},{4,0},{1,5},{5,1},{2,6},{6,2},{3,7},{7,3},{8,12},{12,8},{9,1... | collective-permute-start | bytes 998408 | tf_op jit(solution)/shard_map/ppermute | solution.py:33
